TPU v7x, 128 devices: a whole 4x4x4 slice. The times are simulated.
128 devices in a mesh: dp: 32 (over z, x, core), tensor: 4 (over y).
Axes of the slice: x: 4, y: 4, z: 4, core: 2. Of those that a mesh axis runs over, the one named last changes fastest.
Arguments:
- normed_hidden_state: bfloat16 [4, 2048, 8192], P(None, 'dp', 'tensor'), may hold values from -6 to 6
- query_projection_weight: bfloat16 [8192, 4096], P(None, 'tensor'), may hold values from -0.0625 to 0.0625
- adapter_down_maps: bfloat16 [4096, 8192], P('dp', 'tensor'), may hold values from -0.0625 to 0.0625
- adapter_up_maps: bfloat16 [4096, 4096], P('dp', 'tensor'), may hold values from -0.75 to 0.75
- key_value_cache: bfloat16 [2, 2048, 128, 512], P(None, 'dp', None, 'tensor'), may hold values from -82 to 82
- step_key_value: bfloat16 [4, 2, 2048, 512], P(None, None, 'dp', 'tensor'), may hold values from -6 to 6
- cache_valid_length: int32 [2048], P('dp'), may hold values from 1 to 128, as said below
- adapter_per_request: int32 [2048], P('dp'), may hold values from 0 to 63, as said below
- adapter_pool_position: int32 [64], replicated, may hold values from 0 to 63, as said below
Outputs:
- attended: bfloat16 [4, 2048, 4096], P(None, 'dp', 'tensor')
Inputs may be any that keep to these rules, and one draw needn't show every extreme that they name: `adapter_pool_position`: A permutation: every adapter has its own pool position, and position p is held by dp index p // 2. `adapter_per_request`: within each group of 64 consecutive requests, requests whose adapters sit on the same dp index use the same adapter; some dp index serves an adapter to every group. `cache_valid_length`: each group of 64 consecutive requests holds a request with all 128 positions valid.
All inputs are finite; a program needn't handle non-finite values.
Results may differ from a plain program's by a relative error of at most 0.015.
Values may be sent and summed in bfloat16 or wider, within the bound.
No kernel may reach another device: no remote copies, remote signals or barrier semaphores. Data moves between devices by JAX's collectives and lax.ppermute only.
A program may use at most 192 MiB of HBM per device.

v0:
```python
import math

import jax
import jax.numpy as jnp
from jax import lax
from jax.sharding import PartitionSpec as P

HEAD_SIZE = 128
ADAPTER_RANK = 64


def pool_lookup(adapters, adapter_pool_position):
    table = jnp.arange(adapter_pool_position.shape[0], dtype=jnp.int32)
    match = adapters[:, None] == table[None, :]
    return jnp.sum(jnp.where(match, adapter_pool_position[None, :], 0), axis=1)


def adapt_rows(normed_hidden_state, down_map_pages, up_map_pages):
    shrink_local = jnp.einsum(
        "trd,rjd->trj", normed_hidden_state, down_map_pages, preferred_element_type=jnp.float32
    )
    shrink = lax.psum(shrink_local, "tensor").astype(jnp.bfloat16)
    return jnp.einsum("trj,rjh->trh", shrink, up_map_pages, preferred_element_type=jnp.float32)


def attend(query, key_value_cache, step_key_value, cache_valid_length):
    steps = step_key_value.shape[0]
    requests = step_key_value.shape[2]
    length = key_value_cache.shape[2]
    kv_local = key_value_cache.shape[3] // HEAD_SIZE
    group = query.shape[2] // HEAD_SIZE // kv_local
    scale = 1.0 / math.sqrt(HEAD_SIZE)
    grouped = query.reshape(steps, requests, kv_local, group, HEAD_SIZE)
    keys = key_value_cache[0].reshape(requests, length, kv_local, HEAD_SIZE)
    values = key_value_cache[1].reshape(requests, length, kv_local, HEAD_SIZE)
    new_keys = step_key_value[:, 0].reshape(steps, requests, kv_local, HEAD_SIZE)
    new_values = step_key_value[:, 1].reshape(steps, requests, kv_local, HEAD_SIZE)
    cache_scores = (
        jnp.einsum("trkgd,rckd->trkgc", grouped, keys, preferred_element_type=jnp.float32) * scale
    )
    valid = jnp.arange(length, dtype=jnp.int32)[None, :] < cache_valid_length[:, None]
    cache_scores = jnp.where(valid[None, :, None, None, :], cache_scores, -1e30)
    fresh_scores = (
        jnp.einsum("trkgd,srkd->trkgs", grouped, new_keys, preferred_element_type=jnp.float32)
        * scale
    )
    causal = (
        jnp.arange(steps, dtype=jnp.int32)[:, None] >= jnp.arange(steps, dtype=jnp.int32)[None, :]
    )
    fresh_scores = jnp.where(causal[:, None, None, None, :], fresh_scores, -1e30)
    top = jnp.maximum(jnp.max(cache_scores, axis=-1), jnp.max(fresh_scores, axis=-1))
    cache_expo = jnp.exp(cache_scores - top[..., None])
    fresh_expo = jnp.exp(fresh_scores - top[..., None])
    total = jnp.sum(cache_expo, axis=-1) + jnp.sum(fresh_expo, axis=-1)
    mixed = jnp.einsum(
        "trkgc,rckd->trkgd",
        cache_expo.astype(jnp.bfloat16),
        values,
        preferred_element_type=jnp.float32,
    )
    mixed = mixed + jnp.einsum(
        "trkgs,srkd->trkgd",
        fresh_expo.astype(jnp.bfloat16),
        new_values,
        preferred_element_type=jnp.float32,
    )
    attended = mixed / total[..., None]
    return attended.reshape(steps, requests, -1).astype(jnp.bfloat16)


def per_device(
    normed_hidden_state,
    query_projection_weight,
    adapter_down_maps,
    adapter_up_maps,
    key_value_cache,
    step_key_value,
    cache_valid_length,
    adapter_per_request,
    adapter_pool_position,
):
    steps, requests, part_width = normed_hidden_state.shape
    count_rows = steps * requests
    token_rows = normed_hidden_state.reshape(count_rows, part_width)
    heads_width = query_projection_weight.shape[1]
    position = pool_lookup(adapter_per_request, adapter_pool_position)
    base = jnp.dot(
        lax.all_gather(token_rows, "tensor", axis=1, tiled=True),
        query_projection_weight,
        preferred_element_type=jnp.float32,
    )
    down_all, up_all = (
        lax.all_gather(adapter_down_maps, "dp", axis=0, tiled=True),
        lax.all_gather(adapter_up_maps, "dp", axis=0, tiled=True),
    )
    down_map_pages = jnp.take(down_all.reshape(-1, ADAPTER_RANK, part_width), position, axis=0)
    up_map_pages = jnp.take(up_all.reshape(-1, ADAPTER_RANK, heads_width), position, axis=0)
    delta = adapt_rows(normed_hidden_state, down_map_pages, up_map_pages)
    query = (base.reshape(steps, requests, heads_width) + delta).astype(jnp.bfloat16)
    return attend(query, key_value_cache, step_key_value, cache_valid_length)


def solution(mesh):
    return jax.shard_map(
        per_device,
        mesh=mesh,
        in_specs=(
            P(None, "dp", "tensor"),
            P(None, "tensor"),
            P("dp", "tensor"),
            P("dp", "tensor"),
            P(None, "dp", None, "tensor"),
            P(None, None, "dp", "tensor"),
            P("dp"),
            P("dp"),
            P(),
        ),
        out_specs=P(None, "dp", "tensor"),
        check_vma=False,
    )
```

profile of v0, /device:TPU:1, one launch (start us, length us, event | category | flops | bytes accessed | tf_op | source)
XLA Modules:
  0.0 249.5 jit_solution(4320837906704978882)
XLA Ops:
  6.5 0.0 all-gather.4.cloned.1.call-start
  6.5 0.7 all-gather.4.cloned.1.call-update
  7.3 0.0 all-gather.6.cloned.1.call-start
  7.3 0.7 all-gather.6.cloned.1.call-update
  8.0 0.0 all-gather.8.cloned.1.call-start
  8.1 0.7 all-gather.8.cloned.1.call-update
  8.8 0.8 select_reduce_fusion
  9.6 0.7 iota_compare_fusion.1
  10.4 0.9 fusion.56
  11.3 49.0 %all-gather.4.cloned.1.call-done = bf16[256,8192]{1,0:T(8,128)(2,1)} async-done(((bf16[256,2048]{1,0:T(8,128)(2,1)}), bf16[256,8192]{1,0:T(8,128)(2,1)}) %all-gather.4.cloned.1.call-update) | async-done | bytes 4194320 | tf_op jit(solution)/shard_map/all_gather | solution.py:88
  60.3 9.6 %fusion.59 = f32[256,1024]{1,0:T(8,128)S(1)} fusion(bf16[256,8192]{1,0:T(8,128)(2,1)} %all-gather.4.cloned.1.call-done, bf16[8192,1024]{1,0:T(8,128)(2,1)} %param.10), kind=kOutput, calls=%fused_computation.58 | convolution fusion | flops 4294967296 | bytes 22020096 | tf_op jit(solution)/shard_map/dot_general | solution.py:87
  69.9 46.4 %all-gather.6.cloned.1.call-done = bf16[4096,1024]{1,0:T(8,128)(2,1)} async-done(((bf16[128,1024]{1,0:T(8,128)(2,1)}), bf16[4096,1024]{1,0:T(8,128)(2,1)}) %all-gather.6.cloned.1.call-update) | async-done | bytes 8388624 | tf_op jit(solution)/shard_map/all_gather | solution.py:94
  116.3 8.9 %gather_fusion = bf16[64,64,1024]{2,1,0:T(8,128)(2,1)} fusion(bf16[64,64,1024]{2,1,0:T(8,128)(2,1)} %bitcast.96, s32[1024]{0:T(1024)S(1)} %pad_clamp_fusion), kind=kCustom, calls=%fused_computation | custom fusion | bytes 16777472 | tf_op jit(solution)/shard_map/jit(_take)/gather | solution.py:97
  125.2 65.6 %all-gather.8.cloned.1.call-done = bf16[4096,2048]{1,0:T(8,128)(2,1)} async-done(((bf16[128,2048]{1,0:T(8,128)(2,1)}), bf16[4096,2048]{1,0:T(8,128)(2,1)}) %all-gather.8.cloned.1.call-update) | async-done | bytes 16777232 | tf_op jit(solution)/shard_map/all_gather | solution.py:93
  190.8 0.0 copy-start
  190.8 13.4 %gather_fusion.1 = bf16[64,64,2048]{2,1,0:T(8,128)(2,1)} fusion(bf16[64,64,2048]{2,1,0:T(8,128)(2,1)} %bitcast.95, s32[1024]{0:T(1024)S(1)} %pad_clamp_fusion), kind=kCustom, calls=%fused_computation.1 | custom fusion | bytes 33554688 | tf_op jit(solution)/shard_map/jit(_take)/gather | solution.py:96
  204.2 0.0 copy-done
  204.2 8.1 %fusion.37 = f32[4,64,64]{2,0,1:T(4,128)S(1)} fusion(bf16[64,64,2048]{2,1,0:T(8,128)(2,1)} %gather_fusion.1, pred[64]{0:T(512)(128)(4,1)S(1)} %compare_and_fusion, bf16[4,64,2048]{2,1,0:T(8,128)(2,1)S(1)} %copy-done), kind=kOutput, calls=%fused_computation.27 | convolution fusion | flops 75497472 | bytes 17891392 | tf_op jit(solution)/shard_map/trd,rjd->trj/dot_general | solution.py:19
  212.3 14.8 %psum.7 = bf16[4,64,64]{2,0,1:T(4,128)(2,1)S(1)} all-reduce(f32[4,64,64]{2,0,1:T(4,128)S(1)} %fusion.37), channel_id=1, replica_groups=mesh['dp'=32,'tensor'=4] {'tensor'}, use_global_device_ids=true, to_apply=%region_1.2 | all-reduce | flops 16384 | bytes 98304 | tf_op jit(solution)/shard_map/psum | solution.py:22
  227.1 4.9 %fusion.27 = bf16[4,64,1024]{2,0,1:T(4,128)(2,1)S(1)} fusion(bf16[64,64,1024]{2,1,0:T(8,128)(2,1)} %gather_fusion, pred[64]{0:T(512)(128)(4,1)S(1)} %compare_and_fusion, f32[4,64,1024]{2,1,0:T(8,128)S(1)} %bitcast.98, bf16[4,64,64]{2,0,1:T(4,128)(2,1)S(1)} %psum.7), kind=kOutput, calls=%fused_computation.22 | convolution fusion | flops 38273024 | bytes 9994304 | tf_op jit(solution)/shard_map/trj,rjh->trh/dot_general | solution.py:23
  232.1 0.2 reshape.139
  232.3 2.4 fusion.58
  234.7 2.9 %fusion.57 = (f32[4,64,8]{2,0,1:T(4,128)S(1)}, f32[4,64,1,8,128]{4,3,0,1,2:T(8,128)S(1)}) fusion(bf16[4,64,8,128]{3,2,0,1:T(8,128)(2,1)S(1)} %reshape.139, bf16[2,64,128,128]{3,2,1,0:T(8,128)(2,1)} %param.13, pred[64,128]{1,0:T(8,128)(4,1)S(1)} %iota_compare_fusion.1), kind=kOutput, calls=%fused_computation.56 | convolution fusion | flops 67893248 | bytes 3686400 | tf_op jit(solution)/shard_map/trkgd,rckd->trkgc/dot_general | solution.py:39
  237.6 0.7 fusion.42
  238.4 2.3 fusion.8
  240.7 0.5 fusion.47
  241.2 0.6 divide_convert_fusion
  241.9 0.1 convert_element_type.23
  242.0 1.0 copy.17
  (6 shorter events, 0.1 us)
Async XLA Ops:
  6.5 53.7 %all-gather.4.cloned.1.call-start = ((), (), s32[]{:S(2)}) async-start(), calls=%async_computation | async-start | bytes 5242880 | tf_op jit(solution)/shard_map/all_gather | solution.py:88
  7.3 109.1 %all-gather.6.cloned.1.call-start = ((), (), s32[]{:S(2)}) async-start(), calls=%async_computation.1 | async-start | bytes 8650752 | tf_op jit(solution)/shard_map/all_gather | solution.py:94
  8.0 182.8 %all-gather.8.cloned.1.call-start = ((), (), s32[]{:S(2)}) async-start(), calls=%async_computation.2 | async-start | bytes 17301504 | tf_op jit(solution)/shard_map/all_gather | solution.py:93
  190.8 13.4 %copy-start = (bf16[4,64,2048]{2,1,0:T(8,128)(2,1)S(1)}, bf16[4,64,2048]{2,1,0:T(8,128)(2,1)}, u32[]{:S(2)}) copy-start(bf16[4,64,2048]{2,1,0:T(8,128)(2,1)} %param.9) | copy-start | bytes 3145732
Sparse Core Ops, SparseCore 0:
  9.0 51.2 all-gather.3
  62.5 53.7 all-gather.5
  118.6 72.1 all-gather.7
where the time goes:
time: 252 us; the launch traced here: 249 us
  waiting for transfers between devices  163 us (65%)
  matrix products  30.9 us (12%)
  local copies, waits for them, and re-layouts  24.5 us (10%)
  blocking collectives  14.8 us (6%)
  between operations  13.2 us (5%)
  other arithmetic  2.9 us (1%)
    all_gather x1, waiting for transfers between devices, per_device(): lax.all_gather(adapter_down_maps, 'dp', axis=0, tiled=True)  65.6 us
    all_gather x1, waiting for transfers between devices, per_device(): lax.all_gather(token_rows, 'tensor', axis=1, tiled=True)  49 us
    all_gather x1, waiting for transfers between devices, per_device(): lax.all_gather(adapter_up_maps, 'dp', axis=0, tiled=True)  46.4 us
    psum x1, blocking collectives, adapt_rows(): shrink = lax.psum(shrink_local, 'tensor').astype(jnp.bfloat16)  14.8 us
    gather x1, local copies, waits for them, and re-layouts, per_device(): jnp.take(down_all.reshape(-1, ADAPTER_RANK, part_width), position, axis=0)  13.4 us
    dot_general x1, matrix products, per_device(): jnp.dot(lax.all_gather(token_rows, 'tensor', axis=1, tiled=True), query_p...  9.61 us
    gather x1, local copies, waits for them, and re-layouts, per_device(): jnp.take(up_all.reshape(-1, ADAPTER_RANK, heads_width), position, axis=0)  8.89 us
    dot_general x1, matrix products, adapt_rows(): jnp.einsum('trd,rjd->trj', normed_hidden_state, down_map_pages, preferred...  8.13 us
  transfers between devices with their start and end apart: 3, of which 3 were waited for; matrix products, arithmetic and copies ran while one was open for 8% of the time, Pallas kernels for 0%

commit v1 on v0

--- a/solution.py
+++ b/solution.py
@@ -2,11 +2,14 @@
 
 import jax
 import jax.numpy as jnp
+import numpy as np
 from jax import lax
+from jax.sharding import Mesh
 from jax.sharding import PartitionSpec as P
 
 HEAD_SIZE = 128
 ADAPTER_RANK = 64
+CORES = 2
 
 
 def pool_lookup(adapters, adapter_pool_position):
@@ -15,12 +18,11 @@
     return jnp.sum(jnp.where(match, adapter_pool_position[None, :], 0), axis=1)
 
 
-def adapt_rows(normed_hidden_state, down_map_pages, up_map_pages):
-    shrink_local = jnp.einsum(
-        "trd,rjd->trj", normed_hidden_state, down_map_pages, preferred_element_type=jnp.float32
-    )
-    shrink = lax.psum(shrink_local, "tensor").astype(jnp.bfloat16)
-    return jnp.einsum("trj,rjh->trh", shrink, up_map_pages, preferred_element_type=jnp.float32)
+def shift_all(value, axis, count):
+    pieces = [value]
+    for k in range(1, count):
+        pieces.append(lax.ppermute(value, axis, [(i, (i + k) % count) for i in range(count)]))
+    return pieces
 
 
 def attend(query, key_value_cache, step_key_value, cache_valid_length):
@@ -81,40 +83,79 @@
 ):
     steps, requests, part_width = normed_hidden_state.shape
     count_rows = steps * requests
+    heads_width = query_projection_weight.shape[1]
+    n_tensor = query_projection_weight.shape[0] // part_width
+    pool_dev = adapter_down_maps.shape[0] // ADAPTER_RANK
     token_rows = normed_hidden_state.reshape(count_rows, part_width)
-    heads_width = query_projection_weight.shape[1]
+
+    down_mine = lax.all_gather(adapter_down_maps, "chip", axis=0, tiled=True)
+    up_mine = lax.all_gather(adapter_up_maps, "chip", axis=0, tiled=True)
+    swap = [(0, 1), (1, 0)]
+    down_other = lax.ppermute(down_mine, "core", swap)
+    up_other = lax.ppermute(up_mine, "core", swap)
+    n_slots = down_mine.shape[0] // ADAPTER_RANK
+
+    t = lax.axis_index("tensor")
+    pieces = shift_all(token_rows, "tensor", n_tensor)
+    base = None
+    for k, piece in enumerate(pieces):
+        src = (t - k) % n_tensor
+        w_rows = lax.dynamic_slice_in_dim(query_projection_weight, src * part_width, part_width, 0)
+        part = jnp.dot(piece, w_rows, preferred_element_type=jnp.float32)
+        base = part if base is None else base + part
+
     position = pool_lookup(adapter_per_request, adapter_pool_position)
-    base = jnp.dot(
-        lax.all_gather(token_rows, "tensor", axis=1, tiled=True),
-        query_projection_weight,
-        preferred_element_type=jnp.float32,
+    my_core = lax.axis_index("core")
+    holder = position // pool_dev
+    slot_index = (holder // CORES) * pool_dev + position % pool_dev
+    on_mine = (holder % CORES) == my_core
+    slots = jnp.arange(n_slots, dtype=jnp.int32)[None, :]
+    mask_mine = on_mine[:, None] & (slot_index[:, None] == slots)
+    mask_other = (~on_mine)[:, None] & (slot_index[:, None] == slots)
+
+    def shrink_part(down_block, mask):
+        full = lax.dot_general(
+            token_rows, down_block, (((1,), (1,)), ((), ())), preferred_element_type=jnp.float32
+        ).reshape(steps, requests, n_slots, ADAPTER_RANK)
+        return jnp.sum(jnp.where(mask[None, :, :, None], full, 0.0), axis=2)
+
+    shrink_local = shrink_part(down_mine, mask_mine) + shrink_part(down_other, mask_other)
+    partials = shift_all(shrink_local, "tensor", n_tensor)
+    shrink_sum = partials[0]
+    for p in partials[1:]:
+        shrink_sum = shrink_sum + p
+    shrink = shrink_sum.astype(jnp.bfloat16)
+
+    def expand(mask):
+        wide = jnp.where(mask[None, :, :, None], shrink[:, :, None, :], jnp.zeros((), jnp.bfloat16))
+        return wide.reshape(count_rows, n_slots * ADAPTER_RANK)
+
+    delta = jnp.dot(expand(mask_mine), up_mine, preferred_element_type=jnp.float32) + jnp.dot(
+        expand(mask_other), up_other, preferred_element_type=jnp.float32
     )
-    down_all, up_all = (
-        lax.all_gather(adapter_down_maps, "dp", axis=0, tiled=True),
-        lax.all_gather(adapter_up_maps, "dp", axis=0, tiled=True),
-    )
-    down_map_pages = jnp.take(down_all.reshape(-1, ADAPTER_RANK, part_width), position, axis=0)
-    up_map_pages = jnp.take(up_all.reshape(-1, ADAPTER_RANK, heads_width), position, axis=0)
-    delta = adapt_rows(normed_hidden_state, down_map_pages, up_map_pages)
-    query = (base.reshape(steps, requests, heads_width) + delta).astype(jnp.bfloat16)
+    query = (base + delta).reshape(steps, requests, heads_width).astype(jnp.bfloat16)
     return attend(query, key_value_cache, step_key_value, cache_valid_length)
 
 
 def solution(mesh):
+    devices = np.asarray(mesh.devices)
+    n_dp, n_tensor = devices.shape
+    grid = Mesh(devices.reshape(n_dp // CORES, CORES, n_tensor), ("chip", "core", "tensor"))
+    dp = ("chip", "core")
     return jax.shard_map(
         per_device,
-        mesh=mesh,
+        mesh=grid,
         in_specs=(
-            P(None, "dp", "tensor"),
+            P(None, dp, "tensor"),
             P(None, "tensor"),
-            P("dp", "tensor"),
-            P("dp", "tensor"),
-            P(None, "dp", None, "tensor"),
-            P(None, None, "dp", "tensor"),
-            P("dp"),
-            P("dp"),
+            P(dp, "tensor"),
+            P(dp, "tensor"),
+            P(None, dp, None, "tensor"),
+            P(None, None, dp, "tensor"),
+            P(dp),
+            P(dp),
             P(),
         ),
-        out_specs=P(None, "dp", "tensor"),
+        out_specs=P(None, dp, "tensor"),
         check_vma=False,
     )

time: 252 us -> 212 us (0.84)
  waiting for transfers between devices: 163 us -> 124 us
  blocking collectives: 14.8 us -> 0 us
  matrix products: 30.9 us -> 44.6 us
  starting transfers between devices: 0.08 us -> 10.2 us
  local copies, waits for them, and re-layouts: 24.5 us -> 15.8 us
    all_gather x3 -> x2, waiting for transfers between devices: 161 us -> 122 us  [the longest x1 75.5 us: per_device(): down_mine = lax.all_gather(adapter_down_maps, 'chip', axis=0, tiled=True)]
    gather x2 -> x0, local copies, waits for them, and re-layouts: 22.3 us -> none  [the longest x1 13.4 us: per_device(): jnp.take(down_all.reshape(-1, ADAPTER_RANK, part_width), position, axis=0)]
    dot_general x3 -> x8, matrix products: 22.6 us -> 37.7 us  [the longest x4 18 us: per_device(): part = jnp.dot(piece, w_rows, preferred_element_type=jnp.float32)]
    psum x1 -> x0, blocking collectives: 14.8 us -> none  [adapt_rows(): shrink = lax.psum(shrink_local, 'tensor').astype(jnp.bfloat16)]
    select_n x0 -> x4, local copies, waits for them, and re-layouts: none -> 12.4 us  [expand(): jnp.where(mask[None, :, :, None], shrink[:, :, None, :], jnp.zeros((), jn...]
    ppermute x0 -> x8, starting transfers between devices: none -> 10.1 us  [the longest x6 8.46 us: shift_all(): lax.ppermute(value, axis, [(i, (i + k) % count) for i in range(count)])]
  transfers between devices with their start and end apart: 3 -> 10, of which waited for: 3 -> 3; matrix products, arithmetic and copies ran while one was open for 8% -> 23% of each run, Pallas kernels for 0% -> 0%
where the time goes in v1:
time: 212 us
  waiting for transfers between devices  124 us (58%)
  matrix products  44.6 us (21%)
  local copies, waits for them, and re-layouts  15.8 us (7%)
  between operations  13.8 us (7%)
  starting transfers between devices  10.2 us (5%)
  other arithmetic  3.95 us (2%)
    all_gather x1, waiting for transfers between devices, per_device(): down_mine = lax.all_gather(adapter_down_maps, 'chip', axis=0, tiled=True)  75.5 us
    all_gather x1, waiting for transfers between devices, per_device(): up_mine = lax.all_gather(adapter_up_maps, 'chip', axis=0, tiled=True)  46.1 us
    dot_general x4, matrix products, per_device(): part = jnp.dot(piece, w_rows, preferred_element_type=jnp.float32)  18 us
    select_n x4, local copies, waits for them, and re-layouts, expand(): jnp.where(mask[None, :, :, None], shrink[:, :, None, :], jnp.zeros((), jn...  12.4 us
    dot_general x2, matrix products, shrink_part(): lax.dot_general(token_rows, down_block, (((1,), (1,)), ((), ())), preferr...  11.7 us
    ppermute x6, starting transfers between devices, shift_all(): lax.ppermute(value, axis, [(i, (i + k) % count) for i in range(count)])  8.46 us
  transfers between devices with their start and end apart: 10, of which 3 were waited for; matrix products, arithmetic and copies ran while one was open for 23% of the time, Pallas kernels for 0%

profile of v1, /device:TPU:1, one launch (start us, length us, event | category | flops | bytes accessed | tf_op | source)
XLA Modules:
  0.0 212.0 jit_solution(5723543894141621354)
XLA Ops:
  6.5 0.0 all-gather.3.cloned.1.call-start
  6.5 0.7 all-gather.3.cloned.1.call-update
  7.3 0.0 all-gather.5.cloned.1.call-start
  7.3 0.7 all-gather.5.cloned.1.call-update
  8.0 75.5 %all-gather.3.cloned.1.call-done = bf16[2048,2048]{1,0:T(8,128)(2,1)} async-done(((bf16[128,2048]{1,0:T(8,128)(2,1)}), bf16[2048,2048]{1,0:T(8,128)(2,1)}) %all-gather.3.cloned.1.call-update) | async-done | bytes 8388624 | tf_op jit(solution)/shard_map/all_gather | solution.py:91
  83.5 0.8 collective-permute-start.3
  84.3 2.5 %collective-permute-start.2 = (bf16[256,2048]{1,0:T(8,128)(2,1)}, bf16[256,2048]{1,0:T(8,128)(2,1)S(1)}, u32[]{:S(2)}, u32[]{:S(2)}) collective-permute-start(bf16[256,2048]{1,0:T(8,128)(2,1)} %bitcast.113), channel_id=1, source_target_pairs={{0,3},{1,0},{2,1},{3,2},{4,7},{5,4},{6,5},{7,6},{8,11},{9,8},{10,9... | collective-permute-start | bytes 3145736 | tf_op jit(solution)/shard_map/ppermute | solution.py:24
  86.8 0.5 collective-permute-start.1
  87.3 0.6 collective-permute-start
  87.9 0.8 select_reduce_fusion.2
  88.9 0.7 iota_compare_fusion.1
  89.7 0.9 fusion.69
  90.6 46.1 %all-gather.5.cloned.1.call-done = bf16[2048,1024]{1,0:T(8,128)(2,1)} async-done(((bf16[128,1024]{1,0:T(8,128)(2,1)}), bf16[2048,1024]{1,0:T(8,128)(2,1)}) %all-gather.5.cloned.1.call-update) | async-done | bytes 4194320 | tf_op jit(solution)/shard_map/all_gather | solution.py:92
  136.7 0.8 collective-permute-start.7
  137.5 0.0 slice-start
  137.5 4.9 %fusion.6 = f32[1024,256]{1,0:T(8,128)} fusion(bf16[256,2048]{1,0:T(8,128)(2,1)} %bitcast.116, bf16[8192,1024]{1,0:T(8,128)(2,1)} %param.10, s32[]{:T(128)S(6)} %select_n.112), kind=kOutput, calls=%fused_computation.8 | convolution fusion | flops 1073741824 | bytes 6291460 | tf_op jit(solution)/shard_map/dot_general | solution.py:104
  142.5 0.0 slice-start.1
  142.5 0.0 copy-start.1
  142.5 0.0 collective-permute-done.2
  142.5 4.6 %fusion = f32[1024,256]{1,0:T(8,128)} fusion(bf16[256,2048]{1,0:T(8,128)(2,1)S(1)} %collective-permute-done.2, bf16[8192,1024]{1,0:T(8,128)(2,1)} %param.10, s32[]{:T(128)S(6)} %select_n.118), kind=kOutput, calls=%fused_computation.2 | convolution fusion | flops 1073741824 | bytes 6291460 | tf_op jit(solution)/shard_map/dot_general | solution.py:104
  147.1 0.0 slice-done
  147.1 0.0 slice-done.1
  147.1 0.0 copy-done.1
  147.1 4.8 %select_reduce_fusion.1 = f32[4,64,64]{2,1,0:T(8,128)S(1)} fusion(pred[64,32]{0,1:T(8,128)(4,1)S(1)} %get-tuple-element.13, bf16[32,64,2048,1]{2,1,0,3:T(8,128)(2,1)S(1)} %bitcast.112, bf16[4,64,2048]{2,1,0:T(8,128)(2,1)S(1)} %copy-done.1), kind=kOutput, calls=%fused_computation.1 | convolution fusion | flops 2148515840 | bytes 9504768 | tf_op jit(solution)/shard_map/dot_general | solution.py:117
  151.9 0.0 collective-permute-done.3
  151.9 6.9 %select_reduce_fusion = f32[4,64,64]{2,1,0:T(8,128)S(1)} fusion(pred[64,32]{0,1:T(8,128)(4,1)S(1)} %get-tuple-element.12, bf16[32,64,2048,1]{2,1,0,3:T(8,128)(2,1)} %bitcast.8, bf16[4,64,2048]{2,1,0:T(8,128)(2,1)S(1)} %copy-done.1), kind=kOutput, calls=%fused_computation | convolution fusion | flops 2148515840 | bytes 9504768 | tf_op jit(solution)/shard_map/dot_general | solution.py:117
  158.9 1.3 collective-permute-start.4
  160.2 2.4 %collective-permute-start.5 = (f32[4,64,64]{2,1,0:T(8,128)S(1)}, f32[4,64,64]{2,1,0:T(8,128)S(1)}, u32[]{:S(2)}, u32[]{:S(2)}) collective-permute-start(f32[4,64,64]{2,1,0:T(8,128)S(1)} %add.140), channel_id=1, source_target_pairs={{0,2},{1,3},{2,0},{3,1},{4,6},{5,7},{6,4},{7,5},{8,10},{9,11},{10,... | collective-permute-start | bytes 196616 | tf_op jit(solution)/shard_map/ppermute | solution.py:24
  162.6 0.0 collective-permute-done.1
  162.6 1.2 collective-permute-start.6
  163.8 4.5 %fusion.2 = f32[1024,256]{1,0:T(8,128)} fusion(bf16[256,2048]{1,0:T(8,128)(2,1)S(1)} %collective-permute-done.1, bf16[8192,1024]{1,0:T(8,128)(2,1)} %param.10, s32[]{:T(128)S(6)} %select_n.116), kind=kOutput, calls=%fused_computation.4 | convolution fusion | flops 1073741824 | bytes 6291460 | tf_op jit(solution)/shard_map/dot_general | solution.py:104
  168.2 0.0 collective-permute-done.4
  168.2 0.7 collective-permute-done.5
  169.0 0.0 collective-permute-done.6
  169.0 1.0 broadcast_select_fusion
  170.0 2.7 %copy.27 = bf16[4,64,32,64]{3,2,1,0:T(8,128)(2,1)} copy(bf16[4,64,32,64]{3,1,2,0:T(8,128)(2,1)S(1)} %get-tuple-element.11) | data formatting | bytes 2097152 | tf_op jit(solution)/shard_map/jit(_where)/select_n | solution.py:130
  172.7 3.4 %select_n.127 = bf16[256,2048]{1,0:T(8,128)(2,1)S(1)} reshape(bf16[4,64,32,64]{3,2,1,0:T(8,128)(2,1)} %copy.27) | data formatting | bytes 2097152 | tf_op jit(solution)/shard_map/jit(_where)/select_n | solution.py:130
  176.1 2.7 %copy.28 = bf16[4,64,32,64]{3,2,1,0:T(8,128)(2,1)} copy(bf16[4,64,32,64]{3,1,2,0:T(8,128)(2,1)S(1)} %get-tuple-element.10) | data formatting | bytes 2097152 | tf_op jit(solution)/shard_map/jit(_where)/select_n | solution.py:130
  178.8 3.6 %select_n.129 = bf16[256,2048]{1,0:T(8,128)(2,1)S(1)} reshape(bf16[4,64,32,64]{3,2,1,0:T(8,128)(2,1)} %copy.28) | data formatting | bytes 2097152 | tf_op jit(solution)/shard_map/jit(_where)/select_n | solution.py:130
  182.4 3.9 %fusion.72 = f32[256,1024]{0,1:T(8,128)S(1)} fusion(bf16[256,2048]{1,0:T(8,128)(2,1)S(1)} %select_n.127, bf16[2048,1024]{1,0:T(8,128)(2,1)} %all-gather.5.cloned.1.call-done), kind=kOutput, calls=%fused_computation.77 | convolution fusion | flops 1073741824 | bytes 6291456 | tf_op jit(solution)/shard_map/dot_general | solution.py:133
  186.3 0.0 copy-start.2
  186.4 0.0 copy-start.3
  186.4 0.0 copy-start.4
  186.4 0.0 collective-permute-done.7
  186.4 4.1 %convolution_add_fusion.1 = f32[256,1024]{0,1:T(8,128)S(1)} fusion(f32[256,1024]{0,1:T(8,128)S(1)} %fusion.72, bf16[256,2048]{1,0:T(8,128)(2,1)S(1)} %select_n.129, bf16[2048,1024]{1,0:T(8,128)(2,1)} %collective-permute-done.7), kind=kOutput, calls=%fused_computation.27 | convolution fusion | flops 1074003968 | bytes 7340032 | tf_op jit(solution)/shard_map/dot_general | solution.py:133
  190.5 0.0 collective-permute-done
  190.5 0.0 copy-done.2
  190.5 0.0 copy-done.3
  190.5 0.0 copy-done.4
  190.5 3.9 %fusion.36 = bf16[256,1024]{0,1:T(8,128)(2,1)S(1)} fusion(f32[256,1024]{0,1:T(8,128)S(1)} %convolution_add_fusion.1, f32[1024,256]{1,0:T(8,128)S(1)} %copy-done.3, f32[1024,256]{1,0:T(8,128)S(1)} %copy-done.4, f32[1024,256]{1,0:T(8,128)S(1)} %copy-done.2, bf16[256,2048]{1,0:T(8,128)(2,1)} %collective-permute-done, bf16[8192,1024]{1,0:T(8,128)(2,1)} %param.10, ...), kind=kOutput, calls=%fused_computation.28 | convolution fusion | flops 1075052544 | bytes 9961476 | tf_op jit(solution)/shard_map/dot_general | solution.py:104
  194.5 0.4 reshape.278
  194.9 1.0 copy.32
  195.9 0.0 copy-start
  195.9 3.1 %fusion.70 = (f32[4,64,8]{2,0,1:T(4,128)S(1)}, f32[4,64,1,8,128]{4,3,0,1,2:T(8,128)S(1)}) fusion(bf16[4,64,8,128]{3,2,0,1:T(8,128)(2,1)S(1)} %copy.32, bf16[2,64,128,128]{3,2,1,0:T(8,128)(2,1)} %param.13, pred[64,128]{1,0:T(8,128)(4,1)S(1)} %iota_compare_fusion.1), kind=kOutput, calls=%fused_computation.75 | convolution fusion | flops 67893248 | bytes 3686400 | tf_op jit(solution)/shard_map/trkgd,rckd->trkgc/dot_general | solution.py:41
  199.0 2.4 %fusion.71 = (f32[4,64,8]{2,0,1:T(4,128)S(1)}, f32[4,64,1,8,4]{3,4,0,1,2:T(4,128)S(1)}) fusion(bf16[4,64,8,128]{3,2,0,1:T(8,128)(2,1)S(1)} %copy.32, bf16[4,1,64,128]{3,2,1,0:T(8,128)(2,1)S(1)} %get-tuple-element.9, pred[4,4]{1,0:T(4,128)(4,1)S(1)} %iota_compare_fusion.3), kind=kOutput, calls=%fused_computation.76 | convolution fusion | flops 2119680 | bytes 630800 | tf_op jit(solution)/shard_map/trkgd,srkd->trkgs/dot_general | solution.py:46
  201.5 0.7 fusion.49
  202.2 0.0 copy-done
  202.2 0.7 fusion.8
  202.9 0.5 fusion.54
  203.5 0.6 divide_convert_fusion
  204.1 0.1 convert_element_type.30
  204.2 1.0 copy.36
  (9 shorter events, 0.2 us)
Async XLA Ops:
  6.5 76.9 %all-gather.3.cloned.1.call-start = ((), (), s32[]{:S(2)}) async-start(), calls=%async_computation | async-start | bytes 8912896 | tf_op jit(solution)/shard_map/all_gather | solution.py:91
  7.3 129.4 %all-gather.5.cloned.1.call-start = ((), (), s32[]{:S(2)}) async-start(), calls=%async_computation.1 | async-start | bytes 4456448 | tf_op jit(solution)/shard_map/all_gather | solution.py:92
  83.5 68.4 %collective-permute-start.3 = (bf16[2048,2048]{1,0:T(8,128)(2,1)}, bf16[2048,2048]{1,0:T(8,128)(2,1)}, u32[]{:S(2)}, u32[]{:S(2)}) collective-permute-start(bf16[2048,2048]{1,0:T(8,128)(2,1)} %all-gather.3.cloned.1.call-done), channel_id=1, source_target_pairs={{0,4},{4,0},{1,5},{5,1},{2,6},{6,2},{3,7},{7,3},{8,12},{12,8},{9,1... | collective-permute-start | bytes 25165832 | tf_op jit(solution)/shard_map/ppermute | solution.py:94
  84.3 58.2 %collective-permute-start.2 = (bf16[256,2048]{1,0:T(8,128)(2,1)}, bf16[256,2048]{1,0:T(8,128)(2,1)S(1)}, u32[]{:S(2)}, u32[]{:S(2)}) collective-permute-start(bf16[256,2048]{1,0:T(8,128)(2,1)} %bitcast.113), channel_id=1, source_target_pairs={{0,3},{1,0},{2,1},{3,2},{4,7},{5,4},{6,5},{7,6},{8,11},{9,8},{10,9... | collective-permute-start | bytes 3145736 | tf_op jit(solution)/shard_map/ppermute | solution.py:24
  86.8 75.8 %collective-permute-start.1 = (bf16[256,2048]{1,0:T(8,128)(2,1)}, bf16[256,2048]{1,0:T(8,128)(2,1)S(1)}, u32[]{:S(2)}, u32[]{:S(2)}) collective-permute-start(bf16[256,2048]{1,0:T(8,128)(2,1)} %bitcast.114), channel_id=1, source_target_pairs={{0,2},{1,3},{2,0},{3,1},{4,6},{5,7},{6,4},{7,5},{8,10},{9,11},{10,... | collective-permute-start | bytes 3145736 | tf_op jit(solution)/shard_map/ppermute | solution.py:24
  87.3 103.2 %collective-permute-start = (bf16[256,2048]{1,0:T(8,128)(2,1)}, bf16[256,2048]{1,0:T(8,128)(2,1)}, u32[]{:S(2)}, u32[]{:S(2)}) collective-permute-start(bf16[256,2048]{1,0:T(8,128)(2,1)} %bitcast.115), channel_id=1, source_target_pairs={{0,1},{1,2},{2,3},{3,0},{4,5},{5,6},{6,7},{7,4},{8,9},{9,10},{10,1... | collective-permute-start | bytes 3145736 | tf_op jit(solution)/shard_map/ppermute | solution.py:24
  136.7 49.7 %collective-permute-start.7 = (bf16[2048,1024]{1,0:T(8,128)(2,1)}, bf16[2048,1024]{1,0:T(8,128)(2,1)}, u32[]{:S(2)}, u32[]{:S(2)}) collective-permute-start(bf16[2048,1024]{1,0:T(8,128)(2,1)} %all-gather.5.cloned.1.call-done), channel_id=1, source_target_pairs={{0,4},{4,0},{1,5},{5,1},{2,6},{6,2},{3,7},{7,3},{8,12},{12,8},{9,1... | collective-permute-start | bytes 12582920 | tf_op jit(solution)/shard_map/ppermute | solution.py:95
  137.5 9.6 %slice-start = ((s8[8388608]{0:T(1024)(128)(4,1)}), s8[4194304]{0:T(1024)(128)(4,1)S(1)}, s32[]{:S(2)}) async-start(s8[8388608]{0:T(1024)(128)(4,1)} %bitcast.110), calls=%async_computation.2 | async-start | bytes 8388608
  142.5 4.6 %slice-start.1 = ((s8[8388608]{0:T(1024)(128)(4,1)}), s8[4194304]{0:T(1024)(128)(4,1)S(1)}, s32[]{:S(2)}) async-start(s8[8388608]{0:T(1024)(128)(4,1)} %bitcast.110), calls=%async_computation.3 | async-start | bytes 8388608
  142.5 4.6 %copy-start.1 = (bf16[4,64,2048]{2,1,0:T(8,128)(2,1)S(1)}, bf16[4,64,2048]{2,1,0:T(8,128)(2,1)}, u32[]{:S(2)}) copy-start(bf16[4,64,2048]{2,1,0:T(8,128)(2,1)} %param.9) | copy-start | bytes 3145732
  158.9 9.4 %collective-permute-start.4 = (f32[4,64,64]{2,1,0:T(8,128)S(1)}, f32[4,64,64]{2,1,0:T(8,128)S(1)}, u32[]{:S(2)}, u32[]{:S(2)}) collective-permute-start(f32[4,64,64]{2,1,0:T(8,128)S(1)} %add.140), channel_id=1, source_target_pairs={{0,1},{1,2},{2,3},{3,0},{4,5},{5,6},{6,7},{7,4},{8,9},{9,10},{10,1... | collective-permute-start | bytes 196616 | tf_op jit(solution)/shard_map/ppermute | solution.py:24
  160.2 8.8 %collective-permute-start.5 = (f32[4,64,64]{2,1,0:T(8,128)S(1)}, f32[4,64,64]{2,1,0:T(8,128)S(1)}, u32[]{:S(2)}, u32[]{:S(2)}) collective-permute-start(f32[4,64,64]{2,1,0:T(8,128)S(1)} %add.140), channel_id=1, source_target_pairs={{0,2},{1,3},{2,0},{3,1},{4,6},{5,7},{6,4},{7,5},{8,10},{9,11},{10,... | collective-permute-start | bytes 196616 | tf_op jit(solution)/shard_map/ppermute | solution.py:24
  162.6 6.4 %collective-permute-start.6 = (f32[4,64,64]{2,1,0:T(8,128)S(1)}, f32[4,64,64]{2,1,0:T(8,128)S(1)}, u32[]{:S(2)}, u32[]{:S(2)}) collective-permute-start(f32[4,64,64]{2,1,0:T(8,128)S(1)} %add.140), channel_id=1, source_target_pairs={{0,3},{1,0},{2,1},{3,2},{4,7},{5,4},{6,5},{7,6},{8,11},{9,8},{10,9... | collective-permute-start | bytes 196616 | tf_op jit(solution)/shard_map/ppermute | solution.py:24
  186.3 4.2 %copy-start.2 = (f32[1024,256]{1,0:T(8,128)S(1)}, f32[1024,256]{1,0:T(8,128)}, u32[]{:S(2)}) copy-start(f32[1024,256]{1,0:T(8,128)} %fusion.6) | copy-start | bytes 3145732
  186.4 4.2 %copy-start.3 = (f32[1024,256]{1,0:T(8,128)S(1)}, f32[1024,256]{1,0:T(8,128)}, u32[]{:S(2)}) copy-start(f32[1024,256]{1,0:T(8,128)} %fusion) | copy-start | bytes 3145732
  186.4 4.2 %copy-start.4 = (f32[1024,256]{1,0:T(8,128)S(1)}, f32[1024,256]{1,0:T(8,128)}, u32[]{:S(2)}) copy-start(f32[1024,256]{1,0:T(8,128)} %fusion.2) | copy-start | bytes 3145732
  195.9 6.3 %copy-start = (bf16[2,64,128,128]{3,2,1,0:T(8,128)(2,1)S(1)}, bf16[2,64,128,128]{3,2,1,0:T(8,128)(2,1)}, u32[]{:S(2)}) copy-start(bf16[2,64,128,128]{3,2,1,0:T(8,128)(2,1)} %param.13) | copy-start | bytes 12582916
Sparse Core Ops, SparseCore 0:
  9.5 73.9 all-gather.2
  85.6 51.0 all-gather.4

commit v2 on v0

--- a/solution.py
+++ b/solution.py
@@ -13,14 +13,6 @@
     table = jnp.arange(adapter_pool_position.shape[0], dtype=jnp.int32)
     match = adapters[:, None] == table[None, :]
     return jnp.sum(jnp.where(match, adapter_pool_position[None, :], 0), axis=1)
-
-
-def adapt_rows(normed_hidden_state, down_map_pages, up_map_pages):
-    shrink_local = jnp.einsum(
-        "trd,rjd->trj", normed_hidden_state, down_map_pages, preferred_element_type=jnp.float32
-    )
-    shrink = lax.psum(shrink_local, "tensor").astype(jnp.bfloat16)
-    return jnp.einsum("trj,rjh->trh", shrink, up_map_pages, preferred_element_type=jnp.float32)
 
 
 def attend(query, key_value_cache, step_key_value, cache_valid_length):
@@ -68,6 +60,11 @@
     return attended.reshape(steps, requests, -1).astype(jnp.bfloat16)
 
 
+def gather_tensor(value, axis_name, count):
+    tiled = jnp.broadcast_to(value[None], (count,) + value.shape)
+    return lax.all_to_all(tiled, axis_name, 0, 0, tiled=True)
+
+
 def per_device(
     normed_hidden_state,
     query_projection_weight,
@@ -81,22 +78,34 @@
 ):
     steps, requests, part_width = normed_hidden_state.shape
     count_rows = steps * requests
+    heads_width = query_projection_weight.shape[1]
+    n_tensor = query_projection_weight.shape[0] // part_width
     token_rows = normed_hidden_state.reshape(count_rows, part_width)
-    heads_width = query_projection_weight.shape[1]
+
+    down_all = lax.all_gather(adapter_down_maps, "dp", axis=0, tiled=True)
+    up_all = lax.all_gather(adapter_up_maps, "dp", axis=0, tiled=True)
+    n_pool = down_all.shape[0] // ADAPTER_RANK
+
+    pieces = gather_tensor(token_rows, "tensor", n_tensor)
+    full_rows = jnp.transpose(pieces, (1, 0, 2)).reshape(count_rows, n_tensor * part_width)
+    base = jnp.dot(full_rows, query_projection_weight, preferred_element_type=jnp.float32)
+
     position = pool_lookup(adapter_per_request, adapter_pool_position)
-    base = jnp.dot(
-        lax.all_gather(token_rows, "tensor", axis=1, tiled=True),
-        query_projection_weight,
-        preferred_element_type=jnp.float32,
+    onehot = position[:, None] == jnp.arange(n_pool, dtype=jnp.int32)[None, :]
+    full = lax.dot_general(
+        token_rows, down_all, (((1,), (1,)), ((), ())), preferred_element_type=jnp.float32
+    ).reshape(steps, requests, n_pool, ADAPTER_RANK)
+    shrink_local = jnp.sum(jnp.where(onehot[None, :, :, None], full, 0.0), axis=2)
+    partials = gather_tensor(shrink_local, "tensor", n_tensor)
+    shrink = partials[0]
+    for j in range(1, n_tensor):
+        shrink = shrink + partials[j]
+    shrink = shrink.astype(jnp.bfloat16)
+    wide = jnp.where(onehot[None, :, :, None], shrink[:, :, None, :], jnp.zeros((), jnp.bfloat16))
+    delta = jnp.dot(
+        wide.reshape(count_rows, n_pool * ADAPTER_RANK), up_all, preferred_element_type=jnp.float32
     )
-    down_all, up_all = (
-        lax.all_gather(adapter_down_maps, "dp", axis=0, tiled=True),
-        lax.all_gather(adapter_up_maps, "dp", axis=0, tiled=True),
-    )
-    down_map_pages = jnp.take(down_all.reshape(-1, ADAPTER_RANK, part_width), position, axis=0)
-    up_map_pages = jnp.take(up_all.reshape(-1, ADAPTER_RANK, heads_width), position, axis=0)
-    delta = adapt_rows(normed_hidden_state, down_map_pages, up_map_pages)
-    query = (base.reshape(steps, requests, heads_width) + delta).astype(jnp.bfloat16)
+    query = (base + delta).reshape(steps, requests, heads_width).astype(jnp.bfloat16)
     return attend(query, key_value_cache, step_key_value, cache_valid_length)
 
 

time: 252 us -> 191 us (0.76)
  waiting for transfers between devices: 163 us -> 111 us
  blocking collectives: 14.8 us -> 0 us
  starting transfers between devices: 0.08 us -> 9.03 us
  local copies, waits for them, and re-layouts: 24.5 us -> 16.5 us
  matrix products: 30.9 us -> 34.6 us
    all_gather x3 -> x2, waiting for transfers between devices: 161 us -> 87.1 us  [the longest x1 77 us: per_device(): down_all = lax.all_gather(adapter_down_maps, 'dp', axis=0, tiled=True)]
    all_to_all x0 -> x2, waiting for transfers between devices: none -> 22.8 us  [gather_tensor(): return lax.all_to_all(tiled, axis_name, 0, 0, tiled=True)]
    gather x2 -> x0, local copies, waits for them, and re-layouts: 22.3 us -> none  [the longest x1 13.4 us: per_device(): jnp.take(down_all.reshape(-1, ADAPTER_RANK, part_width), position, axis=0)]
    psum x1 -> x0, blocking collectives: 14.8 us -> none  [adapt_rows(): shrink = lax.psum(shrink_local, 'tensor').astype(jnp.bfloat16)]
    select_n x0 -> x2, local copies, waits for them, and re-layouts: none -> 10.7 us  [per_device(): jnp.where(onehot[None, :, :, None], shrink[:, :, None, :], jnp.zeros((),...]
    all_to_all x0 -> x2, starting transfers between devices: none -> 8.99 us  [gather_tensor(): return lax.all_to_all(tiled, axis_name, 0, 0, tiled=True)]
    dot_general x3, matrix products: 22.6 us -> 29.4 us  [the longest x1 12.1 us: per_device(): lax.dot_general(token_rows, down_all, (((1,), (1,)), ((), ())), preferred...]
    broadcast_in_dim x0 -> x3, local copies, waits for them, and re-layouts: none -> 2.8 us  [gather_tensor(): tiled = jnp.broadcast_to(value[None], (count,) + value.shape)]
  transfers between devices with their start and end apart: 3 -> 4, of which waited for: 3 -> 4; matrix products, arithmetic and copies ran while one was open for 8% -> 19% of each run, Pallas kernels for 0% -> 0%
where the time goes in v2:
time: 191 us; the launch traced here: 190 us
  waiting for transfers between devices  111 us (58%)
  matrix products  34.6 us (18%)
  local copies, waits for them, and re-layouts  16.5 us (9%)
  between operations  13.6 us (7%)
  starting transfers between devices  9.03 us (5%)
  other arithmetic  4.77 us (2%)
    all_gather x1, waiting for transfers between devices, per_device(): down_all = lax.all_gather(adapter_down_maps, 'dp', axis=0, tiled=True)  77 us
    all_to_all x2, waiting for transfers between devices, gather_tensor(): return lax.all_to_all(tiled, axis_name, 0, 0, tiled=True)  22.8 us
    dot_general x1, matrix products, per_device(): lax.dot_general(token_rows, down_all, (((1,), (1,)), ((), ())), preferred...  12.1 us
    dot_general x1, matrix products, per_device(): jnp.dot(full_rows, query_projection_weight, preferred_element_type=jnp.fl...  11.7 us
    select_n x2, local copies, waits for them, and re-layouts, per_device(): jnp.where(onehot[None, :, :, None], shrink[:, :, None, :], jnp.zeros((),...  10.7 us
    all_gather x1, waiting for transfers between devices, per_device(): up_all = lax.all_gather(adapter_up_maps, 'dp', axis=0, tiled=True)  10.1 us
    all_to_all x2, starting transfers between devices, gather_tensor(): return lax.all_to_all(tiled, axis_name, 0, 0, tiled=True)  8.99 us
    dot_general x1, matrix products, per_device(): jnp.dot(wide.reshape(count_rows, n_pool * ADAPTER_RANK), up_all, preferre...  5.7 us
  transfers between devices with their start and end apart: 4, of which 4 were waited for; matrix products, arithmetic and copies ran while one was open for 19% of the time, Pallas kernels for 0%

profile of v2, /device:TPU:1, one launch (start us, length us, event | category | flops | bytes accessed | tf_op | source)
XLA Modules:
  0.0 189.7 jit_solution(7043627760312760634)
XLA Ops:
  6.5 0.0 all-gather.3.cloned.1.call-start
  6.5 0.7 all-gather.3.cloned.1.call-update
  7.3 0.0 all-gather.5.cloned.1.call-start
  7.3 0.7 all-gather.5.cloned.1.call-update
  8.0 0.8 select_reduce_fusion.1
  8.9 77.0 %all-gather.3.cloned.1.call-done = bf16[4096,2048]{1,0:T(8,128)(2,1)} async-done(((bf16[128,2048]{1,0:T(8,128)(2,1)}), bf16[4096,2048]{1,0:T(8,128)(2,1)}) %all-gather.3.cloned.1.call-update) | async-done | bytes 16777232 | tf_op jit(solution)/shard_map/all_gather | solution.py:85
  85.9 0.0 copy-start.1
  85.9 12.1 %select_reduce_fusion = f32[4,64,64]{2,1,0:T(8,128)S(1)} fusion(pred[64,64]{0,1:T(8,128)(4,1)S(1)} %iota_compare_fusion, bf16[64,64,2048,1]{2,1,0,3:T(8,128)(2,1)} %bitcast.112, bf16[4,64,2048]{2,1,0:T(8,128)(2,1)} %param.9), kind=kOutput, calls=%fused_computation | convolution fusion | flops 4297048064 | bytes 17895424 | tf_op jit(solution)/shard_map/dot_general | solution.py:95
  98.0 1.0 reshape.179
  99.1 4.0 %all-to-all-start.1 = ((f32[4,1,16384]{2,1,0:T(1,128)}), f32[4,1,16384]{2,1,0:T(1,128)S(1)}, u32[]{:S(2)}, u32[]{:S(2)}) async-start(f32[4,1,16384]{2,1,0:T(1,128)} %reshape.179), calls=%async_computation.1 | async-start | bytes 524288 | tf_op jit(solution)/shard_map/all_to_all | solution.py:65
  103.1 0.0 copy-done.1
  103.1 0.5 copy.22
  103.6 5.4 %all-to-all-done.1 = f32[4,1,16384]{2,1,0:T(1,128)S(1)} async-done(((f32[4,1,16384]{2,1,0:T(1,128)}), f32[4,1,16384]{2,1,0:T(1,128)S(1)}, u32[]{:S(2)}, u32[]{:S(2)}) %all-to-all-start.1) | async-done | bytes 262176 | tf_op jit(solution)/shard_map/all_to_all | solution.py:65
  109.0 2.2 %broadcast_in_dim.98 = bf16[4,256,2048]{1,2,0:T(8,128)(2,1)} broadcast(bf16[256,2048]{0,1:T(8,128)(2,1)S(1)} %copy.22), dimensions={1,2} | broadcast | bytes 5242880 | tf_op jit(solution)/shard_map/broadcast_in_dim | solution.py:64
  111.2 0.0 copy-start.3
  111.2 0.0 copy-start.2
  111.2 5.0 %all-to-all-start = ((bf16[4,256,2048]{1,2,0:T(8,128)(2,1)}), bf16[4,256,2048]{1,2,0:T(8,128)(2,1)}, u32[]{:S(2)}, u32[]{:S(2)}) async-start(bf16[4,256,2048]{1,2,0:T(8,128)(2,1)} %broadcast_in_dim.98), calls=%async_computation | async-start | bytes 8388608 | tf_op jit(solution)/shard_map/all_to_all | solution.py:65
  116.3 0.0 copy-done.3
  116.3 0.1 iota_compare_fusion.2
  116.3 0.0 copy-done.2
  116.4 0.5 broadcast.56
  116.9 1.4 reduce.4
  118.2 0.3 reshape.180
  118.6 1.1 broadcast_select_fusion
  119.7 4.7 %copy.23 = bf16[4,64,64,64]{3,2,1,0:T(8,128)(2,1)} copy(bf16[4,64,64,64]{3,1,2,0:T(8,128)(2,1)S(1)} %broadcast_select_fusion) | data formatting | bytes 4194304 | tf_op jit(solution)/shard_map/jit(_where)/select_n | solution.py:104
  124.4 6.0 %select_n.30 = bf16[256,4096]{1,0:T(8,128)(2,1)S(1)} reshape(bf16[4,64,64,64]{3,2,1,0:T(8,128)(2,1)} %copy.23) | data formatting | bytes 4194304 | tf_op jit(solution)/shard_map/jit(_where)/select_n | solution.py:104
  130.4 10.1 %all-gather.5.cloned.1.call-done = bf16[4096,1024]{1,0:T(8,128)(2,1)} async-done(((bf16[128,1024]{1,0:T(8,128)(2,1)}), bf16[4096,1024]{1,0:T(8,128)(2,1)}) %all-gather.5.cloned.1.call-update) | async-done | bytes 8388624 | tf_op jit(solution)/shard_map/all_gather | solution.py:86
  140.4 5.7 %fusion.41 = f32[256,1024]{1,0:T(8,128)S(1)} fusion(bf16[256,4096]{1,0:T(8,128)(2,1)S(1)} %select_n.30, bf16[4096,1024]{1,0:T(8,128)(2,1)} %all-gather.5.cloned.1.call-done), kind=kOutput, calls=%fused_computation.49 | convolution fusion | flops 2147483648 | bytes 11534336 | tf_op jit(solution)/shard_map/dot_general | solution.py:105
  146.2 17.4 %all-to-all-done = bf16[4,256,2048]{1,2,0:T(8,128)(2,1)} async-done(((bf16[4,256,2048]{1,2,0:T(8,128)(2,1)}), bf16[4,256,2048]{1,2,0:T(8,128)(2,1)}, u32[]{:S(2)}, u32[]{:S(2)}) %all-to-all-start) | async-done | bytes 4194336 | tf_op jit(solution)/shard_map/all_to_all | solution.py:65
  163.5 0.0 copy-start
  163.5 11.7 %fusion.21 = bf16[32,8,8,128]{3,1,2,0:T(8,128)(2,1)S(1)} fusion(f32[256,1024]{1,0:T(8,128)S(1)} %fusion.41, bf16[256,8192]{0,1:T(8,128)(2,1)} %bitcast.2, bf16[8192,1024]{1,0:T(8,128)(2,1)} %param.10), kind=kOutput, calls=%fused_computation.18 | convolution fusion | flops 4295491584 | bytes 22544384 | tf_op jit(solution)/shard_map/dot_general | solution.py:91
  175.2 0.1 copy.36
  175.3 2.5 %fusion.40 = (f32[4,64,8]{2,0,1:T(4,128)S(1)}, f32[4,64,1,8,4]{3,4,0,1,2:T(4,128)S(1)}) fusion(bf16[4,1,64,128]{3,2,1,0:T(8,128)(2,1)S(1)} %get-tuple-element.6, pred[4,4]{1,0:T(4,128)(4,1)S(1)} %iota_compare_fusion.3, bf16[4,64,8,128]{3,2,1,0:T(8,128)(2,1)S(1)} %bitcast.109), kind=kOutput, calls=%fused_computation.48 | convolution fusion | flops 2119680 | bytes 630800 | tf_op jit(solution)/shard_map/trkgd,srkd->trkgs/dot_general | solution.py:36
  177.8 0.0 copy-done
  177.8 1.3 fusion.39
  179.2 0.7 fusion.24
  179.9 0.7 fusion
  180.7 0.5 fusion.31
  181.2 0.6 divide_convert_fusion
  181.8 0.1 convert_element_type.38
  181.9 1.0 copy.28
  (7 shorter events, 0.2 us)
Async XLA Ops:
  6.5 79.4 %all-gather.3.cloned.1.call-start = ((), (), s32[]{:S(2)}) async-start(), calls=%async_computation.2 | async-start | bytes 17301504 | tf_op jit(solution)/shard_map/all_gather | solution.py:85
  7.3 133.2 %all-gather.5.cloned.1.call-start = ((), (), s32[]{:S(2)}) async-start(), calls=%async_computation.3 | async-start | bytes 8650752 | tf_op jit(solution)/shard_map/all_gather | solution.py:86
  85.9 17.2 %copy-start.1 = (bf16[4,64,2048]{2,1,0:T(8,128)(2,1)S(1)}, bf16[4,64,2048]{2,1,0:T(8,128)(2,1)}, u32[]{:S(2)}) copy-start(bf16[4,64,2048]{2,1,0:T(8,128)(2,1)} %param.9) | copy-start | bytes 3145732
  99.1 9.9 %all-to-all-start.1 = ((f32[4,1,16384]{2,1,0:T(1,128)}), f32[4,1,16384]{2,1,0:T(1,128)S(1)}, u32[]{:S(2)}, u32[]{:S(2)}) async-start(f32[4,1,16384]{2,1,0:T(1,128)} %reshape.179), calls=%async_computation.1 | async-start | bytes 524288 | tf_op jit(solution)/shard_map/all_to_all | solution.py:65
  111.2 5.0 %copy-start.3 = (s32[64]{0:T(128)S(1)}, s32[64]{0:T(128)}, u32[]{:S(2)}) copy-start(s32[64]{0:T(128)} %param.15) | copy-start | bytes 772
  111.2 5.1 %copy-start.2 = (bf16[4,2,64,128]{3,2,1,0:T(8,128)(2,1)S(1)}, bf16[4,2,64,128]{3,2,1,0:T(8,128)(2,1)}, u32[]{:S(2)}) copy-start(bf16[4,2,64,128]{3,2,1,0:T(8,128)(2,1)} %param.14) | copy-start | bytes 393220
  111.2 52.3 %all-to-all-start = ((bf16[4,256,2048]{1,2,0:T(8,128)(2,1)}), bf16[4,256,2048]{1,2,0:T(8,128)(2,1)}, u32[]{:S(2)}, u32[]{:S(2)}) async-start(bf16[4,256,2048]{1,2,0:T(8,128)(2,1)} %broadcast_in_dim.98), calls=%async_computation | async-start | bytes 8388608 | tf_op jit(solution)/shard_map/all_to_all | solution.py:65
  163.5 14.3 %copy-start = (bf16[2,64,128,128]{3,2,1,0:T(8,128)(2,1)S(1)}, bf16[2,64,128,128]{3,2,1,0:T(8,128)(2,1)}, u32[]{:S(2)}) copy-start(bf16[2,64,128,128]{3,2,1,0:T(8,128)(2,1)} %param.13) | copy-start | bytes 12582916
Sparse Core Ops, SparseCore 0:
  9.6 76.2 all-gather.2
  88.2 52.2 all-gather.4

commit v3 on v2

--- a/solution.py
+++ b/solution.py
@@ -83,12 +83,14 @@
     token_rows = normed_hidden_state.reshape(count_rows, part_width)
 
     down_all = lax.all_gather(adapter_down_maps, "dp", axis=0, tiled=True)
-    up_all = lax.all_gather(adapter_up_maps, "dp", axis=0, tiled=True)
     n_pool = down_all.shape[0] // ADAPTER_RANK
 
     pieces = gather_tensor(token_rows, "tensor", n_tensor)
     full_rows = jnp.transpose(pieces, (1, 0, 2)).reshape(count_rows, n_tensor * part_width)
     base = jnp.dot(full_rows, query_projection_weight, preferred_element_type=jnp.float32)
+
+    up_local, down_all, base = lax.optimization_barrier((adapter_up_maps, down_all, base))
+    up_all = lax.all_gather(up_local, "dp", axis=0, tiled=True)
 
     position = pool_lookup(adapter_per_request, adapter_pool_position)
     onehot = position[:, None] == jnp.arange(n_pool, dtype=jnp.int32)[None, :]

time: 191 us -> 161 us (0.84)
  waiting for transfers between devices: 111 us -> 26.9 us
  blocking collectives: 0 us -> 52.7 us
  other arithmetic: 4.77 us -> 14.3 us
  starting transfers between devices: 9.03 us -> 4.05 us
  matrix products: 34.6 us -> 30.1 us
  local copies, waits for them, and re-layouts: 16.5 us -> 19.2 us
    all_gather x1, waiting for transfers between devices: 77 us -> 15.2 us  [per_device(): down_all = lax.all_gather(adapter_down_maps, 'dp', axis=0, tiled=True)]
    all_to_all x0 -> x1, blocking collectives: none -> 52.7 us  [gather_tensor(): return lax.all_to_all(tiled, axis_name, 0, 0, tiled=True)]
    all_to_all x2 -> x1, waiting for transfers between devices: 22.8 us -> 5.96 us  [gather_tensor(): return lax.all_to_all(tiled, axis_name, 0, 0, tiled=True)]
    reshape x0 -> x1, local copies, waits for them, and re-layouts: none -> 8.07 us  [per_device(): full = lax.dot_general(token_rows, down_all, (((1,), (1,)), ((), ())), pr...]
    reduce_sum x0 -> x1, other arithmetic: none -> 8.01 us  [per_device(): jnp.sum(jnp.where(onehot[None, :, :, None], full, 0.0), axis=2)]
    all_gather x1, waiting for transfers between devices: 10.1 us -> 5.02 us  [per_device(): up_all = lax.all_gather(up_local, 'dp', axis=0, tiled=True)]
    all_to_all x2 -> x1, starting transfers between devices: 8.99 us -> 4.01 us  [gather_tensor(): return lax.all_to_all(tiled, axis_name, 0, 0, tiled=True)]
    select_n x2 -> x1, local copies, waits for them, and re-layouts: 10.7 us -> 5.99 us  [per_device(): jnp.where(onehot[None, :, :, None], shrink[:, :, None, :], jnp.zeros((),...]
  transfers between devices with their start and end apart: 4 -> 3, of which waited for: 4 -> 3; matrix products, arithmetic and copies ran while one was open for 19% -> 31% of each run, Pallas kernels for 0% -> 0%
where the time goes in v3:
time: 161 us
  blocking collectives  52.7 us (33%)
  matrix products  30.1 us (19%)
  waiting for transfers between devices  26.9 us (17%)
  local copies, waits for them, and re-layouts  19.2 us (12%)
  other arithmetic  14.3 us (9%)
  between operations  13.6 us (8%)
  starting transfers between devices  4.05 us (3%)
    all_to_all x1, blocking collectives, gather_tensor(): return lax.all_to_all(tiled, axis_name, 0, 0, tiled=True)  52.7 us
    all_gather x1, waiting for transfers between devices, per_device(): down_all = lax.all_gather(adapter_down_maps, 'dp', axis=0, tiled=True)  15.2 us
    dot_general x1, matrix products, per_device(): lax.dot_general(token_rows, down_all, (((1,), (1,)), ((), ())), preferred...  10.1 us
    dot_general x1, matrix products, per_device(): jnp.dot(full_rows, query_projection_weight, preferred_element_type=jnp.fl...  8.91 us
    reshape x1, local copies, waits for them, and re-layouts, per_device(): full = lax.dot_general(token_rows, down_all, (((1,), (1,)), ((), ())), pr...  8.07 us
    reduce_sum x1, other arithmetic, per_device(): jnp.sum(jnp.where(onehot[None, :, :, None], full, 0.0), axis=2)  8.01 us
    select_n x1, local copies, waits for them, and re-layouts, per_device(): jnp.where(onehot[None, :, :, None], shrink[:, :, None, :], jnp.zeros((),...  5.99 us
    all_to_all x1, waiting for transfers between devices, gather_tensor(): return lax.all_to_all(tiled, axis_name, 0, 0, tiled=True)  5.96 us
  transfers between devices with their start and end apart: 3, of which 3 were waited for; matrix products, arithmetic and copies ran while one was open for 31% of the time, Pallas kernels for 0%

profile of v3, /device:TPU:1, one launch (start us, length us, event | category | flops | bytes accessed | tf_op | source)
XLA Modules:
  0.0 160.9 jit_solution(7092207523622909441)
XLA Ops:
  6.5 0.0 all-gather.3.cloned.1.call-start
  6.5 0.7 all-gather.3.cloned.1.call-update
  7.3 0.0 all-gather.5.cloned.1.call-start
  7.3 1.5 copy.21
  8.8 0.3 broadcast_in_dim.98
  9.1 52.7 %all_to_all.10 = bf16[4,256,2048]{1,2,0:T(8,128)(2,1)S(1)} all-to-all(bf16[4,256,2048]{1,2,0:T(8,128)(2,1)S(1)} %broadcast_in_dim.98), channel_id=1, replica_groups=mesh['dp'=32,'tensor'=4] {'tensor'}, dimensions={0} | all-to-all | bytes 8388608 | tf_op jit(solution)/shard_map/all_to_all | solution.py:65
  61.8 0.0 copy-start.4
  61.8 0.0 copy-start.5
  61.8 0.0 copy-start.2
  61.8 0.0 copy-start.1
  61.8 8.9 %fusion.40 = f32[256,1024]{1,0:T(8,128)S(1)} fusion(bf16[256,8192]{0,1:T(8,128)(2,1)S(1)} %bitcast.109, bf16[8192,1024]{1,0:T(8,128)(2,1)} %param.10), kind=kOutput, calls=%fused_computation.50 | convolution fusion | flops 4294967296 | bytes 22020096 | tf_op jit(solution)/shard_map/dot_general | solution.py:90
  70.7 15.2 %all-gather.3.cloned.1.call-done = bf16[4096,2048]{1,0:T(8,128)(2,1)} async-done(((bf16[128,2048]{1,0:T(8,128)(2,1)}), bf16[4096,2048]{1,0:T(8,128)(2,1)}) %all-gather.3.cloned.1.call-update) | async-done | bytes 16777232 | tf_op jit(solution)/shard_map/all_gather | solution.py:85
  85.9 0.0 all-gather.5.cloned.1.call-update
  85.9 0.0 copy-done.4
  86.0 0.0 copy-done.5
  86.0 0.2 select_reduce_fusion.1
  86.2 0.0 copy-done.2
  86.2 0.0 copy-done.1
  86.2 10.1 %convolution_bitcast_fusion = f32[256,4096]{0,1:T(8,128)} fusion(bf16[4096,2048]{1,0:T(8,128)(2,1)} %all-gather.3.cloned.1.call-done, bf16[256,2048]{1,0:T(8,128)(2,1)S(1)} %bitcast.114), kind=kOutput, calls=%fused_computation.1 | convolution fusion | flops 4294967296 | bytes 22020096 | tf_op jit(solution)/shard_map/dot_general | solution.py:97
  96.4 8.1 %reshape.166 = f32[4,64,64,64]{1,0,3,2:T(4,128)} reshape(f32[256,4096]{0,1:T(8,128)} %convolution_bitcast_fusion) | data formatting | bytes 8388608 | tf_op jit(solution)/shard_map/reshape | solution.py:99
  104.4 0.0 copy-start.3
  104.4 8.0 %select_reduce_fusion = f32[4,64,64]{1,0,2:T(4,128)S(1)} fusion(f32[4,64,64,64]{1,0,3,2:T(4,128)} %reshape.166, pred[64,64]{0,1:T(8,128)(4,1)S(1)} %iota_compare_fusion), kind=kLoop, calls=%fused_computation | loop fusion | flops 2080768 | bytes 4263936 | tf_op jit(solution)/shard_map/reduce_sum | solution.py:100
  112.4 0.1 broadcast_bitcast_fusion
  112.5 1.2 reshape.177
  113.7 4.0 %all-to-all-start.1 = ((f32[4,1,16384]{2,1,0:T(1,128)}), f32[4,1,16384]{2,1,0:T(1,128)S(1)}, u32[]{:S(2)}, u32[]{:S(2)}) async-start(f32[4,1,16384]{2,1,0:T(1,128)} %reshape.177), calls=%async_computation.1 | async-start | bytes 524288 | tf_op jit(solution)/shard_map/all_to_all | solution.py:65
  117.7 0.0 copy-done.3
  117.7 0.1 iota_compare_fusion.2
  117.8 6.0 %all-to-all-done.1 = f32[4,1,16384]{2,1,0:T(1,128)S(1)} async-done(((f32[4,1,16384]{2,1,0:T(1,128)}), f32[4,1,16384]{2,1,0:T(1,128)S(1)}, u32[]{:S(2)}, u32[]{:S(2)}) %all-to-all-start.1) | async-done | bytes 262176 | tf_op jit(solution)/shard_map/all_to_all | solution.py:65
  123.8 0.5 broadcast.56
  124.3 1.4 reduce.4
  125.6 0.4 reshape.178
  126.0 0.1 fusion.36
  126.1 3.3 %broadcast_select_fusion = bf16[4,64,64,64]{1,0,3,2:T(4,128)(2,1)} fusion(pred[64,64]{0,1:T(8,128)(4,1)S(1)} %iota_compare_fusion, bf16[4,64,64]{1,0,2:T(4,128)(2,1)S(1)} %fusion.36), kind=kLoop, calls=%fused_computation.2 | loop fusion | flops 1048576 | bytes 2134016 | tf_op jit(solution)/shard_map/jit(_where)/select_n | solution.py:106
  129.4 6.0 %select_n.30 = bf16[256,4096]{0,1:T(8,128)(2,1)S(1)} reshape(bf16[4,64,64,64]{1,0,3,2:T(4,128)(2,1)} %broadcast_select_fusion) | data formatting | bytes 4194304 | tf_op jit(solution)/shard_map/jit(_where)/select_n | solution.py:106
  135.4 5.0 %all-gather.5.cloned.1.call-done = bf16[4096,1024]{1,0:T(8,128)(2,1)} async-done(((bf16[128,1024]{1,0:T(8,128)(2,1)}), bf16[4096,1024]{1,0:T(8,128)(2,1)}) %all-gather.5.cloned.1.call-update) | async-done | bytes 8388624 | tf_op jit(solution)/shard_map/all_gather | solution.py:93
  140.4 0.0 copy-start
  140.5 5.9 %fusion.21 = bf16[32,8,8,128]{3,1,2,0:T(8,128)(2,1)S(1)} fusion(f32[256,1024]{1,0:T(8,128)S(1)} %fusion.40, bf16[256,4096]{0,1:T(8,128)(2,1)S(1)} %select_n.30, bf16[4096,1024]{1,0:T(8,128)(2,1)} %all-gather.5.cloned.1.call-done), kind=kOutput, calls=%fused_computation.19 | convolution fusion | flops 2148007936 | bytes 12058624 | tf_op jit(solution)/shard_map/dot_general | solution.py:107
  146.3 0.1 copy.33
  146.4 2.5 %fusion.39 = (f32[4,64,8]{2,0,1:T(4,128)S(1)}, f32[4,64,1,8,4]{3,4,0,1,2:T(4,128)S(1)}) fusion(bf16[4,1,64,128]{3,2,1,0:T(8,128)(2,1)S(1)} %get-tuple-element.12, pred[4,4]{1,0:T(4,128)(4,1)S(1)} %iota_compare_fusion.3, bf16[4,64,8,128]{3,2,1,0:T(8,128)(2,1)S(1)} %bitcast.111), kind=kOutput, calls=%fused_computation.48 | convolution fusion | flops 2119680 | bytes 630800 | tf_op jit(solution)/shard_map/trkgd,srkd->trkgs/dot_general | solution.py:36
  148.9 0.0 copy-done
  148.9 1.3 fusion.38
  150.3 0.7 fusion.23
  151.0 0.7 fusion
  151.8 0.5 fusion.30
  152.3 0.6 divide_convert_fusion
  152.9 0.1 convert_element_type.38
  153.1 1.0 copy.26
  (5 shorter events, 0.1 us)
Async XLA Ops:
  6.5 79.4 %all-gather.3.cloned.1.call-start = ((), (), s32[]{:S(2)}) async-start(), calls=%async_computation.2 | async-start | bytes 17301504 | tf_op jit(solution)/shard_map/all_gather | solution.py:85
  7.3 133.2 %all-gather.5.cloned.1.call-start = ((), (), s32[]{:S(2)}) async-start(), calls=%async_computation.3 | async-start | bytes 8650752 | tf_op jit(solution)/shard_map/all_gather | solution.py:93
  61.8 24.1 %copy-start.4 = (s32[64]{0:T(128)S(1)}, s32[64]{0:T(128)}, u32[]{:S(2)}) copy-start(s32[64]{0:T(128)} %param.17) | copy-start | bytes 772
  61.8 24.1 %copy-start.5 = (s32[64]{0:T(128)S(1)}, s32[64]{0:T(128)}, u32[]{:S(2)}) copy-start(s32[64]{0:T(128)} %param.16) | copy-start | bytes 772
  61.8 24.3 %copy-start.2 = (bf16[4,2,64,128]{3,2,1,0:T(8,128)(2,1)S(1)}, bf16[4,2,64,128]{3,2,1,0:T(8,128)(2,1)}, u32[]{:S(2)}) copy-start(bf16[4,2,64,128]{3,2,1,0:T(8,128)(2,1)} %param.14) | copy-start | bytes 393220
  61.8 24.4 %copy-start.1 = (bf16[4,64,2048]{2,1,0:T(8,128)(2,1)S(1)}, bf16[4,64,2048]{2,1,0:T(8,128)(2,1)}, u32[]{:S(2)}) copy-start(bf16[4,64,2048]{2,1,0:T(8,128)(2,1)} %param.9) | copy-start | bytes 3145732
  104.4 13.3 %copy-start.3 = (s32[64]{0:T(128)S(1)}, s32[64]{0:T(128)}, u32[]{:S(2)}) copy-start(s32[64]{0:T(128)} %param.15) | copy-start | bytes 772
  113.7 10.0 %all-to-all-start.1 = ((f32[4,1,16384]{2,1,0:T(1,128)}), f32[4,1,16384]{2,1,0:T(1,128)S(1)}, u32[]{:S(2)}, u32[]{:S(2)}) async-start(f32[4,1,16384]{2,1,0:T(1,128)} %reshape.177), calls=%async_computation.1 | async-start | bytes 524288 | tf_op jit(solution)/shard_map/all_to_all | solution.py:65
  140.4 8.5 %copy-start = (bf16[2,64,128,128]{3,2,1,0:T(8,128)(2,1)S(1)}, bf16[2,64,128,128]{3,2,1,0:T(8,128)(2,1)}, u32[]{:S(2)}) copy-start(bf16[2,64,128,128]{3,2,1,0:T(8,128)(2,1)} %param.13) | copy-start | bytes 12582916
Sparse Core Ops, SparseCore 0:
  9.6 76.2 all-gather.2
  88.2 52.2 all-gather.4

commit v4 on v3

--- a/solution.py
+++ b/solution.py
@@ -93,19 +93,23 @@
     up_all = lax.all_gather(up_local, "dp", axis=0, tiled=True)
 
     position = pool_lookup(adapter_per_request, adapter_pool_position)
-    onehot = position[:, None] == jnp.arange(n_pool, dtype=jnp.int32)[None, :]
-    full = lax.dot_general(
-        token_rows, down_all, (((1,), (1,)), ((), ())), preferred_element_type=jnp.float32
-    ).reshape(steps, requests, n_pool, ADAPTER_RANK)
-    shrink_local = jnp.sum(jnp.where(onehot[None, :, :, None], full, 0.0), axis=2)
+    row_position = jnp.tile(position, steps)
+    pick = jnp.arange(n_pool, dtype=jnp.int32)[:, None] == row_position[None, :]
+    full_t = lax.dot_general(
+        down_all, token_rows, (((1,), (1,)), ((), ())), preferred_element_type=jnp.float32
+    ).reshape(n_pool, ADAPTER_RANK, count_rows)
+    shrink_local = jnp.sum(jnp.where(pick[:, None, :], full_t, 0.0), axis=0)
     partials = gather_tensor(shrink_local, "tensor", n_tensor)
     shrink = partials[0]
     for j in range(1, n_tensor):
         shrink = shrink + partials[j]
     shrink = shrink.astype(jnp.bfloat16)
-    wide = jnp.where(onehot[None, :, :, None], shrink[:, :, None, :], jnp.zeros((), jnp.bfloat16))
-    delta = jnp.dot(
-        wide.reshape(count_rows, n_pool * ADAPTER_RANK), up_all, preferred_element_type=jnp.float32
+    wide_t = jnp.where(pick[:, None, :], shrink[None, :, :], jnp.zeros((), jnp.bfloat16))
+    delta = lax.dot_general(
+        wide_t.reshape(n_pool * ADAPTER_RANK, count_rows),
+        up_all,
+        (((0,), (0,)), ((), ())),
+        preferred_element_type=jnp.float32,
     )
     query = (base + delta).reshape(steps, requests, heads_width).astype(jnp.bfloat16)
     return attend(query, key_value_cache, step_key_value, cache_valid_length)

time: 161 us -> 161 us (level)
  waiting for transfers between devices: 26.9 us -> 54.6 us
  local copies, waits for them, and re-layouts: 19.2 us -> 3.77 us
  other arithmetic: 14.3 us -> 1.72 us
    all_gather x1, waiting for transfers between devices: 5.02 us -> 32.8 us  [per_device(): up_all = lax.all_gather(up_local, 'dp', axis=0, tiled=True)]
    reshape x1 -> x0, local copies, waits for them, and re-layouts: 8.07 us -> none  [per_device(): full = lax.dot_general(token_rows, down_all, (((1,), (1,)), ((), ())), pr...]
    reduce_sum x1 -> x0, other arithmetic: 8.01 us -> none  [per_device(): jnp.sum(jnp.where(onehot[None, :, :, None], full, 0.0), axis=2)]
    select_n x1 -> x0, local copies, waits for them, and re-layouts: 5.99 us -> none  [per_device(): jnp.where(onehot[None, :, :, None], shrink[:, :, None, :], jnp.zeros((),...]
    select_n x1, other arithmetic: 3.35 us -> 0.14 us  [per_device(): jnp.where(pick[:, None, :], shrink[None, :, :], jnp.zeros((), jnp.bfloat16))]
    unnamed x16 -> x13, local copies, waits for them, and re-layouts: 1.76 us -> 0.12 us
  transfers between devices with their start and end apart: 3 -> 3, of which waited for: 3 -> 3; matrix products, arithmetic and copies ran while one was open for 31% -> 14% of each run, Pallas kernels for 0% -> 0%
where the time goes in v4:
time: 161 us
  waiting for transfers between devices  54.6 us (34%)
  blocking collectives  52.7 us (33%)
  matrix products  30.4 us (19%)
  between operations  13.6 us (8%)
  starting transfers between devices  4.04 us (3%)
  local copies, waits for them, and re-layouts  3.77 us (2%)
  other arithmetic  1.72 us (1%)
    all_to_all x1, blocking collectives, gather_tensor(): return lax.all_to_all(tiled, axis_name, 0, 0, tiled=True)  52.7 us
    all_gather x1, waiting for transfers between devices, per_device(): up_all = lax.all_gather(up_local, 'dp', axis=0, tiled=True)  32.8 us
    all_gather x1, waiting for transfers between devices, per_device(): down_all = lax.all_gather(adapter_down_maps, 'dp', axis=0, tiled=True)  15.2 us
    dot_general x1, matrix products, per_device(): lax.dot_general(down_all, token_rows, (((1,), (1,)), ((), ())), preferred...  10.5 us
    dot_general x1, matrix products, per_device(): jnp.dot(full_rows, query_projection_weight, preferred_element_type=jnp.fl...  8.91 us
    all_to_all x1, waiting for transfers between devices, gather_tensor(): return lax.all_to_all(tiled, axis_name, 0, 0, tiled=True)  5.9 us
    dot_general x1, matrix products, per_device(): lax.dot_general(wide_t.reshape(n_pool * ADAPTER_RANK, count_rows), up_all...  5.88 us
    all_to_all x1, starting transfers between devices, gather_tensor(): return lax.all_to_all(tiled, axis_name, 0, 0, tiled=True)  4 us
  transfers between devices with their start and end apart: 3, of which 3 were waited for; matrix products, arithmetic and copies ran while one was open for 14% of the time, Pallas kernels for 0%

profile of v4, /device:TPU:1, one launch (start us, length us, event | category | flops | bytes accessed | tf_op | source)
XLA Modules:
  0.0 160.9 jit_solution(6580476369434188526)
XLA Ops:
  6.5 0.0 all-gather.3.cloned.1.call-start
  6.5 0.7 all-gather.3.cloned.1.call-update
  7.3 0.0 all-gather.5.cloned.1.call-start
  7.3 1.5 copy.21
  8.8 0.3 broadcast_in_dim.99
  9.1 52.7 %all_to_all.10 = bf16[4,256,2048]{1,2,0:T(8,128)(2,1)S(1)} all-to-all(bf16[4,256,2048]{1,2,0:T(8,128)(2,1)S(1)} %broadcast_in_dim.99), channel_id=1, replica_groups=mesh['dp'=32,'tensor'=4] {'tensor'}, dimensions={0} | all-to-all | bytes 8388608 | tf_op jit(solution)/shard_map/all_to_all | solution.py:65
  61.8 0.0 copy-start.4
  61.8 0.0 copy-start.5
  61.8 0.0 copy-start.2
  61.8 0.0 copy-start.1
  61.8 8.9 %fusion.40 = f32[256,1024]{1,0:T(8,128)S(1)} fusion(bf16[256,8192]{0,1:T(8,128)(2,1)S(1)} %bitcast.104, bf16[8192,1024]{1,0:T(8,128)(2,1)} %param.10), kind=kOutput, calls=%fused_computation.48 | convolution fusion | flops 4294967296 | bytes 22020096 | tf_op jit(solution)/shard_map/dot_general | solution.py:90
  70.7 15.2 %all-gather.3.cloned.1.call-done = bf16[4096,2048]{1,0:T(8,128)(2,1)} async-done(((bf16[128,2048]{1,0:T(8,128)(2,1)}), bf16[4096,2048]{1,0:T(8,128)(2,1)}) %all-gather.3.cloned.1.call-update) | async-done | bytes 16777232 | tf_op jit(solution)/shard_map/all_gather | solution.py:85
  85.9 0.0 all-gather.5.cloned.1.call-update
  85.9 0.0 copy-done.4
  85.9 0.0 copy-done.5
  86.0 0.2 select_reduce_fusion.1
  86.1 0.1 eq.36
  86.3 0.0 copy-done.2
  86.3 0.0 copy-done.1
  86.3 0.0 copy-start.3
  86.3 10.5 %select_reduce_fusion = f32[64,256]{1,0:T(8,128)S(1)} fusion(pred[64,256]{1,0:T(8,128)(4,1)S(1)} %iota_compare_fusion, bf16[64,64,2048]{2,1,0:T(8,128)(2,1)} %bitcast.110, bf16[256,2048,1]{1,0,2:T(8,128)(2,1)S(1)} %bitcast.109), kind=kOutput, calls=%fused_computation | convolution fusion | flops 4297048064 | bytes 17907712 | tf_op jit(solution)/shard_map/dot_general | solution.py:98
  96.8 0.7 broadcast_in_dim.104
  97.5 4.0 %all-to-all-start.1 = ((f32[4,64,256]{2,1,0:T(8,128)}), f32[4,64,256]{2,1,0:T(8,128)S(1)}, u32[]{:S(2)}, u32[]{:S(2)}) async-start(f32[4,64,256]{2,1,0:T(8,128)} %broadcast_in_dim.104), calls=%async_computation.1 | async-start | bytes 524288 | tf_op jit(solution)/shard_map/all_to_all | solution.py:65
  101.5 0.0 copy-done.3
  101.5 0.1 iota_compare_fusion.2
  101.6 5.9 %all-to-all-done.1 = f32[4,64,256]{2,1,0:T(8,128)S(1)} async-done(((f32[4,64,256]{2,1,0:T(8,128)}), f32[4,64,256]{2,1,0:T(8,128)S(1)}, u32[]{:S(2)}, u32[]{:S(2)}) %all-to-all-start.1) | async-done | bytes 262176 | tf_op jit(solution)/shard_map/all_to_all | solution.py:65
  107.5 0.1 broadcast_select_fusion
  107.7 32.8 %all-gather.5.cloned.1.call-done = bf16[4096,1024]{1,0:T(8,128)(2,1)} async-done(((bf16[128,1024]{1,0:T(8,128)(2,1)}), bf16[4096,1024]{1,0:T(8,128)(2,1)}) %all-gather.5.cloned.1.call-update) | async-done | bytes 8388624 | tf_op jit(solution)/shard_map/all_gather | solution.py:93
  140.4 0.0 copy-start
  140.5 5.9 %fusion.21 = bf16[32,8,8,128]{3,1,2,0:T(8,128)(2,1)S(1)} fusion(f32[256,1024]{1,0:T(8,128)S(1)} %fusion.40, bf16[4096,256]{1,0:T(8,128)(2,1)S(1)} %bitcast.105, bf16[4096,1024]{1,0:T(8,128)(2,1)} %all-gather.5.cloned.1.call-done), kind=kOutput, calls=%fused_computation.18 | convolution fusion | flops 2148007936 | bytes 12058624 | tf_op jit(solution)/shard_map/dot_general | solution.py:108
  146.3 0.1 copy.33
  146.4 2.5 %fusion.39 = (f32[4,64,8]{2,0,1:T(4,128)S(1)}, f32[4,64,1,8,4]{3,4,0,1,2:T(4,128)S(1)}) fusion(bf16[4,1,64,128]{3,2,1,0:T(8,128)(2,1)S(1)} %get-tuple-element.12, pred[4,4]{1,0:T(4,128)(4,1)S(1)} %iota_compare_fusion.3, bf16[4,64,8,128]{3,2,1,0:T(8,128)(2,1)S(1)} %bitcast.106), kind=kOutput, calls=%fused_computation.47 | convolution fusion | flops 2119680 | bytes 630800 | tf_op jit(solution)/shard_map/trkgd,srkd->trkgs/dot_general | solution.py:36
  148.9 0.0 copy-done
  148.9 1.3 fusion.38
  150.3 0.7 fusion.23
  151.0 0.7 fusion
  151.8 0.5 fusion.30
  152.3 0.6 divide_convert_fusion
  152.9 0.1 convert_element_type.31
  153.1 1.0 copy.26
  (7 shorter events, 0.1 us)
Async XLA Ops:
  6.5 79.4 %all-gather.3.cloned.1.call-start = ((), (), s32[]{:S(2)}) async-start(), calls=%async_computation.2 | async-start | bytes 17301504 | tf_op jit(solution)/shard_map/all_gather | solution.py:85
  7.3 133.2 %all-gather.5.cloned.1.call-start = ((), (), s32[]{:S(2)}) async-start(), calls=%async_computation.3 | async-start | bytes 8650752 | tf_op jit(solution)/shard_map/all_gather | solution.py:93
  61.8 24.1 %copy-start.4 = (s32[64]{0:T(128)S(1)}, s32[64]{0:T(128)}, u32[]{:S(2)}) copy-start(s32[64]{0:T(128)} %param.17) | copy-start | bytes 772
  61.8 24.1 %copy-start.5 = (s32[64]{0:T(128)S(1)}, s32[64]{0:T(128)}, u32[]{:S(2)}) copy-start(s32[64]{0:T(128)} %param.16) | copy-start | bytes 772
  61.8 24.4 %copy-start.2 = (bf16[4,2,64,128]{3,2,1,0:T(8,128)(2,1)S(1)}, bf16[4,2,64,128]{3,2,1,0:T(8,128)(2,1)}, u32[]{:S(2)}) copy-start(bf16[4,2,64,128]{3,2,1,0:T(8,128)(2,1)} %param.14) | copy-start | bytes 393220
  61.8 24.5 %copy-start.1 = (bf16[4,64,2048]{2,1,0:T(8,128)(2,1)S(1)}, bf16[4,64,2048]{2,1,0:T(8,128)(2,1)}, u32[]{:S(2)}) copy-start(bf16[4,64,2048]{2,1,0:T(8,128)(2,1)} %param.9) | copy-start | bytes 3145732
  86.3 15.2 %copy-start.3 = (s32[64]{0:T(128)S(1)}, s32[64]{0:T(128)}, u32[]{:S(2)}) copy-start(s32[64]{0:T(128)} %param.15) | copy-start | bytes 772
  97.5 10.0 %all-to-all-start.1 = ((f32[4,64,256]{2,1,0:T(8,128)}), f32[4,64,256]{2,1,0:T(8,128)S(1)}, u32[]{:S(2)}, u32[]{:S(2)}) async-start(f32[4,64,256]{2,1,0:T(8,128)} %broadcast_in_dim.104), calls=%async_computation.1 | async-start | bytes 524288 | tf_op jit(solution)/shard_map/all_to_all | solution.py:65
  140.4 8.5 %copy-start = (bf16[2,64,128,128]{3,2,1,0:T(8,128)(2,1)S(1)}, bf16[2,64,128,128]{3,2,1,0:T(8,128)(2,1)}, u32[]{:S(2)}) copy-start(bf16[2,64,128,128]{3,2,1,0:T(8,128)(2,1)} %param.13) | copy-start | bytes 12582916
Sparse Core Ops, SparseCore 0:
  9.6 76.2 all-gather.2
  88.2 52.2 all-gather.4

commit v5 on v4

--- a/solution.py
+++ b/solution.py
@@ -3,6 +3,7 @@
 import jax
 import jax.numpy as jnp
 from jax import lax
+from jax.experimental import pallas as pl
 from jax.sharding import PartitionSpec as P
 
 HEAD_SIZE = 128
@@ -15,49 +16,78 @@
     return jnp.sum(jnp.where(match, adapter_pool_position[None, :], 0), axis=1)
 
 
+REQ_BLOCK = 16
+
+
+def attend_kernel(q_ref, k_ref, v_ref, nk_ref, nv_ref, valid_ref, o_ref):
+    scale = 1.0 / math.sqrt(HEAD_SIZE)
+    q = q_ref[...]
+    keys = k_ref[0]
+    values = v_ref[0]
+    new_keys = nk_ref[...]
+    new_values = nv_ref[...]
+    cache_scores = lax.dot_general(
+        q, keys, (((2,), (2,)), ((0,), (0,))), preferred_element_type=jnp.float32
+    ) * scale
+    cache_scores = jnp.where(valid_ref[...] > 0, cache_scores, -1e30)
+    fresh_scores = lax.dot_general(
+        q, new_keys, (((2,), (2,)), ((0,), (0,))), preferred_element_type=jnp.float32
+    ) * scale
+    rows = q.shape[1]
+    group = rows // new_keys.shape[1]
+    row_id = lax.broadcasted_iota(jnp.int32, fresh_scores.shape, 1)
+    step_id = lax.broadcasted_iota(jnp.int32, fresh_scores.shape, 2)
+    fresh_scores = jnp.where(row_id >= step_id * group, fresh_scores, -1e30)
+    top = jnp.maximum(
+        jnp.max(cache_scores, axis=-1, keepdims=True), jnp.max(fresh_scores, axis=-1, keepdims=True)
+    )
+    cache_expo = jnp.exp(cache_scores - top)
+    fresh_expo = jnp.exp(fresh_scores - top)
+    total = jnp.sum(cache_expo, axis=-1, keepdims=True) + jnp.sum(fresh_expo, axis=-1, keepdims=True)
+    mixed = lax.dot_general(
+        cache_expo.astype(jnp.bfloat16), values, (((2,), (1,)), ((0,), (0,))),
+        preferred_element_type=jnp.float32,
+    )
+    mixed = mixed + lax.dot_general(
+        fresh_expo.astype(jnp.bfloat16), new_values, (((2,), (1,)), ((0,), (0,))),
+        preferred_element_type=jnp.float32,
+    )
+    o_ref[...] = (mixed / total).astype(o_ref.dtype)
+
+
 def attend(query, key_value_cache, step_key_value, cache_valid_length):
-    steps = step_key_value.shape[0]
-    requests = step_key_value.shape[2]
+    steps, requests, width = query.shape
     length = key_value_cache.shape[2]
     kv_local = key_value_cache.shape[3] // HEAD_SIZE
-    group = query.shape[2] // HEAD_SIZE // kv_local
-    scale = 1.0 / math.sqrt(HEAD_SIZE)
-    grouped = query.reshape(steps, requests, kv_local, group, HEAD_SIZE)
-    keys = key_value_cache[0].reshape(requests, length, kv_local, HEAD_SIZE)
-    values = key_value_cache[1].reshape(requests, length, kv_local, HEAD_SIZE)
-    new_keys = step_key_value[:, 0].reshape(steps, requests, kv_local, HEAD_SIZE)
-    new_values = step_key_value[:, 1].reshape(steps, requests, kv_local, HEAD_SIZE)
-    cache_scores = (
-        jnp.einsum("trkgd,rckd->trkgc", grouped, keys, preferred_element_type=jnp.float32) * scale
-    )
+    heads = width // HEAD_SIZE
+    group = heads // kv_local
+    rows = steps * group
+    q = query.reshape(steps, requests, kv_local, group, HEAD_SIZE)
+    q = jnp.transpose(q, (1, 2, 0, 3, 4)).reshape(requests * kv_local, rows, HEAD_SIZE)
+    cache = key_value_cache.reshape(2, requests, length, kv_local, HEAD_SIZE)
+    cache = jnp.transpose(cache, (0, 1, 3, 2, 4)).reshape(2, requests * kv_local, length, HEAD_SIZE)
+    fresh = step_key_value.reshape(steps, 2, requests, kv_local, HEAD_SIZE)
+    fresh = jnp.transpose(fresh, (1, 2, 3, 0, 4)).reshape(2, requests * kv_local, steps, HEAD_SIZE)
     valid = jnp.arange(length, dtype=jnp.int32)[None, :] < cache_valid_length[:, None]
-    cache_scores = jnp.where(valid[None, :, None, None, :], cache_scores, -1e30)
-    fresh_scores = (
-        jnp.einsum("trkgd,srkd->trkgs", grouped, new_keys, preferred_element_type=jnp.float32)
-        * scale
-    )
-    causal = (
-        jnp.arange(steps, dtype=jnp.int32)[:, None] >= jnp.arange(steps, dtype=jnp.int32)[None, :]
-    )
-    fresh_scores = jnp.where(causal[:, None, None, None, :], fresh_scores, -1e30)
-    top = jnp.maximum(jnp.max(cache_scores, axis=-1), jnp.max(fresh_scores, axis=-1))
-    cache_expo = jnp.exp(cache_scores - top[..., None])
-    fresh_expo = jnp.exp(fresh_scores - top[..., None])
-    total = jnp.sum(cache_expo, axis=-1) + jnp.sum(fresh_expo, axis=-1)
-    mixed = jnp.einsum(
-        "trkgc,rckd->trkgd",
-        cache_expo.astype(jnp.bfloat16),
-        values,
-        preferred_element_type=jnp.float32,
-    )
-    mixed = mixed + jnp.einsum(
-        "trkgs,srkd->trkgd",
-        fresh_expo.astype(jnp.bfloat16),
-        new_values,
-        preferred_element_type=jnp.float32,
-    )
-    attended = mixed / total[..., None]
-    return attended.reshape(steps, requests, -1).astype(jnp.bfloat16)
+    valid = jnp.repeat(valid.astype(jnp.int32), kv_local, axis=0)[:, None, :]
+    batch = requests * kv_local
+    blk = min(REQ_BLOCK, batch)
+    out = pl.pallas_call(
+        attend_kernel,
+        grid=(batch // blk,),
+        in_specs=[
+            pl.BlockSpec((blk, rows, HEAD_SIZE), lambda i: (i, 0, 0)),
+            pl.BlockSpec((1, blk, length, HEAD_SIZE), lambda i: (0, i, 0, 0)),
+            pl.BlockSpec((1, blk, length, HEAD_SIZE), lambda i: (1, i, 0, 0)),
+            pl.BlockSpec((blk, steps, HEAD_SIZE), lambda i: (i, 0, 0)),
+            pl.BlockSpec((blk, steps, HEAD_SIZE), lambda i: (i, 0, 0)),
+            pl.BlockSpec((blk, 1, length), lambda i: (i, 0, 0)),
+        ],
+        out_specs=pl.BlockSpec((blk, rows, HEAD_SIZE), lambda i: (i, 0, 0)),
+        out_shape=jax.ShapeDtypeStruct((batch, rows, HEAD_SIZE), query.dtype),
+    )(q, cache, cache, fresh[0], fresh[1], valid)
+    out = out.reshape(requests, kv_local, steps, group, HEAD_SIZE)
+    return jnp.transpose(out, (2, 0, 1, 3, 4)).reshape(steps, requests, width)
 
 
 def gather_tensor(value, axis_name, count):

time: 161 us -> 162 us (level)
  Pallas kernels: 0 us -> 5.83 us
  matrix products: 30.4 us -> 25.1 us
  local copies, waits for them, and re-layouts: 3.77 us -> 6.5 us
    pallas_call x0 -> x1, Pallas kernels: none -> 5.83 us  [attend(): pl.pallas_call(attend_kernel, grid=(batch // blk,), in_specs=[pl.BlockSpe...]
    dot_general x4 -> x0, matrix products: 5.14 us -> none  [the longest x1 2.46 us: attend(): jnp.einsum('trkgd,srkd->trkgs', grouped, new_keys, preferred_element_type...]
    reshape x0 -> x2, local copies, waits for them, and re-layouts: none -> 2.12 us  [attend(): return jnp.transpose(out, (2, 0, 1, 3, 4)).reshape(steps, requests, width)]
  transfers between devices with their start and end apart: 3 -> 3, of which waited for: 3 -> 3; matrix products, arithmetic and copies ran while one was open for 14% -> 15% of each run, Pallas kernels for 0% -> 0%
where the time goes in v5:
time: 162 us
  waiting for transfers between devices  53.1 us (33%)
  blocking collectives  52.7 us (33%)
  matrix products  25.1 us (15%)
  between operations  13.5 us (8%)
  local copies, waits for them, and re-layouts  6.5 us (4%)
  Pallas kernels  5.83 us (4%)
  starting transfers between devices  4.04 us (2%)
    all_to_all x1, blocking collectives, gather_tensor(): return lax.all_to_all(tiled, axis_name, 0, 0, tiled=True)  52.7 us
    all_gather x1, waiting for transfers between devices, per_device(): up_all = lax.all_gather(up_local, 'dp', axis=0, tiled=True)  32 us
    all_gather x1, waiting for transfers between devices, per_device(): down_all = lax.all_gather(adapter_down_maps, 'dp', axis=0, tiled=True)  15.2 us
    dot_general x1, matrix products, per_device(): lax.dot_general(down_all, token_rows, (((1,), (1,)), ((), ())), preferred...  10.5 us
    dot_general x1, matrix products, per_device(): jnp.dot(full_rows, query_projection_weight, preferred_element_type=jnp.fl...  8.91 us
    pallas_call x1, Pallas kernels, attend(): pl.pallas_call(attend_kernel, grid=(batch // blk,), in_specs=[pl.BlockSpe...  5.83 us
    dot_general x1, matrix products, per_device(): lax.dot_general(wide_t.reshape(n_pool * ADAPTER_RANK, count_rows), up_all...  5.74 us
    all_to_all x1, waiting for transfers between devices, gather_tensor(): return lax.all_to_all(tiled, axis_name, 0, 0, tiled=True)  5.19 us
  transfers between devices with their start and end apart: 3, of which 3 were waited for; matrix products, arithmetic and copies ran while one was open for 15% of the time, Pallas kernels for 0%

profile of v5, /device:TPU:1, one launch (start us, length us, event | category | flops | bytes accessed | tf_op | source)
XLA Modules:
  0.0 162.0 jit_solution(15332823021406834648)
XLA Ops:
  6.5 0.0 all-gather.3.cloned.1.call-start
  6.5 0.7 all-gather.3.cloned.1.call-update
  7.3 0.0 all-gather.5.cloned.1.call-start
  7.3 1.5 copy.17
  8.8 0.3 broadcast_in_dim.68
  9.1 52.7 %all_to_all.10 = bf16[4,256,2048]{1,2,0:T(8,128)(2,1)S(1)} all-to-all(bf16[4,256,2048]{1,2,0:T(8,128)(2,1)S(1)} %broadcast_in_dim.68), channel_id=1, replica_groups=mesh['dp'=32,'tensor'=4] {'tensor'}, dimensions={0} | all-to-all | bytes 8388608 | tf_op jit(solution)/shard_map/all_to_all | solution.py:95
  61.8 0.0 copy-start.3
  61.8 0.0 copy-start.4
  61.8 0.0 copy-start.1
  61.8 0.0 copy-start
  61.8 8.9 %fusion.4 = f32[256,1024]{1,0:T(8,128)S(1)} fusion(bf16[256,8192]{0,1:T(8,128)(2,1)S(1)} %bitcast.42, bf16[8192,1024]{1,0:T(8,128)(2,1)} %param.10), kind=kOutput, calls=%fused_computation.18 | convolution fusion | flops 4294967296 | bytes 22020096 | tf_op jit(solution)/shard_map/dot_general | solution.py:120
  70.7 15.2 %all-gather.3.cloned.1.call-done = bf16[4096,2048]{1,0:T(8,128)(2,1)} async-done(((bf16[128,2048]{1,0:T(8,128)(2,1)}), bf16[4096,2048]{1,0:T(8,128)(2,1)}) %all-gather.3.cloned.1.call-update) | async-done | bytes 16777232 | tf_op jit(solution)/shard_map/all_gather | solution.py:115
  85.9 0.0 all-gather.5.cloned.1.call-update
  85.9 0.0 copy-done.3
  85.9 0.0 copy-done.4
  86.0 0.2 select_reduce_fusion.1
  86.1 0.1 eq.36
  86.2 0.0 copy-done.1
  86.2 0.1 copy.26
  86.4 0.7 slice_bitcast_fusion
  87.1 0.0 copy-done
  87.1 0.0 copy-start.2
  87.1 10.5 %select_reduce_fusion = f32[64,256]{1,0:T(8,128)S(1)} fusion(pred[64,256]{1,0:T(8,128)(4,1)S(1)} %iota_compare_fusion, bf16[64,64,2048]{2,1,0:T(8,128)(2,1)} %bitcast.50, bf16[256,2048,1]{1,0,2:T(8,128)(2,1)S(1)} %bitcast.48), kind=kOutput, calls=%fused_computation | convolution fusion | flops 4297048064 | bytes 17907712 | tf_op jit(solution)/shard_map/dot_general | solution.py:128
  97.6 0.7 broadcast_in_dim.73
  98.3 4.0 %all-to-all-start.1 = ((f32[4,64,256]{2,1,0:T(8,128)}), f32[4,64,256]{2,1,0:T(8,128)S(1)}, u32[]{:S(2)}, u32[]{:S(2)}) async-start(f32[4,64,256]{2,1,0:T(8,128)} %broadcast_in_dim.73), calls=%async_computation.1 | async-start | bytes 524288 | tf_op jit(solution)/shard_map/all_to_all | solution.py:95
  102.3 0.0 copy-done.2
  102.3 0.7 compare_convert_fusion.valid_ref
  103.1 5.2 %all-to-all-done.1 = f32[4,64,256]{2,1,0:T(8,128)S(1)} async-done(((f32[4,64,256]{2,1,0:T(8,128)}), f32[4,64,256]{2,1,0:T(8,128)S(1)}, u32[]{:S(2)}, u32[]{:S(2)}) %all-to-all-start.1) | async-done | bytes 262176 | tf_op jit(solution)/shard_map/all_to_all | solution.py:95
  108.3 0.1 broadcast_select_fusion
  108.4 32.0 %all-gather.5.cloned.1.call-done = bf16[4096,1024]{1,0:T(8,128)(2,1)} async-done(((bf16[128,1024]{1,0:T(8,128)(2,1)}), bf16[4096,1024]{1,0:T(8,128)(2,1)}) %all-gather.5.cloned.1.call-update) | async-done | bytes 8388624 | tf_op jit(solution)/shard_map/all_gather | solution.py:123
  140.4 5.7 %fusion.1 = bf16[32,8,8,128]{3,1,2,0:T(8,128)(2,1)S(1)} fusion(f32[256,1024]{1,0:T(8,128)S(1)} %fusion.4, bf16[4096,256]{1,0:T(8,128)(2,1)S(1)} %bitcast.43, bf16[4096,1024]{1,0:T(8,128)(2,1)} %all-gather.5.cloned.1.call-done), kind=kOutput, calls=%fused_computation.4 | convolution fusion | flops 2148007936 | bytes 12058624 | tf_op jit(solution)/shard_map/dot_general | solution.py:138
  146.2 0.1 copy.22
  146.3 0.9 copy.25
  147.2 5.8 %shard_map.91 = bf16[64,32,128]{2,1,0:T(8,128)(2,1)} custom-call(bf16[64,32,128]{2,1,0:T(8,128)(2,1)} %bitcast.44, bf16[2,64,128,128]{3,2,1,0:T(8,128)(2,1)} %v_ref.1, bf16[2,64,128,128]{3,2,1,0:T(8,128)(2,1)} %v_ref.1, bf16[64,4,128]{2,1,0:T(4,128)(2,1)} %get-tuple-element.12.nk_ref, bf16[64,4,128]{2,1,0:T(4,128)(2,1)} %get-tuple-element.11.nv_ref, ...), custom_call_target="tpu_custom_call" | custom-call | tf_op jit(solution)/shard_map/pallas_call | solution.py:75
  153.0 1.2 reshape.102
  154.2 1.0 copy.21
  (3 shorter events, 0.0 us)
Async XLA Ops:
  6.5 79.4 %all-gather.3.cloned.1.call-start = ((), (), s32[]{:S(2)}) async-start(), calls=%async_computation.2 | async-start | bytes 17301504 | tf_op jit(solution)/shard_map/all_gather | solution.py:115
  7.3 133.2 %all-gather.5.cloned.1.call-start = ((), (), s32[]{:S(2)}) async-start(), calls=%async_computation.3 | async-start | bytes 8650752 | tf_op jit(solution)/shard_map/all_gather | solution.py:123
  61.8 24.1 %copy-start.3 = (s32[64]{0:T(128)S(1)}, s32[64]{0:T(128)}, u32[]{:S(2)}) copy-start(s32[64]{0:T(128)} %param.17) | copy-start | bytes 772
  61.8 24.1 %copy-start.4 = (s32[64]{0:T(128)S(1)}, s32[64]{0:T(128)}, u32[]{:S(2)}) copy-start(s32[64]{0:T(128)} %param.16) | copy-start | bytes 772
  61.8 24.4 %copy-start.1 = (bf16[4,2,64,128]{3,2,1,0:T(8,128)(2,1)S(1)}, bf16[4,2,64,128]{3,2,1,0:T(8,128)(2,1)}, u32[]{:S(2)}) copy-start(bf16[4,2,64,128]{3,2,1,0:T(8,128)(2,1)} %param.14) | copy-start | bytes 393220
  61.8 25.3 %copy-start = (bf16[4,64,2048]{2,1,0:T(8,128)(2,1)S(1)}, bf16[4,64,2048]{2,1,0:T(8,128)(2,1)}, u32[]{:S(2)}) copy-start(bf16[4,64,2048]{2,1,0:T(8,128)(2,1)} %param.9) | copy-start | bytes 3145732
  87.1 15.2 %copy-start.2 = (s32[64]{0:T(128)S(1)}, s32[64]{0:T(128)}, u32[]{:S(2)}) copy-start(s32[64]{0:T(128)} %param.15) | copy-start | bytes 772
  98.3 9.9 %all-to-all-start.1 = ((f32[4,64,256]{2,1,0:T(8,128)}), f32[4,64,256]{2,1,0:T(8,128)S(1)}, u32[]{:S(2)}, u32[]{:S(2)}) async-start(f32[4,64,256]{2,1,0:T(8,128)} %broadcast_in_dim.73), calls=%async_computation.1 | async-start | bytes 524288 | tf_op jit(solution)/shard_map/all_to_all | solution.py:95
Sparse Core Ops, SparseCore 0:
  9.6 76.2 all-gather.2
  88.2 52.2 all-gather.4

commit v6 on v5

v6 whole, which is shorter than its diff:
```python
import math

import jax
import jax.numpy as jnp
from jax import lax
from jax.experimental import pallas as pl
from jax.sharding import PartitionSpec as P

HEAD_SIZE = 128
ADAPTER_RANK = 64


def pool_lookup(adapters, adapter_pool_position):
    table = jnp.arange(adapter_pool_position.shape[0], dtype=jnp.int32)
    match = adapters[:, None] == table[None, :]
    return jnp.sum(jnp.where(match, adapter_pool_position[None, :], 0), axis=1)


def attend_kernel(q_ref, kt_ref, v_ref, lens_ref, o_ref):
    scale = 1.0 / math.sqrt(HEAD_SIZE)
    q = q_ref[...]
    scores = lax.dot_general(
        q, kt_ref[...], (((2,), (1,)), ((0,), (0,))), preferred_element_type=jnp.float32
    ) * scale
    length = v_ref.shape[1] // 2
    rows = q.shape[1]
    col = lax.broadcasted_iota(jnp.int32, scores.shape, 2)
    row = lax.broadcasted_iota(jnp.int32, scores.shape, 1)
    fresh = col - length
    group = rows // 4
    limit = jnp.broadcast_to(lens_ref[...], scores.shape)
    valid = ((col < length) & (col < limit)) | ((col >= length) & (fresh < 4) & (row >= fresh * group))
    scores = jnp.where(valid, scores, -1e30)
    top = jnp.max(scores, axis=-1, keepdims=True)
    expo = jnp.exp(scores - top)
    total = jnp.sum(expo, axis=-1, keepdims=True)
    mixed = lax.dot_general(
        expo.astype(jnp.bfloat16), v_ref[...], (((2,), (1,)), ((0,), (0,))),
        preferred_element_type=jnp.float32,
    )
    o_ref[...] = (mixed / total).astype(o_ref.dtype)


def prepare_keys(key_value_cache, step_key_value, cache_valid_length):
    _, requests, length, width = key_value_cache.shape
    steps = step_key_value.shape[0]
    kv_local = width // HEAD_SIZE
    batch = requests * kv_local
    cache = key_value_cache.reshape(2, requests, length, kv_local, HEAD_SIZE)
    cache = jnp.transpose(cache, (0, 1, 3, 2, 4)).reshape(2, batch, length, HEAD_SIZE)
    fresh = step_key_value.reshape(steps, 2, requests, kv_local, HEAD_SIZE)
    fresh = jnp.transpose(fresh, (1, 2, 3, 0, 4)).reshape(2, batch, steps, HEAD_SIZE)
    pad = jnp.zeros((2, batch, length - steps, HEAD_SIZE), fresh.dtype)
    ext = jnp.concatenate([cache, fresh, pad], axis=2)
    keys_t = jnp.transpose(ext[0], (0, 2, 1))
    lens = jnp.repeat(cache_valid_length, kv_local)
    lens = jnp.broadcast_to(lens[:, None, None], (batch, 1, 2 * length)).astype(jnp.int32)
    return keys_t, ext[1], lens


def attend(query, keys_t, values, lens, blk=32):
    steps, requests, width = query.shape
    batch, _, keys = keys_t.shape
    kv_local = batch // requests
    group = width // HEAD_SIZE // kv_local
    rows = steps * group
    q = query.reshape(steps, requests, kv_local, group, HEAD_SIZE)
    q = jnp.transpose(q, (1, 2, 0, 3, 4)).reshape(batch, rows, HEAD_SIZE)
    blk = min(blk, batch)
    out = pl.pallas_call(
        attend_kernel,
        grid=(batch // blk,),
        in_specs=[
            pl.BlockSpec((blk, rows, HEAD_SIZE), lambda i: (i, 0, 0)),
            pl.BlockSpec((blk, HEAD_SIZE, keys), lambda i: (i, 0, 0)),
            pl.BlockSpec((blk, keys, HEAD_SIZE), lambda i: (i, 0, 0)),
            pl.BlockSpec((blk, 1, keys), lambda i: (i, 0, 0)),
        ],
        out_specs=pl.BlockSpec((blk, rows, HEAD_SIZE), lambda i: (i, 0, 0)),
        out_shape=jax.ShapeDtypeStruct((batch, rows, HEAD_SIZE), query.dtype),
    )(q, keys_t, values, lens)
    out = out.reshape(requests, kv_local, steps, group, HEAD_SIZE)
    return jnp.transpose(out, (2, 0, 1, 3, 4)).reshape(steps, requests, width)


def gather_tensor(value, axis_name, count):
    tiled = jnp.broadcast_to(value[None], (count,) + value.shape)
    return lax.all_to_all(tiled, axis_name, 0, 0, tiled=True)


def per_device(
    normed_hidden_state,
    query_projection_weight,
    adapter_down_maps,
    adapter_up_maps,
    key_value_cache,
    step_key_value,
    cache_valid_length,
    adapter_per_request,
    adapter_pool_position,
):
    steps, requests, part_width = normed_hidden_state.shape
    count_rows = steps * requests
    heads_width = query_projection_weight.shape[1]
    n_tensor = query_projection_weight.shape[0] // part_width
    token_rows = normed_hidden_state.reshape(count_rows, part_width)

    down_all = lax.all_gather(adapter_down_maps, "dp", axis=0, tiled=True)
    n_pool = down_all.shape[0] // ADAPTER_RANK

    pieces = gather_tensor(token_rows, "tensor", n_tensor)
    full_rows = jnp.transpose(pieces, (1, 0, 2)).reshape(count_rows, n_tensor * part_width)
    base = jnp.dot(full_rows, query_projection_weight, preferred_element_type=jnp.float32)

    up_local, down_all, base = lax.optimization_barrier((adapter_up_maps, down_all, base))
    up_all = lax.all_gather(up_local, "dp", axis=0, tiled=True)

    position = pool_lookup(adapter_per_request, adapter_pool_position)
    row_position = jnp.tile(position, steps)
    pick = jnp.arange(n_pool, dtype=jnp.int32)[:, None] == row_position[None, :]
    full_t = lax.dot_general(
        down_all, token_rows, (((1,), (1,)), ((), ())), preferred_element_type=jnp.float32
    ).reshape(n_pool, ADAPTER_RANK, count_rows)
    shrink_local = jnp.sum(jnp.where(pick[:, None, :], full_t, 0.0), axis=0)
    partials = gather_tensor(shrink_local, "tensor", n_tensor)
    shrink = partials[0]
    for j in range(1, n_tensor):
        shrink = shrink + partials[j]
    shrink = shrink.astype(jnp.bfloat16)
    wide_t = jnp.where(pick[:, None, :], shrink[None, :, :], jnp.zeros((), jnp.bfloat16))
    delta = lax.dot_general(
        wide_t.reshape(n_pool * ADAPTER_RANK, count_rows),
        up_all,
        (((0,), (0,)), ((), ())),
        preferred_element_type=jnp.float32,
    )
    query = (base + delta).reshape(steps, requests, heads_width).astype(jnp.bfloat16)
    keys_t, values, lens = prepare_keys(key_value_cache, step_key_value, cache_valid_length)
    return attend(query, keys_t, values, lens)


def solution(mesh):
    return jax.shard_map(
        per_device,
        mesh=mesh,
        in_specs=(
            P(None, "dp", "tensor"),
            P(None, "tensor"),
            P("dp", "tensor"),
            P("dp", "tensor"),
            P(None, "dp", None, "tensor"),
            P(None, None, "dp", "tensor"),
            P("dp"),
            P("dp"),
            P(),
        ),
        out_specs=P(None, "dp", "tensor"),
        check_vma=False,
    )
```

time: 162 us -> 163 us (level)
  waiting for transfers between devices: 53.1 us -> 33.5 us
  local copies, waits for them, and re-layouts: 6.5 us -> 19.1 us
  other arithmetic: 1.08 us -> 8.64 us
    all_gather x1, waiting for transfers between devices: 32 us -> 17.6 us  [per_device(): up_all = lax.all_gather(up_local, 'dp', axis=0, tiled=True)]
    concatenate x0 -> x1, other arithmetic: none -> 8.3 us  [prepare_keys(): ext = jnp.concatenate([cache, fresh, pad], axis=2)]
    transpose x0 -> x1, local copies, waits for them, and re-layouts: none -> 6.49 us  [prepare_keys(): keys_t = jnp.transpose(ext[0], (0, 2, 1))]
    squeeze x1, local copies, waits for them, and re-layouts: 0.72 us -> 5.95 us  [prepare_keys(): return (keys_t, ext[1], lens)]
    all_to_all x1, waiting for transfers between devices: 5.19 us -> 0.01 us  [gather_tensor(): return lax.all_to_all(tiled, axis_name, 0, 0, tiled=True)]
  transfers between devices with their start and end apart: 3 -> 3, of which waited for: 3 -> 2; matrix products, arithmetic and copies ran while one was open for 15% -> 27% of each run, Pallas kernels for 0% -> 0%
where the time goes in v6:
time: 163 us; the launch traced here: 162 us
  blocking collectives  52.7 us (32%)
  waiting for transfers between devices  33.5 us (21%)
  matrix products  25.4 us (16%)
  local copies, waits for them, and re-layouts  19.1 us (12%)
  between operations  13.5 us (8%)
  other arithmetic  8.64 us (5%)
  Pallas kernels  5.12 us (3%)
  starting transfers between devices  4.05 us (2%)
    all_to_all x1, blocking collectives, gather_tensor(): return lax.all_to_all(tiled, axis_name, 0, 0, tiled=True)  52.7 us
    all_gather x1, waiting for transfers between devices, per_device(): up_all = lax.all_gather(up_local, 'dp', axis=0, tiled=True)  17.6 us
    all_gather x1, waiting for transfers between devices, per_device(): down_all = lax.all_gather(adapter_down_maps, 'dp', axis=0, tiled=True)  15.2 us
    dot_general x1, matrix products, per_device(): lax.dot_general(down_all, token_rows, (((1,), (1,)), ((), ())), preferred...  10.8 us
    dot_general x1, matrix products, per_device(): jnp.dot(full_rows, query_projection_weight, preferred_element_type=jnp.fl...  8.85 us
    concatenate x1, other arithmetic, prepare_keys(): ext = jnp.concatenate([cache, fresh, pad], axis=2)  8.3 us
    transpose x1, local copies, waits for them, and re-layouts, prepare_keys(): keys_t = jnp.transpose(ext[0], (0, 2, 1))  6.49 us
    squeeze x1, local copies, waits for them, and re-layouts, prepare_keys(): return (keys_t, ext[1], lens)  5.95 us
  transfers between devices with their start and end apart: 3, of which 2 were waited for; matrix products, arithmetic and copies ran while one was open for 27% of the time, Pallas kernels for 0%

profile of v6, /device:TPU:1, one launch (start us, length us, event | category | flops | bytes accessed | tf_op | source)
XLA Modules:
  0.0 162.0 jit_solution(11322299638604984691)
XLA Ops:
  6.5 0.0 all-gather.3.cloned.1.call-start
  6.5 0.7 all-gather.3.cloned.1.call-update
  7.3 0.0 all-gather.5.cloned.1.call-start
  7.3 1.5 copy.19
  8.8 0.3 broadcast_in_dim.73
  9.1 52.7 %all_to_all.10 = bf16[4,256,2048]{1,2,0:T(8,128)(2,1)S(1)} all-to-all(bf16[4,256,2048]{1,2,0:T(8,128)(2,1)S(1)} %broadcast_in_dim.73), channel_id=1, replica_groups=mesh['dp'=32,'tensor'=4] {'tensor'}, dimensions={0} | all-to-all | bytes 8388608 | tf_op jit(solution)/shard_map/all_to_all | solution.py:88
  61.8 0.0 copy-start.3
  61.8 0.0 copy-start.4
  61.8 0.0 copy-start.1
  61.8 8.9 %fusion.4 = f32[256,1024]{1,0:T(8,128)S(1)} fusion(bf16[256,8192]{0,1:T(8,128)(2,1)S(1)} %bitcast.46, bf16[8192,1024]{1,0:T(8,128)(2,1)} %param.10), kind=kOutput, calls=%fused_computation.18 | convolution fusion | flops 4294967296 | bytes 22020096 | tf_op jit(solution)/shard_map/dot_general | solution.py:113
  70.7 0.0 copy-start
  70.7 15.2 %all-gather.3.cloned.1.call-done = bf16[4096,2048]{1,0:T(8,128)(2,1)} async-done(((bf16[128,2048]{1,0:T(8,128)(2,1)}), bf16[4096,2048]{1,0:T(8,128)(2,1)}) %all-gather.3.cloned.1.call-update) | async-done | bytes 16777232 | tf_op jit(solution)/shard_map/all_gather | solution.py:108
  85.9 0.0 all-gather.5.cloned.1.call-update
  85.9 0.0 copy-done.3
  85.9 0.0 copy-done.4
  86.0 0.2 select_reduce_fusion.1
  86.1 0.1 eq.36
  86.2 0.0 copy-done.1
  86.2 0.1 copy.29
  86.4 0.1 pad.2.clone
  86.4 8.3 %maximum_maximum_fusion = bf16[2,64,256,128]{3,2,1,0:T(8,128)(2,1)} fusion(bf16[2,64,4,128]{3,2,1,0:T(4,128)(2,1)S(1)} %bitcast.53, bf16[2,64,128,128]{3,2,1,0:T(8,128)(2,1)} %param.13, bf16[256]{0:T(256)(128)(2,1)S(1)} %pad.2.clone), kind=kLoop, calls=%fused_computation | loop fusion | flops 25165824 | bytes 12714496 | tf_op jit(solution)/shard_map/concatenate | solution.py:54
  94.7 0.0 copy-done
  94.7 10.8 %select_reduce_fusion = f32[64,256]{1,0:T(8,128)S(1)} fusion(pred[64,256]{1,0:T(8,128)(4,1)S(1)} %iota_compare_fusion, bf16[64,64,2048]{2,1,0:T(8,128)(2,1)} %bitcast.54, bf16[256,2048,1]{1,0,2:T(8,128)(2,1)S(1)} %bitcast.52), kind=kOutput, calls=%fused_computation.3 | convolution fusion | flops 4297048064 | bytes 17907712 | tf_op jit(solution)/shard_map/dot_general | solution.py:121
  105.5 0.7 broadcast_in_dim.78
  106.2 4.0 %all-to-all-start.1 = ((f32[4,64,256]{2,1,0:T(8,128)}), f32[4,64,256]{2,1,0:T(8,128)S(1)}, u32[]{:S(2)}, u32[]{:S(2)}) async-start(f32[4,64,256]{2,1,0:T(8,128)} %broadcast_in_dim.78), calls=%async_computation.1 | async-start | bytes 524288 | tf_op jit(solution)/shard_map/all_to_all | solution.py:88
  110.3 6.0 %slice_bitcast_fusion = (bf16[64,256,128]{2,1,0:T(8,128)(2,1)}, bf16[64,128,256]{1,2,0:T(8,128)(2,1)}) fusion(bf16[2,64,256,128]{3,2,1,0:T(8,128)(2,1)} %maximum_maximum_fusion), kind=kLoop, calls=%fused_computation.1 | loop fusion | bytes 16777216 | tf_op jit(solution)/shard_map/squeeze | solution.py:58
  116.2 6.5 %copy.22.kt_ref = bf16[64,128,256]{2,1,0:T(8,128)(2,1)} copy(bf16[64,128,256]{1,2,0:T(8,128)(2,1)} %get-tuple-element.12) | data formatting | bytes 8388608 | tf_op jit(solution)/shard_map/transpose | solution.py:55
  122.7 0.0 all-to-all-done.1
  122.7 0.1 broadcast_select_fusion
  122.9 17.6 %all-gather.5.cloned.1.call-done = bf16[4096,1024]{1,0:T(8,128)(2,1)} async-done(((bf16[128,1024]{1,0:T(8,128)(2,1)}), bf16[4096,1024]{1,0:T(8,128)(2,1)}) %all-gather.5.cloned.1.call-update) | async-done | bytes 8388624 | tf_op jit(solution)/shard_map/all_gather | solution.py:116
  140.4 0.0 copy-start.2
  140.5 5.7 %fusion.1 = bf16[32,8,8,128]{3,1,2,0:T(8,128)(2,1)S(1)} fusion(f32[256,1024]{1,0:T(8,128)S(1)} %fusion.4, bf16[4096,256]{1,0:T(8,128)(2,1)S(1)} %bitcast.47, bf16[4096,1024]{1,0:T(8,128)(2,1)} %all-gather.5.cloned.1.call-done), kind=kOutput, calls=%fused_computation.7 | convolution fusion | flops 2148007936 | bytes 12058624 | tf_op jit(solution)/shard_map/dot_general | solution.py:131
  146.2 0.1 copy.25
  146.3 0.9 copy.28
  147.2 0.0 copy-done.2
  147.2 0.8 broadcast_in_dim.83.lens_ref
  148.0 5.1 %shard_map.91 = bf16[64,32,128]{2,1,0:T(8,128)(2,1)} custom-call(bf16[64,32,128]{2,1,0:T(8,128)(2,1)} %bitcast.48, bf16[64,128,256]{2,1,0:T(8,128)(2,1)} %copy.22.kt_ref, bf16[64,256,128]{2,1,0:T(8,128)(2,1)} %get-tuple-element.11.v_ref, s32[64,1,256]{2,1,0:T(1,128)} %broadcast_in_dim.83.lens_ref), custom_call_target="tpu_custom_call" | custom-call | tf_op jit(solution)/shard_map/pallas_call | solution.py:70
  153.1 1.2 reshape.74
  154.2 1.0 copy.24
  (4 shorter events, 0.0 us)
Async XLA Ops:
  6.5 79.4 %all-gather.3.cloned.1.call-start = ((), (), s32[]{:S(2)}) async-start(), calls=%async_computation.2 | async-start | bytes 17301504 | tf_op jit(solution)/shard_map/all_gather | solution.py:108
  7.3 133.2 %all-gather.5.cloned.1.call-start = ((), (), s32[]{:S(2)}) async-start(), calls=%async_computation.3 | async-start | bytes 8650752 | tf_op jit(solution)/shard_map/all_gather | solution.py:116
  61.8 24.1 %copy-start.3 = (s32[64]{0:T(128)S(1)}, s32[64]{0:T(128)}, u32[]{:S(2)}) copy-start(s32[64]{0:T(128)} %param.17) | copy-start | bytes 772
  61.8 24.1 %copy-start.4 = (s32[64]{0:T(128)S(1)}, s32[64]{0:T(128)}, u32[]{:S(2)}) copy-start(s32[64]{0:T(128)} %param.16) | copy-start | bytes 772
  61.8 24.4 %copy-start.1 = (bf16[4,2,64,128]{3,2,1,0:T(8,128)(2,1)S(1)}, bf16[4,2,64,128]{3,2,1,0:T(8,128)(2,1)}, u32[]{:S(2)}) copy-start(bf16[4,2,64,128]{3,2,1,0:T(8,128)(2,1)} %param.14) | copy-start | bytes 393220
  70.7 24.1 %copy-start = (bf16[4,64,2048]{2,1,0:T(8,128)(2,1)S(1)}, bf16[4,64,2048]{2,1,0:T(8,128)(2,1)}, u32[]{:S(2)}) copy-start(bf16[4,64,2048]{2,1,0:T(8,128)(2,1)} %param.9) | copy-start | bytes 3145732
  106.2 16.5 %all-to-all-start.1 = ((f32[4,64,256]{2,1,0:T(8,128)}), f32[4,64,256]{2,1,0:T(8,128)S(1)}, u32[]{:S(2)}, u32[]{:S(2)}) async-start(f32[4,64,256]{2,1,0:T(8,128)} %broadcast_in_dim.78), calls=%async_computation.1 | async-start | bytes 524288 | tf_op jit(solution)/shard_map/all_to_all | solution.py:88
  140.4 6.7 %copy-start.2 = (s32[64]{0:T(128)S(1)}, s32[64]{0:T(128)}, u32[]{:S(2)}) copy-start(s32[64]{0:T(128)} %param.15) | copy-start | bytes 772
Sparse Core Ops, SparseCore 0:
  9.6 76.2 all-gather.2
  88.2 52.2 all-gather.4

commit v7 on v4

--- a/solution.py
+++ b/solution.py
@@ -90,7 +90,9 @@
     base = jnp.dot(full_rows, query_projection_weight, preferred_element_type=jnp.float32)
 
     up_local, down_all, base = lax.optimization_barrier((adapter_up_maps, down_all, base))
-    up_all = lax.all_gather(up_local, "dp", axis=0, tiled=True)
+    half = heads_width // 2
+    up_first = lax.all_gather(up_local[:, :half], "dp", axis=0, tiled=True)
+    up_second = lax.all_gather(up_local[:, half:], "dp", axis=0, tiled=True)
 
     position = pool_lookup(adapter_per_request, adapter_pool_position)
     row_position = jnp.tile(position, steps)
@@ -105,15 +107,18 @@
         shrink = shrink + partials[j]
     shrink = shrink.astype(jnp.bfloat16)
     wide_t = jnp.where(pick[:, None, :], shrink[None, :, :], jnp.zeros((), jnp.bfloat16))
-    delta = lax.dot_general(
-        wide_t.reshape(n_pool * ADAPTER_RANK, count_rows),
-        up_all,
-        (((0,), (0,)), ((), ())),
-        preferred_element_type=jnp.float32,
-    )
-    query = (base + delta).reshape(steps, requests, heads_width).astype(jnp.bfloat16)
-    return attend(query, key_value_cache, step_key_value, cache_valid_length)
+    wide_rows = wide_t.reshape(n_pool * ADAPTER_RANK, count_rows)
+    def heads(cols, up_part):
+        delta = lax.dot_general(
+            wide_rows, up_part, (((0,), (0,)), ((), ())), preferred_element_type=jnp.float32
+        )
+        query = (base[:, cols] + delta).reshape(steps, requests, half).astype(jnp.bfloat16)
+        return attend(query, key_value_cache, step_key_value, cache_valid_length)
 
+    first = heads(slice(0, half), up_first)
+    first, up_second = lax.optimization_barrier((first, up_second))
+    second = heads(slice(half, heads_width), up_second)
+    return jnp.concatenate([first, second], axis=-1)
 
 def solution(mesh):
     return jax.shard_map(

time: 161 us -> 203 us (1.26)
  waiting for transfers between devices: 54.6 us -> 79.8 us
  matrix products: 30.4 us -> 42.1 us
  local copies, waits for them, and re-layouts: 3.77 us -> 6.61 us
  other arithmetic: 1.72 us -> 3.88 us
    all_gather x1 -> x2, waiting for transfers between devices: 32.8 us -> 57.4 us  [the longest x1 32.8 us: per_device(): up_second = lax.all_gather(up_local[:, half:], 'dp', axis=0, tiled=True)]
    dot_general x1 -> x2, matrix products: 1.33 us -> 5.98 us  [attend(): jnp.einsum('trkgd,rckd->trkgc', grouped, keys, preferred_element_type=jnp...]
    dot_general x1 -> x2, matrix products: 2.46 us -> 4.91 us  [attend(): jnp.einsum('trkgd,srkd->trkgs', grouped, new_keys, preferred_element_type...]
    dot_general x1 -> x2, matrix products: 5.88 us -> 8.31 us  [heads(): lax.dot_general(wide_rows, up_part, (((0,), (0,)), ((), ())), preferred_e...]
  transfers between devices with their start and end apart: 3 -> 4, of which waited for: 3 -> 4; matrix products, arithmetic and copies ran while one was open for 14% -> 18% of each run, Pallas kernels for 0% -> 0%
where the time goes in v7:
time: 203 us
  waiting for transfers between devices  79.8 us (39%)
  blocking collectives  52.7 us (26%)
  matrix products  42.1 us (21%)
  between operations  13.4 us (7%)
  local copies, waits for them, and re-layouts  6.61 us (3%)
  starting transfers between devices  4.08 us (2%)
  other arithmetic  3.88 us (2%)
    all_to_all x1, blocking collectives, gather_tensor(): return lax.all_to_all(tiled, axis_name, 0, 0, tiled=True)  52.7 us
    all_gather x1, waiting for transfers between devices, per_device(): up_second = lax.all_gather(up_local[:, half:], 'dp', axis=0, tiled=True)  32.8 us
    all_gather x1, waiting for transfers between devices, per_device(): up_first = lax.all_gather(up_local[:, :half], 'dp', axis=0, tiled=True)  24.6 us
    all_gather x1, waiting for transfers between devices, per_device(): down_all = lax.all_gather(adapter_down_maps, 'dp', axis=0, tiled=True)  15.1 us
    dot_general x1, matrix products, per_device(): lax.dot_general(down_all, token_rows, (((1,), (1,)), ((), ())), preferred...  10.5 us
    dot_general x1, matrix products, per_device(): jnp.dot(full_rows, query_projection_weight, preferred_element_type=jnp.fl...  8.92 us
    dot_general x2, matrix products, heads(): lax.dot_general(wide_rows, up_part, (((0,), (0,)), ((), ())), preferred_e...  8.31 us
    dot_general x2, matrix products, attend(): jnp.einsum('trkgd,rckd->trkgc', grouped, keys, preferred_element_type=jnp...  5.98 us
  transfers between devices with their start and end apart: 4, of which 4 were waited for; matrix products, arithmetic and copies ran while one was open for 18% of the time, Pallas kernels for 0%

profile of v7, /device:TPU:1, one launch (start us, length us, event | category | flops | bytes accessed | tf_op | source)
XLA Modules:
  0.0 202.6 jit_solution(9933313771713877359)
XLA Ops:
  6.5 0.0 all-gather.4.cloned.1.call-start
  6.5 0.7 all-gather.4.cloned.1.call-update
  7.3 0.0 all-gather.6.cloned.1.call-start
  7.3 1.5 copy.31
  8.8 0.3 broadcast_in_dim.118
  9.1 52.7 %all_to_all.10 = bf16[4,256,2048]{1,2,0:T(8,128)(2,1)S(1)} all-to-all(bf16[4,256,2048]{1,2,0:T(8,128)(2,1)S(1)} %broadcast_in_dim.118), channel_id=1, replica_groups=mesh['dp'=32,'tensor'=4] {'tensor'}, dimensions={0} | all-to-all | bytes 8388608 | tf_op jit(solution)/shard_map/all_to_all | solution.py:65
  61.8 0.0 copy-start.1
  61.8 0.0 copy-start.6
  61.8 0.0 copy-start.7
  61.8 0.0 copy-start.2
  61.8 0.0 copy-start
  61.8 8.9 %fusion.100 = f32[256,1024]{1,0:T(8,128)S(1)} fusion(bf16[256,8192]{0,1:T(8,128)(2,1)S(1)} %bitcast.160, bf16[8192,1024]{1,0:T(8,128)(2,1)} %param.10), kind=kOutput, calls=%fused_computation.85 | convolution fusion | flops 4294967296 | bytes 22020096 | tf_op jit(solution)/shard_map/dot_general | solution.py:90
  70.8 15.1 %all-gather.4.cloned.1.call-done = bf16[4096,2048]{1,0:T(8,128)(2,1)} async-done(((bf16[128,2048]{1,0:T(8,128)(2,1)}), bf16[4096,2048]{1,0:T(8,128)(2,1)}) %all-gather.4.cloned.1.call-update) | async-done | bytes 16777232 | tf_op jit(solution)/shard_map/all_gather | solution.py:85
  85.9 0.0 copy-done.1
  85.9 0.7 fusion.94
  86.6 0.0 all-gather.6.cloned.1.call-update
  86.7 0.0 all-gather.8.cloned.1.call-start
  86.7 0.7 all-gather.8.cloned.1.call-update
  87.4 0.0 copy-done.6
  87.4 0.0 copy-done.7
  87.4 0.2 select_reduce_fusion.1
  87.6 0.1 eq.36
  87.7 0.0 copy-done.2
  87.7 0.0 copy-done
  87.8 0.0 copy-start.3
  87.8 10.5 %select_reduce_fusion = f32[64,256]{1,0:T(8,128)S(1)} fusion(pred[64,256]{1,0:T(8,128)(4,1)S(1)} %iota_compare_fusion, bf16[64,64,2048]{2,1,0:T(8,128)(2,1)} %bitcast.165, bf16[256,2048,1]{1,0,2:T(8,128)(2,1)S(1)} %bitcast.164), kind=kOutput, calls=%fused_computation | convolution fusion | flops 4297048064 | bytes 17907712 | tf_op jit(solution)/shard_map/dot_general | solution.py:100
  98.3 0.7 broadcast_in_dim.123
  99.0 4.0 %all-to-all-start.1 = ((f32[4,64,256]{2,1,0:T(8,128)}), f32[4,64,256]{2,1,0:T(8,128)S(1)}, u32[]{:S(2)}, u32[]{:S(2)}) async-start(f32[4,64,256]{2,1,0:T(8,128)} %broadcast_in_dim.123), calls=%async_computation.1 | async-start | bytes 524288 | tf_op jit(solution)/shard_map/all_to_all | solution.py:65
  103.0 0.0 copy-done.3
  103.0 0.1 iota_compare_fusion.2
  103.1 5.8 %all-to-all-done.1 = f32[4,64,256]{2,1,0:T(8,128)S(1)} async-done(((f32[4,64,256]{2,1,0:T(8,128)}), f32[4,64,256]{2,1,0:T(8,128)S(1)}, u32[]{:S(2)}, u32[]{:S(2)}) %all-to-all-start.1) | async-done | bytes 262176 | tf_op jit(solution)/shard_map/all_to_all | solution.py:65
  109.0 0.1 broadcast_select_fusion
  109.1 24.6 %all-gather.6.cloned.1.call-done = bf16[4096,512]{1,0:T(8,128)(2,1)} async-done(((bf16[128,512]{1,0:T(8,128)(2,1)}), bf16[4096,512]{1,0:T(8,128)(2,1)}) %all-gather.6.cloned.1.call-update) | async-done | bytes 4194320 | tf_op jit(solution)/shard_map/all_gather | solution.py:94
  133.8 4.2 %fusion.38 = bf16[256,512]{1,0:T(8,128)(2,1)} fusion(bf16[4096,256]{1,0:T(8,128)(2,1)S(1)} %bitcast.161, bf16[4096,512]{1,0:T(8,128)(2,1)} %all-gather.6.cloned.1.call-done, f32[256,1024]{1,0:T(8,128)S(1)} %fusion.100), kind=kOutput, calls=%fused_computation.28 | convolution fusion | flops 1074003968 | bytes 7077888 | tf_op jit(solution)/shard_map/dot_general | solution.py:112
  137.9 1.0 convert_element_type.48
  138.9 0.0 copy-start.4
  138.9 2.5 %fusion.97 = (f32[4,64,4]{2,0,1:T(4,128)S(1)}, f32[4,64,1,4,4]{3,4,0,1,2:T(4,128)S(1)}) fusion(bf16[4,1,64,128]{3,2,1,0:T(8,128)(2,1)S(1)} %get-tuple-element.18, bf16[4,64,4,128]{3,2,1,0:T(4,128)(2,1)S(1)} %convert_element_type.48, pred[4,4]{1,0:T(4,128)(4,1)S(1)} %iota_compare_fusion.3), kind=kOutput, calls=%fused_computation.82 | convolution fusion | flops 1059840 | bytes 348176 | tf_op jit(solution)/shard_map/trkgd,srkd->trkgs/dot_general | solution.py:36
  141.4 2.9 %fusion.96 = (f32[4,64,4]{2,0,1:T(4,128)S(1)}, f32[4,64,1,4,128]{4,3,0,1,2:T(4,128)S(1)}) fusion(bf16[2,64,128,128]{3,2,1,0:T(8,128)(2,1)} %param.13, bf16[4,64,4,128]{3,2,1,0:T(4,128)(2,1)S(1)} %convert_element_type.48, pred[64,128]{1,0:T(8,128)(4,1)S(1)} %iota_compare_fusion.2), kind=kOutput, calls=%fused_computation.81 | convolution fusion | flops 33946624 | bytes 2895872 | tf_op jit(solution)/shard_map/trkgd,rckd->trkgc/dot_general | solution.py:31
  144.4 0.5 fusion.68
  144.8 0.7 fusion.66
  145.6 0.4 fusion.80
  146.0 0.0 copy-done.4
  146.1 1.6 fusion.63
  147.7 1.1 convert_element_type.52
  148.7 32.8 %all-gather.8.cloned.1.call-done = bf16[4096,512]{1,0:T(8,128)(2,1)} async-done(((bf16[128,512]{1,0:T(8,128)(2,1)}), bf16[4096,512]{1,0:T(8,128)(2,1)}) %all-gather.8.cloned.1.call-update) | async-done | bytes 4194320 | tf_op jit(solution)/shard_map/all_gather | solution.py:95
  181.5 4.2 %fusion.39 = bf16[256,512]{1,0:T(8,128)(2,1)} fusion(bf16[4096,256]{1,0:T(8,128)(2,1)S(1)} %bitcast.162, bf16[4096,512]{1,0:T(8,128)(2,1)} %all-gather.8.cloned.1.call-done, f32[256,1024]{1,0:T(8,128)S(1)} %fusion.100), kind=kOutput, calls=%fused_computation.29 | convolution fusion | flops 1074003968 | bytes 7077888 | tf_op jit(solution)/shard_map/dot_general | solution.py:112
  185.7 1.0 convert_element_type.54
  186.7 0.0 copy-start.5
  186.7 3.1 %fusion.98 = (f32[4,64,4]{2,0,1:T(4,128)S(1)}, f32[4,64,1,4,128]{4,3,0,1,2:T(4,128)S(1)}) fusion(bf16[2,64,128,128]{3,2,1,0:T(8,128)(2,1)} %param.13, bf16[4,64,4,128]{3,2,1,0:T(4,128)(2,1)S(1)} %convert_element_type.54, pred[64,128]{1,0:T(8,128)(4,1)S(1)} %iota_compare_fusion.2), kind=kOutput, calls=%fused_computation.83 | convolution fusion | flops 33946624 | bytes 2895872 | tf_op jit(solution)/shard_map/trkgd,rckd->trkgc/dot_general | solution.py:31
  189.8 2.5 %fusion.99 = (f32[4,64,4]{2,0,1:T(4,128)S(1)}, f32[4,64,1,4,4]{3,4,0,1,2:T(4,128)S(1)}) fusion(bf16[4,1,64,128]{3,2,1,0:T(8,128)(2,1)S(1)} %get-tuple-element.18, bf16[4,64,4,128]{3,2,1,0:T(4,128)(2,1)S(1)} %convert_element_type.54, pred[4,4]{1,0:T(4,128)(4,1)S(1)} %iota_compare_fusion.3), kind=kOutput, calls=%fused_computation.84 | convolution fusion | flops 1059840 | bytes 348176 | tf_op jit(solution)/shard_map/trkgd,srkd->trkgs/dot_general | solution.py:36
  192.3 0.5 fusion.72
  192.7 0.4 fusion.75
  193.2 0.7 fusion.70
  193.9 0.0 copy-done.5
  194.0 1.0 fusion.57
  195.0 0.1 convert_element_type.58
  195.2 0.9 pad_maximum_fusion
  (11 shorter events, 0.3 us)
Async XLA Ops:
  6.5 79.4 %all-gather.4.cloned.1.call-start = ((), (), s32[]{:S(2)}) async-start(), calls=%async_computation.2 | async-start | bytes 17301504 | tf_op jit(solution)/shard_map/all_gather | solution.py:85
  7.3 126.5 %all-gather.6.cloned.1.call-start = ((), (), s32[]{:S(2)}) async-start(), calls=%async_computation.3 | async-start | bytes 4325376 | tf_op jit(solution)/shard_map/all_gather | solution.py:94
  61.8 24.1 %copy-start.1 = (bf16[128,1024]{1,0:T(8,128)(2,1)S(1)}, bf16[128,1024]{1,0:T(8,128)(2,1)}, u32[]{:S(2)}) copy-start(bf16[128,1024]{1,0:T(8,128)(2,1)} %param.12) | copy-start | bytes 786436
  61.8 25.6 %copy-start.6 = (s32[64]{0:T(128)S(1)}, s32[64]{0:T(128)}, u32[]{:S(2)}) copy-start(s32[64]{0:T(128)} %param.17) | copy-start | bytes 772
  61.8 25.6 %copy-start.7 = (s32[64]{0:T(128)S(1)}, s32[64]{0:T(128)}, u32[]{:S(2)}) copy-start(s32[64]{0:T(128)} %param.16) | copy-start | bytes 772
  61.8 25.9 %copy-start.2 = (bf16[4,2,64,128]{3,2,1,0:T(8,128)(2,1)S(1)}, bf16[4,2,64,128]{3,2,1,0:T(8,128)(2,1)}, u32[]{:S(2)}) copy-start(bf16[4,2,64,128]{3,2,1,0:T(8,128)(2,1)} %param.14) | copy-start | bytes 393220
  61.8 25.9 %copy-start = (bf16[4,64,2048]{2,1,0:T(8,128)(2,1)S(1)}, bf16[4,64,2048]{2,1,0:T(8,128)(2,1)}, u32[]{:S(2)}) copy-start(bf16[4,64,2048]{2,1,0:T(8,128)(2,1)} %param.9) | copy-start | bytes 3145732
  86.7 94.8 %all-gather.8.cloned.1.call-start = ((), (), s32[]{:S(2)}) async-start(), calls=%async_computation.4 | async-start | bytes 4325376 | tf_op jit(solution)/shard_map/all_gather | solution.py:95
  87.8 15.3 %copy-start.3 = (s32[64]{0:T(128)S(1)}, s32[64]{0:T(128)}, u32[]{:S(2)}) copy-start(s32[64]{0:T(128)} %param.15) | copy-start | bytes 772
  99.0 9.9 %all-to-all-start.1 = ((f32[4,64,256]{2,1,0:T(8,128)}), f32[4,64,256]{2,1,0:T(8,128)S(1)}, u32[]{:S(2)}, u32[]{:S(2)}) async-start(f32[4,64,256]{2,1,0:T(8,128)} %broadcast_in_dim.123), calls=%async_computation.1 | async-start | bytes 524288 | tf_op jit(solution)/shard_map/all_to_all | solution.py:65
  138.9 7.1 %copy-start.4 = (bf16[2,64,128,128]{3,2,1,0:T(8,128)(2,1)S(1)}, bf16[2,64,128,128]{3,2,1,0:T(8,128)(2,1)}, u32[]{:S(2)}) copy-start(bf16[2,64,128,128]{3,2,1,0:T(8,128)(2,1)} %param.13) | copy-start | bytes 12582916
  186.7 7.3 %copy-start.5 = (bf16[2,64,128,128]{3,2,1,0:T(8,128)(2,1)S(1)}, bf16[2,64,128,128]{3,2,1,0:T(8,128)(2,1)}, u32[]{:S(2)}) copy-start(bf16[2,64,128,128]{3,2,1,0:T(8,128)(2,1)} %param.13) | copy-start | bytes 12582916
Sparse Core Ops, SparseCore 0:
  9.6 76.2 all-gather.3
  88.2 45.5 all-gather.5
  136.0 45.4 all-gather.7

commit v8 on v4

--- a/solution.py
+++ b/solution.py
@@ -85,12 +85,19 @@
     down_all = lax.all_gather(adapter_down_maps, "dp", axis=0, tiled=True)
     n_pool = down_all.shape[0] // ADAPTER_RANK
 
-    pieces = gather_tensor(token_rows, "tensor", n_tensor)
-    full_rows = jnp.transpose(pieces, (1, 0, 2)).reshape(count_rows, n_tensor * part_width)
-    base = jnp.dot(full_rows, query_projection_weight, preferred_element_type=jnp.float32)
+    def base_rows(rows):
+        pieces = gather_tensor(rows, "tensor", n_tensor)
+        full_rows = jnp.transpose(pieces, (1, 0, 2)).reshape(rows.shape[0], n_tensor * part_width)
+        return jnp.dot(full_rows, query_projection_weight, preferred_element_type=jnp.float32)
 
-    up_local, down_all, base = lax.optimization_barrier((adapter_up_maps, down_all, base))
+    split = count_rows // 2
+    base_first = base_rows(token_rows[:split])
+
+    up_local, down_all, base_first = lax.optimization_barrier(
+        (adapter_up_maps, down_all, base_first)
+    )
     up_all = lax.all_gather(up_local, "dp", axis=0, tiled=True)
+    base = jnp.concatenate([base_first, base_rows(token_rows[split:])], axis=0)
 
     position = pool_lookup(adapter_per_request, adapter_pool_position)
     row_position = jnp.tile(position, steps)

time: 161 us -> 161 us (level)
  blocking collectives: 52.7 us -> 30.3 us
  matrix products: 30.4 us -> 39 us
  waiting for transfers between devices: 54.6 us -> 61.7 us
  starting transfers between devices: 4.04 us -> 7.63 us
  local copies, waits for them, and re-layouts: 3.77 us -> 5.74 us
    all_gather x1, waiting for transfers between devices: 32.8 us -> 9.44 us  [per_device(): up_all = lax.all_gather(up_local, 'dp', axis=0, tiled=True)]
    all_gather x1, waiting for transfers between devices: 15.2 us -> 38.2 us  [per_device(): down_all = lax.all_gather(adapter_down_maps, 'dp', axis=0, tiled=True)]
    all_to_all x1, blocking collectives: 52.7 us -> 30.3 us  [gather_tensor(): return lax.all_to_all(tiled, axis_name, 0, 0, tiled=True)]
    dot_general x1 -> x2, matrix products: 8.91 us -> 17 us  [base_rows(): jnp.dot(full_rows, query_projection_weight, preferred_element_type=jnp.fl...]
    all_to_all x1 -> x2, waiting for transfers between devices: 5.9 us -> 13.3 us  [gather_tensor(): return lax.all_to_all(tiled, axis_name, 0, 0, tiled=True)]
    all_to_all x1 -> x2, starting transfers between devices: 4 us -> 7.59 us  [gather_tensor(): return lax.all_to_all(tiled, axis_name, 0, 0, tiled=True)]
  transfers between devices with their start and end apart: 3 -> 4, of which waited for: 3 -> 3; matrix products, arithmetic and copies ran while one was open for 14% -> 21% of each run, Pallas kernels for 0% -> 0%
where the time goes in v8:
time: 161 us
  waiting for transfers between devices  61.7 us (38%)
  matrix products  39 us (24%)
  blocking collectives  30.3 us (19%)
  between operations  13.6 us (8%)
  starting transfers between devices  7.63 us (5%)
  local copies, waits for them, and re-layouts  5.74 us (4%)
  other arithmetic  2.86 us (2%)
    all_gather x1, waiting for transfers between devices, per_device(): down_all = lax.all_gather(adapter_down_maps, 'dp', axis=0, tiled=True)  38.2 us
    all_to_all x1, blocking collectives, gather_tensor(): return lax.all_to_all(tiled, axis_name, 0, 0, tiled=True)  30.3 us
    dot_general x2, matrix products, base_rows(): jnp.dot(full_rows, query_projection_weight, preferred_element_type=jnp.fl...  17 us
    all_to_all x2, waiting for transfers between devices, gather_tensor(): return lax.all_to_all(tiled, axis_name, 0, 0, tiled=True)  13.3 us
    dot_general x1, matrix products, per_device(): lax.dot_general(down_all, token_rows, (((1,), (1,)), ((), ())), preferred...  11 us
    all_gather x1, waiting for transfers between devices, per_device(): up_all = lax.all_gather(up_local, 'dp', axis=0, tiled=True)  9.44 us
    all_to_all x2, starting transfers between devices, gather_tensor(): return lax.all_to_all(tiled, axis_name, 0, 0, tiled=True)  7.59 us
    dot_general x1, matrix products, per_device(): lax.dot_general(wide_t.reshape(n_pool * ADAPTER_RANK, count_rows), up_all...  5.89 us
  transfers between devices with their start and end apart: 4, of which 3 were waited for; matrix products, arithmetic and copies ran while one was open for 21% of the time, Pallas kernels for 0%

profile of v8, /device:TPU:1, one launch (start us, length us, event | category | flops | bytes accessed | tf_op | source)
XLA Modules:
  0.0 160.9 jit_solution(12153968295516909911)
XLA Ops:
  6.5 0.0 all-gather.3.cloned.1.call-start
  6.5 0.7 all-gather.3.cloned.1.call-update
  7.3 0.0 all-gather.5.cloned.1.call-start
  7.3 1.3 fusion.37
  8.6 0.3 copy.22
  8.9 0.3 broadcast_in_dim.108
  9.1 30.3 %all_to_all.15 = bf16[4,128,2048]{1,2,0:T(8,128)(2,1)S(1)} all-to-all(bf16[4,128,2048]{1,2,0:T(8,128)(2,1)S(1)} %broadcast_in_dim.108), channel_id=1, replica_groups=mesh['dp'=32,'tensor'=4] {'tensor'}, dimensions={0} | all-to-all | bytes 4194304 | tf_op jit(solution)/shard_map/all_to_all | solution.py:65
  39.4 8.2 %fusion.41 = f32[128,1024]{1,0:T(8,128)S(1)} fusion(bf16[128,8192]{0,1:T(8,128)(2,1)S(1)} %bitcast.113, bf16[8192,1024]{1,0:T(8,128)(2,1)} %param.10), kind=kOutput, calls=%fused_computation.49 | convolution fusion | flops 2147483648 | bytes 19398656 | tf_op jit(solution)/shard_map/dot_general | solution.py:91
  47.7 0.0 copy-start.4
  47.7 0.0 copy-start.5
  47.7 0.0 copy-start.3
  47.7 0.0 copy-start.1
  47.7 38.2 %all-gather.3.cloned.1.call-done = bf16[4096,2048]{1,0:T(8,128)(2,1)} async-done(((bf16[128,2048]{1,0:T(8,128)(2,1)}), bf16[4096,2048]{1,0:T(8,128)(2,1)}) %all-gather.3.cloned.1.call-update) | async-done | bytes 16777232 | tf_op jit(solution)/shard_map/all_gather | solution.py:85
  85.9 0.0 all-gather.5.cloned.1.call-update
  85.9 0.3 copy.23
  86.2 1.6 %broadcast_in_dim.110 = bf16[4,128,2048]{1,2,0:T(8,128)(2,1)} broadcast(bf16[128,2048]{0,1:T(8,128)(2,1)S(1)} %copy.23), dimensions={1,2} | broadcast | bytes 2621440 | tf_op jit(solution)/shard_map/broadcast_in_dim | solution.py:64
  87.8 4.0 %all-to-all-start.1 = ((bf16[4,128,2048]{1,2,0:T(8,128)(2,1)}), bf16[4,128,2048]{1,2,0:T(8,128)(2,1)S(1)}, u32[]{:S(2)}, u32[]{:S(2)}) async-start(bf16[4,128,2048]{1,2,0:T(8,128)(2,1)} %broadcast_in_dim.110), calls=%async_computation.1 | async-start | bytes 4194304 | tf_op jit(solution)/shard_map/all_to_all | solution.py:65
  91.8 0.0 copy-done.4
  91.8 0.0 copy-done.5
  91.9 0.2 select_reduce_fusion.1
  92.0 0.1 eq.36
  92.1 0.0 copy-done.3
  92.1 0.7 iota_compare_fusion.2
  92.8 0.5 iota_compare_fusion.3
  93.4 0.0 copy-done.1
  93.4 11.0 %select_reduce_fusion = f32[64,256]{1,0:T(8,128)S(1)} fusion(pred[64,256]{1,0:T(8,128)(4,1)S(1)} %iota_compare_fusion, bf16[64,64,2048]{2,1,0:T(8,128)(2,1)} %bitcast.119, bf16[256,2048,1]{1,0,2:T(8,128)(2,1)} %bitcast.118), kind=kOutput, calls=%fused_computation | convolution fusion | flops 4297048064 | bytes 17907712 | tf_op jit(solution)/shard_map/dot_general | solution.py:105
  104.4 13.3 %all-to-all-done.1 = bf16[4,128,2048]{1,2,0:T(8,128)(2,1)S(1)} async-done(((bf16[4,128,2048]{1,2,0:T(8,128)(2,1)}), bf16[4,128,2048]{1,2,0:T(8,128)(2,1)S(1)}, u32[]{:S(2)}, u32[]{:S(2)}) %all-to-all-start.1) | async-done | bytes 2097184 | tf_op jit(solution)/shard_map/all_to_all | solution.py:65
  117.7 0.7 broadcast_in_dim.115
  118.5 3.6 %all-to-all-start.2 = ((f32[4,64,256]{2,1,0:T(8,128)}), f32[4,64,256]{2,1,0:T(8,128)S(1)}, u32[]{:S(2)}, u32[]{:S(2)}) async-start(f32[4,64,256]{2,1,0:T(8,128)} %broadcast_in_dim.115), calls=%async_computation.2 | async-start | bytes 524288 | tf_op jit(solution)/shard_map/all_to_all | solution.py:65
  122.1 8.8 %fusion.42 = f32[128,1024]{1,0:T(8,128)S(1)} fusion(bf16[128,8192]{0,1:T(8,128)(2,1)S(1)} %bitcast.112, bf16[8192,1024]{1,0:T(8,128)(2,1)} %param.10), kind=kOutput, calls=%fused_computation.50 | convolution fusion | flops 2147483648 | bytes 19398656 | tf_op jit(solution)/shard_map/dot_general | solution.py:91
  130.8 0.0 all-to-all-done.2
  130.9 0.1 broadcast_select_fusion
  131.0 9.4 %all-gather.5.cloned.1.call-done = bf16[4096,1024]{1,0:T(8,128)(2,1)} async-done(((bf16[128,1024]{1,0:T(8,128)(2,1)}), bf16[4096,1024]{1,0:T(8,128)(2,1)}) %all-gather.5.cloned.1.call-update) | async-done | bytes 8388624 | tf_op jit(solution)/shard_map/all_gather | solution.py:99
  140.4 0.0 copy-start.6
  140.5 0.0 copy-start
  140.5 0.0 copy-start.2
  140.5 5.9 %fusion.21 = bf16[32,8,8,128]{3,1,2,0:T(8,128)(2,1)S(1)} fusion(bf16[4096,256]{1,0:T(8,128)(2,1)S(1)} %bitcast.111, bf16[4096,1024]{1,0:T(8,128)(2,1)} %all-gather.5.cloned.1.call-done, f32[128,1024]{1,0:T(8,128)S(1)} %fusion.42, f32[128,1024]{1,0:T(8,128)S(1)} %fusion.41), kind=kOutput, calls=%fused_computation.18 | convolution fusion | flops 2148270080 | bytes 12058624 | tf_op jit(solution)/shard_map/dot_general | solution.py:115
  146.4 0.1 copy.35
  146.5 0.0 copy-done.6
  146.5 2.5 %fusion.40 = (f32[4,64,8]{2,0,1:T(4,128)S(1)}, f32[4,64,1,8,4]{3,4,0,1,2:T(4,128)S(1)}) fusion(bf16[4,1,64,128]{3,2,1,0:T(8,128)(2,1)S(1)} %get-tuple-element.14, pred[4,4]{1,0:T(4,128)(4,1)S(1)} %copy-done.6, bf16[4,64,8,128]{3,2,1,0:T(8,128)(2,1)S(1)} %bitcast.116), kind=kOutput, calls=%fused_computation.48 | convolution fusion | flops 2119680 | bytes 630800 | tf_op jit(solution)/shard_map/trkgd,srkd->trkgs/dot_general | solution.py:36
  148.9 0.0 copy-done
  148.9 0.0 copy-done.2
  148.9 1.3 fusion.39
  150.3 0.7 fusion.23
  151.1 0.7 fusion
  151.8 0.5 fusion.30
  152.3 0.6 divide_convert_fusion
  153.0 0.1 convert_element_type.31
  153.1 1.0 copy.28
  (6 shorter events, 0.1 us)
Async XLA Ops:
  6.5 79.4 %all-gather.3.cloned.1.call-start = ((), (), s32[]{:S(2)}) async-start(), calls=%async_computation.3 | async-start | bytes 17301504 | tf_op jit(solution)/shard_map/all_gather | solution.py:85
  7.3 133.2 %all-gather.5.cloned.1.call-start = ((), (), s32[]{:S(2)}) async-start(), calls=%async_computation.4 | async-start | bytes 8650752 | tf_op jit(solution)/shard_map/all_gather | solution.py:99
  47.7 44.2 %copy-start.4 = (s32[64]{0:T(128)S(1)}, s32[64]{0:T(128)}, u32[]{:S(2)}) copy-start(s32[64]{0:T(128)} %param.17) | copy-start | bytes 772
  47.7 44.2 %copy-start.5 = (s32[64]{0:T(128)S(1)}, s32[64]{0:T(128)}, u32[]{:S(2)}) copy-start(s32[64]{0:T(128)} %param.16) | copy-start | bytes 772
  47.7 44.4 %copy-start.3 = (s32[64]{0:T(128)S(1)}, s32[64]{0:T(128)}, u32[]{:S(2)}) copy-start(s32[64]{0:T(128)} %param.15) | copy-start | bytes 772
  47.7 45.7 %copy-start.1 = (bf16[4,2,64,128]{3,2,1,0:T(8,128)(2,1)S(1)}, bf16[4,2,64,128]{3,2,1,0:T(8,128)(2,1)}, u32[]{:S(2)}) copy-start(bf16[4,2,64,128]{3,2,1,0:T(8,128)(2,1)} %param.14) | copy-start | bytes 393220
  87.8 29.9 %all-to-all-start.1 = ((bf16[4,128,2048]{1,2,0:T(8,128)(2,1)}), bf16[4,128,2048]{1,2,0:T(8,128)(2,1)S(1)}, u32[]{:S(2)}, u32[]{:S(2)}) async-start(bf16[4,128,2048]{1,2,0:T(8,128)(2,1)} %broadcast_in_dim.110), calls=%async_computation.1 | async-start | bytes 4194304 | tf_op jit(solution)/shard_map/all_to_all | solution.py:65
  118.5 12.4 %all-to-all-start.2 = ((f32[4,64,256]{2,1,0:T(8,128)}), f32[4,64,256]{2,1,0:T(8,128)S(1)}, u32[]{:S(2)}, u32[]{:S(2)}) async-start(f32[4,64,256]{2,1,0:T(8,128)} %broadcast_in_dim.115), calls=%async_computation.2 | async-start | bytes 524288 | tf_op jit(solution)/shard_map/all_to_all | solution.py:65
  140.4 6.0 %copy-start.6 = (pred[4,4]{1,0:T(4,128)(4,1)S(1)}, pred[4,4]{1,0:T(4,128)(4,1)}, u32[]{:S(2)}) copy-start(pred[4,4]{1,0:T(4,128)(4,1)} %iota_compare_fusion.3) | copy-start | bytes 52
  140.5 8.5 %copy-start = (bf16[2,64,128,128]{3,2,1,0:T(8,128)(2,1)S(1)}, bf16[2,64,128,128]{3,2,1,0:T(8,128)(2,1)}, u32[]{:S(2)}) copy-start(bf16[2,64,128,128]{3,2,1,0:T(8,128)(2,1)} %param.13) | copy-start | bytes 12582916
  140.5 8.5 %copy-start.2 = (pred[64,128]{1,0:T(8,128)(4,1)S(1)}, pred[64,128]{1,0:T(8,128)(4,1)}, u32[]{:S(2)}) copy-start(pred[64,128]{1,0:T(8,128)(4,1)} %iota_compare_fusion.2) | copy-start | bytes 24580
Sparse Core Ops, SparseCore 0:
  9.6 76.2 all-gather.2
  88.2 52.2 all-gather.4

commit v9 on v4

--- a/solution.py
+++ b/solution.py
@@ -82,15 +82,19 @@
     n_tensor = query_projection_weight.shape[0] // part_width
     token_rows = normed_hidden_state.reshape(count_rows, part_width)
 
-    down_all = lax.all_gather(adapter_down_maps, "dp", axis=0, tiled=True)
+    down_width = adapter_down_maps.shape[1]
+    both = jnp.concatenate([adapter_down_maps, adapter_up_maps], axis=1)
+    both_all = lax.all_gather(both, "dp", axis=0, tiled=True)
+    down_all = both_all[:, :down_width]
+    up_all = both_all[:, down_width:]
     n_pool = down_all.shape[0] // ADAPTER_RANK
 
     pieces = gather_tensor(token_rows, "tensor", n_tensor)
     full_rows = jnp.transpose(pieces, (1, 0, 2)).reshape(count_rows, n_tensor * part_width)
     base = jnp.dot(full_rows, query_projection_weight, preferred_element_type=jnp.float32)
+    lengths_in, base = lax.optimization_barrier((cache_valid_length, base))
+    lengths_all = lax.all_gather(lengths_in, "dp", axis=0, tiled=True)
 
-    up_local, down_all, base = lax.optimization_barrier((adapter_up_maps, down_all, base))
-    up_all = lax.all_gather(up_local, "dp", axis=0, tiled=True)
 
     position = pool_lookup(adapter_per_request, adapter_pool_position)
     row_position = jnp.tile(position, steps)
@@ -112,6 +116,7 @@
         preferred_element_type=jnp.float32,
     )
     query = (base + delta).reshape(steps, requests, heads_width).astype(jnp.bfloat16)
+    query, lengths_all = lax.optimization_barrier((query, lengths_all))
     return attend(query, key_value_cache, step_key_value, cache_valid_length)
 
 

time: 161 us -> 151 us (0.938)
  blocking collectives: 52.7 us -> 0 us
  waiting for transfers between devices: 54.6 us -> 87.4 us
  local copies, waits for them, and re-layouts: 3.77 us -> 11.5 us
  starting transfers between devices: 4.04 us -> 9.15 us
  matrix products: 30.4 us -> 25.5 us
  other arithmetic: 1.72 us -> 3.8 us
    all_to_all x1 -> x0, blocking collectives: 52.7 us -> none  [gather_tensor(): return lax.all_to_all(tiled, axis_name, 0, 0, tiled=True)]
    all_gather x2 -> x1, waiting for transfers between devices: 47.9 us -> 87.3 us  [per_device(): both_all = lax.all_gather(both, 'dp', axis=0, tiled=True)]
    all_to_all x1 -> x2, waiting for transfers between devices: 5.9 us -> 0.01 us  [gather_tensor(): return lax.all_to_all(tiled, axis_name, 0, 0, tiled=True)]
    slice x0 -> x2, local copies, waits for them, and re-layouts: none -> 5.77 us  [per_device(): down_all = both_all[:, :down_width]]
    dot_general x1, matrix products: 10.5 us -> 4.82 us  [per_device(): lax.dot_general(down_all, token_rows, (((1,), (1,)), ((), ())), preferred...]
    all_to_all x1 -> x2, starting transfers between devices: 4 us -> 9.15 us  [gather_tensor(): return lax.all_to_all(tiled, axis_name, 0, 0, tiled=True)]
    concatenate x0 -> x1, other arithmetic: none -> 2.08 us  [per_device(): both = jnp.concatenate([adapter_down_maps, adapter_up_maps], axis=1)]
    broadcast_in_dim x3, local copies, waits for them, and re-layouts: 2.47 us -> 4.41 us  [gather_tensor(): tiled = jnp.broadcast_to(value[None], (count,) + value.shape)]
  transfers between devices with their start and end apart: 3 -> 3, of which waited for: 3 -> 1; matrix products, arithmetic and copies ran while one was open for 14% -> 12% of each run, Pallas kernels for 0% -> 0%
where the time goes in v9:
time: 151 us
  waiting for transfers between devices  87.4 us (58%)
  matrix products  25.5 us (17%)
  between operations  13.6 us (9%)
  local copies, waits for them, and re-layouts  11.5 us (8%)
  starting transfers between devices  9.15 us (6%)
  other arithmetic  3.8 us (3%)
    all_gather x1, waiting for transfers between devices, per_device(): both_all = lax.all_gather(both, 'dp', axis=0, tiled=True)  87.3 us
    dot_general x1, matrix products, per_device(): jnp.dot(full_rows, query_projection_weight, preferred_element_type=jnp.fl...  9.65 us
    all_to_all x2, starting transfers between devices, gather_tensor(): return lax.all_to_all(tiled, axis_name, 0, 0, tiled=True)  9.15 us
    dot_general x1, matrix products, per_device(): lax.dot_general(wide_t.reshape(n_pool * ADAPTER_RANK, count_rows), up_all...  5.9 us
    slice x2, local copies, waits for them, and re-layouts, per_device(): down_all = both_all[:, :down_width]  5.77 us
    dot_general x1, matrix products, per_device(): lax.dot_general(down_all, token_rows, (((1,), (1,)), ((), ())), preferred...  4.82 us
    broadcast_in_dim x3, local copies, waits for them, and re-layouts, gather_tensor(): tiled = jnp.broadcast_to(value[None], (count,) + value.shape)  4.41 us
  transfers between devices with their start and end apart: 3, of which 1 were waited for; matrix products, arithmetic and copies ran while one was open for 12% of the time, Pallas kernels for 0%

profile of v9, /device:TPU:1, one launch (start us, length us, event | category | flops | bytes accessed | tf_op | source)
XLA Modules:
  0.0 150.9 jit_solution(1708303056237930174)
XLA Ops:
  6.5 0.0 all-gather.2.cloned.1.call-start
  6.5 2.1 %pad_maximum_fusion = bf16[128,3072]{1,0:T(8,128)(2,1)} fusion(bf16[128,1024]{1,0:T(8,128)(2,1)} %param.12, bf16[128,2048]{1,0:T(8,128)(2,1)} %param.11), kind=kLoop, calls=%fused_computation.25 | loop fusion | flops 1572864 | bytes 1572864 | tf_op jit(solution)/shard_map/concatenate | solution.py:86
  8.6 0.0 all-gather.2.cloned.1.call-update
  8.6 1.5 copy.19
  10.1 2.2 %broadcast_in_dim.99 = bf16[4,256,2048]{1,2,0:T(8,128)(2,1)} broadcast(bf16[256,2048]{0,1:T(8,128)(2,1)S(1)} %copy.19), dimensions={1,2} | broadcast | bytes 5242880 | tf_op jit(solution)/shard_map/broadcast_in_dim | solution.py:64
  12.3 0.0 copy-start.4
  12.3 0.0 copy-start.5
  12.3 0.0 copy-start.3
  12.3 0.0 copy-start.2
  12.4 5.1 %all-to-all-start = ((bf16[4,256,2048]{1,2,0:T(8,128)(2,1)}), bf16[4,256,2048]{1,2,0:T(8,128)(2,1)}, u32[]{:S(2)}, u32[]{:S(2)}) async-start(bf16[4,256,2048]{1,2,0:T(8,128)(2,1)} %broadcast_in_dim.99), calls=%async_computation | async-start | bytes 8388608 | tf_op jit(solution)/shard_map/all_to_all | solution.py:65
  17.5 0.0 copy-done.4
  17.5 0.0 copy-done.5
  17.5 0.2 select_reduce_fusion.1
  17.7 0.1 eq.36
  17.8 0.0 copy-done.3
  17.8 0.1 iota_compare_fusion.2
  17.9 0.0 copy-done.2
  17.9 0.0 copy-start.1
  17.9 87.3 %all-gather.2.cloned.1.call-done = bf16[4096,3072]{1,0:T(8,128)(2,1)} async-done(((bf16[128,3072]{1,0:T(8,128)(2,1)}), bf16[4096,3072]{1,0:T(8,128)(2,1)}) %all-gather.2.cloned.1.call-update) | async-done | bytes 25165840 | tf_op jit(solution)/shard_map/all_gather | solution.py:87
  105.3 0.0 slice-start
  105.3 0.0 copy-done.1
  105.3 5.8 %slice-done = bf16[4096,2048]{1,0:T(8,128)(2,1)S(1)} async-done(((bf16[4096,3072]{1,0:T(8,128)(2,1)}), bf16[4096,2048]{1,0:T(8,128)(2,1)S(1)}, s32[]{:S(2)}) %slice-start) | async-done | bytes 16777240 | tf_op jit(solution)/shard_map/slice | solution.py:88
  111.0 4.8 %select_reduce_fusion = f32[64,256]{1,0:T(8,128)S(1)} fusion(pred[64,256]{1,0:T(8,128)(4,1)S(1)} %iota_compare_fusion, bf16[64,64,2048]{2,1,0:T(8,128)(2,1)S(1)} %bitcast.104, bf16[256,2048,1]{1,0,2:T(8,128)(2,1)S(1)} %bitcast.109), kind=kOutput, calls=%fused_computation.2 | convolution fusion | flops 4297048064 | bytes 17907712 | tf_op jit(solution)/shard_map/dot_general | solution.py:102
  115.9 0.0 all-to-all-done
  115.9 0.7 broadcast_in_dim.104
  116.6 4.0 %all-to-all-start.1 = ((f32[4,64,256]{2,1,0:T(8,128)}), f32[4,64,256]{2,1,0:T(8,128)S(1)}, u32[]{:S(2)}, u32[]{:S(2)}) async-start(f32[4,64,256]{2,1,0:T(8,128)} %broadcast_in_dim.104), calls=%async_computation.1 | async-start | bytes 524288 | tf_op jit(solution)/shard_map/all_to_all | solution.py:65
  120.6 9.6 %fusion.46 = f32[256,1024]{1,0:T(8,128)S(1)} fusion(bf16[256,8192]{0,1:T(8,128)(2,1)} %bitcast.2, bf16[8192,1024]{1,0:T(8,128)(2,1)} %param.10), kind=kOutput, calls=%fused_computation.50 | convolution fusion | flops 4294967296 | bytes 22020096 | tf_op jit(solution)/shard_map/dot_general | solution.py:94
  130.3 0.0 all-to-all-done.1
  130.3 0.1 broadcast_select_fusion
  130.4 0.0 copy-start
  130.5 5.9 %fusion.18 = bf16[256,1024]{1,0:T(8,128)(2,1)S(1)} fusion(f32[256,1024]{1,0:T(8,128)S(1)} %fusion.46, bf16[4096,256]{1,0:T(8,128)(2,1)S(1)} %bitcast.105, bf16[4096,3072]{1,0:T(8,128)(2,1)} %all-gather.2.cloned.1.call-done), kind=kOutput, calls=%fused_computation.15 | convolution fusion | flops 2148007936 | bytes 12058624 | tf_op jit(solution)/shard_map/dot_general | solution.py:112
  136.4 0.1 copy.31
  136.5 2.5 %fusion.45 = (f32[4,64,8]{2,0,1:T(4,128)S(1)}, f32[4,64,1,8,4]{3,4,0,1,2:T(4,128)S(1)}) fusion(bf16[4,1,64,128]{3,2,1,0:T(8,128)(2,1)S(1)} %get-tuple-element.8, pred[4,4]{1,0:T(4,128)(4,1)S(1)} %iota_compare_fusion.3, bf16[4,64,8,128]{3,2,1,0:T(8,128)(2,1)S(1)} %bitcast.106), kind=kOutput, calls=%fused_computation.49 | convolution fusion | flops 2119680 | bytes 630800 | tf_op jit(solution)/shard_map/trkgd,srkd->trkgs/dot_general | solution.py:36
  138.9 0.0 copy-done
  138.9 1.3 fusion.44
  140.3 0.7 fusion.29
  141.1 0.7 fusion.2
  141.8 0.5 fusion.36
  142.3 0.6 divide_convert_fusion
  143.0 0.1 convert_element_type.28
  143.1 1.0 copy.23
  (7 shorter events, 0.1 us)
Async XLA Ops:
  6.5 98.7 %all-gather.2.cloned.1.call-start = ((), (), s32[]{:S(2)}) async-start(), calls=%async_computation.2 | async-start | bytes 25952256 | tf_op jit(solution)/shard_map/all_gather | solution.py:87
  12.3 5.2 %copy-start.4 = (s32[64]{0:T(128)S(1)}, s32[64]{0:T(128)}, u32[]{:S(2)}) copy-start(s32[64]{0:T(128)} %param.17) | copy-start | bytes 772
  12.3 5.2 %copy-start.5 = (s32[64]{0:T(128)S(1)}, s32[64]{0:T(128)}, u32[]{:S(2)}) copy-start(s32[64]{0:T(128)} %param.16) | copy-start | bytes 772
  12.3 5.4 %copy-start.3 = (s32[64]{0:T(128)S(1)}, s32[64]{0:T(128)}, u32[]{:S(2)}) copy-start(s32[64]{0:T(128)} %param.15) | copy-start | bytes 772
  12.3 5.5 %copy-start.2 = (bf16[4,2,64,128]{3,2,1,0:T(8,128)(2,1)S(1)}, bf16[4,2,64,128]{3,2,1,0:T(8,128)(2,1)}, u32[]{:S(2)}) copy-start(bf16[4,2,64,128]{3,2,1,0:T(8,128)(2,1)} %param.14) | copy-start | bytes 393220
  12.4 103.5 %all-to-all-start = ((bf16[4,256,2048]{1,2,0:T(8,128)(2,1)}), bf16[4,256,2048]{1,2,0:T(8,128)(2,1)}, u32[]{:S(2)}, u32[]{:S(2)}) async-start(bf16[4,256,2048]{1,2,0:T(8,128)(2,1)} %broadcast_in_dim.99), calls=%async_computation | async-start | bytes 8388608 | tf_op jit(solution)/shard_map/all_to_all | solution.py:65
  17.9 87.3 %copy-start.1 = (bf16[4,64,2048]{2,1,0:T(8,128)(2,1)S(1)}, bf16[4,64,2048]{2,1,0:T(8,128)(2,1)}, u32[]{:S(2)}) copy-start(bf16[4,64,2048]{2,1,0:T(8,128)(2,1)} %param.9) | copy-start | bytes 3145732
  105.3 5.8 %slice-start = ((bf16[4096,3072]{1,0:T(8,128)(2,1)}), bf16[4096,2048]{1,0:T(8,128)(2,1)S(1)}, s32[]{:S(2)}) async-start(bf16[4096,3072]{1,0:T(8,128)(2,1)} %all-gather.2.cloned.1.call-done), calls=%async_computation.3 | async-start | bytes 33554432 | tf_op jit(solution)/shard_map/slice | solution.py:88
  116.6 13.7 %all-to-all-start.1 = ((f32[4,64,256]{2,1,0:T(8,128)}), f32[4,64,256]{2,1,0:T(8,128)S(1)}, u32[]{:S(2)}, u32[]{:S(2)}) async-start(f32[4,64,256]{2,1,0:T(8,128)} %broadcast_in_dim.104), calls=%async_computation.1 | async-start | bytes 524288 | tf_op jit(solution)/shard_map/all_to_all | solution.py:65
  130.4 8.5 %copy-start = (bf16[2,64,128,128]{3,2,1,0:T(8,128)(2,1)S(1)}, bf16[2,64,128,128]{3,2,1,0:T(8,128)(2,1)}, u32[]{:S(2)}) copy-start(bf16[2,64,128,128]{3,2,1,0:T(8,128)(2,1)} %param.13) | copy-start | bytes 12582916
Sparse Core Ops, SparseCore 0:
  9.6 95.6 all-gather.1

commit v10 on v9

--- a/solution.py
+++ b/solution.py
@@ -82,11 +82,13 @@
     n_tensor = query_projection_weight.shape[0] // part_width
     token_rows = normed_hidden_state.reshape(count_rows, part_width)
 
-    down_width = adapter_down_maps.shape[1]
-    both = jnp.concatenate([adapter_down_maps, adapter_up_maps], axis=1)
-    both_all = lax.all_gather(both, "dp", axis=0, tiled=True)
-    down_all = both_all[:, :down_width]
-    up_all = both_all[:, down_width:]
+    down_rows, down_width = adapter_down_maps.shape
+    up_rows = adapter_up_maps.size // down_width
+    both = jnp.concatenate([adapter_down_maps, adapter_up_maps.reshape(up_rows, down_width)], axis=0)
+    both_all = lax.all_gather(both, "dp", axis=0, tiled=False)
+    n_holders = both_all.shape[0]
+    down_all = both_all[:, :down_rows].reshape(n_holders * down_rows, down_width)
+    up_all = both_all[:, down_rows:].reshape(n_holders * down_rows, heads_width)
     n_pool = down_all.shape[0] // ADAPTER_RANK
 
     pieces = gather_tensor(token_rows, "tensor", n_tensor)

time: 151 us -> 176 us (1.17)
  local copies, waits for them, and re-layouts: 11.5 us -> 36.5 us
    reshape x0 -> x2, local copies, waits for them, and re-layouts: none -> 13.9 us  [the longest x1 12.9 us: per_device(): up_all = both_all[:, down_rows:].reshape(n_holders * down_rows, heads_width)]
    slice x2, local copies, waits for them, and re-layouts: 5.77 us -> 16.8 us  [the longest x1 8.57 us: per_device(): both_all[:, :down_rows].reshape(n_holders * down_rows, down_width)]
  transfers between devices with their start and end apart: 3 -> 3, of which waited for: 1 -> 1; matrix products, arithmetic and copies ran while one was open for 12% -> 28% of each run, Pallas kernels for 0% -> 0%
where the time goes in v10:
time: 176 us; the launch traced here: 175 us
  waiting for transfers between devices  86.5 us (49%)
  local copies, waits for them, and re-layouts  36.5 us (21%)
  matrix products  25.6 us (15%)
  between operations  13.6 us (8%)
  starting transfers between devices  9.15 us (5%)
  other arithmetic  3.73 us (2%)
    all_gather x1, waiting for transfers between devices, per_device(): both_all = lax.all_gather(both, 'dp', axis=0, tiled=False)  86.5 us
    reshape x1, local copies, waits for them, and re-layouts, per_device(): up_all = both_all[:, down_rows:].reshape(n_holders * down_rows, heads_width)  12.9 us
    dot_general x1, matrix products, per_device(): jnp.dot(full_rows, query_projection_weight, preferred_element_type=jnp.fl...  9.65 us
    all_to_all x2, starting transfers between devices, gather_tensor(): return lax.all_to_all(tiled, axis_name, 0, 0, tiled=True)  9.15 us
    slice x1, local copies, waits for them, and re-layouts, per_device(): both_all[:, :down_rows].reshape(n_holders * down_rows, down_width)  8.57 us
    slice x1, local copies, waits for them, and re-layouts, per_device(): up_all = both_all[:, down_rows:].reshape(n_holders * down_rows, heads_width)  8.26 us
    dot_general x1, matrix products, per_device(): lax.dot_general(wide_t.reshape(n_pool * ADAPTER_RANK, count_rows), up_all...  5.92 us
    dot_general x1, matrix products, per_device(): lax.dot_general(down_all, token_rows, (((1,), (1,)), ((), ())), preferred...  4.84 us
  transfers between devices with their start and end apart: 3, of which 1 were waited for; matrix products, arithmetic and copies ran while one was open for 28% of the time, Pallas kernels for 0%

profile of v10, /device:TPU:1, one launch (start us, length us, event | category | flops | bytes accessed | tf_op | source)
XLA Modules:
  0.0 175.0 jit_solution(17876831229118585618)
XLA Ops:
  6.5 0.0 all-gather.3.cloned.1.call-start
  6.5 1.0 reshape.158
  7.6 2.0 %pad_maximum_fusion = bf16[192,2048]{1,0:T(8,128)(2,1)} fusion(bf16[64,2048]{1,0:T(8,128)(2,1)S(1)} %reshape.158, bf16[128,2048]{1,0:T(8,128)(2,1)} %param.11), kind=kLoop, calls=%fused_computation.23 | loop fusion | flops 1572864 | bytes 1572864 | tf_op jit(solution)/shard_map/concatenate | solution.py:87
  9.6 0.0 all-gather.3.cloned.1.call-update
  9.6 1.5 copy.19
  11.1 2.2 %broadcast_in_dim.99 = bf16[4,256,2048]{1,2,0:T(8,128)(2,1)} broadcast(bf16[256,2048]{0,1:T(8,128)(2,1)S(1)} %copy.19), dimensions={1,2} | broadcast | bytes 5242880 | tf_op jit(solution)/shard_map/broadcast_in_dim | solution.py:64
  13.3 0.0 copy-start.4
  13.3 0.0 copy-start.5
  13.3 0.0 copy-start.3
  13.3 0.0 copy-start.2
  13.3 5.1 %all-to-all-start = ((bf16[4,256,2048]{1,2,0:T(8,128)(2,1)}), bf16[4,256,2048]{1,2,0:T(8,128)(2,1)}, u32[]{:S(2)}, u32[]{:S(2)}) async-start(bf16[4,256,2048]{1,2,0:T(8,128)(2,1)} %broadcast_in_dim.99), calls=%async_computation | async-start | bytes 8388608 | tf_op jit(solution)/shard_map/all_to_all | solution.py:65
  18.5 0.0 copy-done.4
  18.5 0.0 copy-done.5
  18.5 0.2 select_reduce_fusion.1
  18.7 0.1 eq.36
  18.8 0.0 copy-done.3
  18.8 0.1 iota_compare_fusion.2
  18.9 0.0 copy-done.2
  18.9 86.5 %all-gather.3.cloned.1.call-done = bf16[6144,2048]{1,0:T(8,128)(2,1)} async-done(((bf16[192,2048]{1,0:T(8,128)(2,1)}), bf16[6144,2048]{1,0:T(8,128)(2,1)}) %all-gather.3.cloned.1.call-update) | async-done | bytes 25165840 | tf_op jit(solution)/shard_map/all_gather | solution.py:88
  105.4 0.0 copy-start.1
  105.4 8.6 %slice.40 = bf16[32,128,2048]{2,1,0:T(8,128)(2,1)S(1)} slice(bf16[32,192,2048]{2,1,0:T(8,128)(2,1)} %bitcast.106), slice={[0:32], [0:128], [0:2048]} | slice | bytes 33554432 | tf_op jit(solution)/shard_map/slice | solution.py:90
  114.0 0.0 copy-done.1
  114.0 4.8 %select_reduce_fusion = f32[64,256]{1,0:T(8,128)S(1)} fusion(pred[64,256]{1,0:T(8,128)(4,1)S(1)} %iota_compare_fusion, bf16[64,64,2048]{2,1,0:T(8,128)(2,1)S(1)} %bitcast.108, bf16[256,2048,1]{1,0,2:T(8,128)(2,1)S(1)} %bitcast.114), kind=kOutput, calls=%fused_computation | convolution fusion | flops 4297048064 | bytes 17907712 | tf_op jit(solution)/shard_map/dot_general | solution.py:104
  118.8 0.0 all-to-all-done
  118.9 0.7 broadcast_in_dim.104
  119.6 4.0 %all-to-all-start.1 = ((f32[4,64,256]{2,1,0:T(8,128)}), f32[4,64,256]{2,1,0:T(8,128)S(1)}, u32[]{:S(2)}, u32[]{:S(2)}) async-start(f32[4,64,256]{2,1,0:T(8,128)} %broadcast_in_dim.104), calls=%async_computation.1 | async-start | bytes 524288 | tf_op jit(solution)/shard_map/all_to_all | solution.py:65
  123.6 9.7 %fusion.39 = f32[256,1024]{1,0:T(8,128)S(1)} fusion(bf16[256,8192]{0,1:T(8,128)(2,1)} %bitcast.2, bf16[8192,1024]{1,0:T(8,128)(2,1)} %param.10), kind=kOutput, calls=%fused_computation.48 | convolution fusion | flops 4294967296 | bytes 22020096 | tf_op jit(solution)/shard_map/dot_general | solution.py:96
  133.2 8.3 %slice.45 = bf16[32,64,2048]{2,1,0:T(8,128)(2,1)} slice(bf16[32,192,2048]{2,1,0:T(8,128)(2,1)} %bitcast.107), slice={[0:32], [128:192], [0:2048]} | slice | bytes 16777216 | tf_op jit(solution)/shard_map/slice | solution.py:91
  141.5 12.9 %reshape.159 = bf16[4096,1024]{1,0:T(8,128)(2,1)} reshape(bf16[32,64,2048]{2,1,0:T(8,128)(2,1)} %slice.45) | data formatting | bytes 16777216 | tf_op jit(solution)/shard_map/reshape | solution.py:91
  154.4 0.0 all-to-all-done.1
  154.4 0.1 broadcast_select_fusion
  154.6 0.0 copy-start
  154.6 5.9 %fusion.13 = bf16[256,1024]{1,0:T(8,128)(2,1)S(1)} fusion(f32[256,1024]{1,0:T(8,128)S(1)} %fusion.39, bf16[4096,256]{1,0:T(8,128)(2,1)S(1)} %bitcast.109, bf16[4096,1024]{1,0:T(8,128)(2,1)} %reshape.159), kind=kOutput, calls=%fused_computation.13 | convolution fusion | flops 2148007936 | bytes 12058624 | tf_op jit(solution)/shard_map/dot_general | solution.py:114
  160.5 0.1 copy.31
  160.6 2.5 %fusion.38 = (f32[4,64,8]{2,0,1:T(4,128)S(1)}, f32[4,64,1,8,4]{3,4,0,1,2:T(4,128)S(1)}) fusion(bf16[4,1,64,128]{3,2,1,0:T(8,128)(2,1)S(1)} %get-tuple-element.8, pred[4,4]{1,0:T(4,128)(4,1)S(1)} %iota_compare_fusion.3, bf16[4,64,8,128]{3,2,1,0:T(8,128)(2,1)S(1)} %bitcast.111), kind=kOutput, calls=%fused_computation.47 | convolution fusion | flops 2119680 | bytes 630800 | tf_op jit(solution)/shard_map/trkgd,srkd->trkgs/dot_general | solution.py:36
  163.1 0.0 copy-done
  163.1 1.3 fusion.37
  164.5 0.7 fusion.22
  165.2 0.7 fusion
  166.0 0.5 fusion.29
  166.5 0.6 divide_convert_fusion
  167.1 0.1 convert_element_type.28
  167.2 1.0 copy.23
  (7 shorter events, 0.1 us)
Async XLA Ops:
  6.5 98.9 %all-gather.3.cloned.1.call-start = ((), (), s32[]{:S(2)}) async-start(), calls=%async_computation.2 | async-start | bytes 25952256 | tf_op jit(solution)/shard_map/all_gather | solution.py:88
  13.3 5.2 %copy-start.4 = (s32[64]{0:T(128)S(1)}, s32[64]{0:T(128)}, u32[]{:S(2)}) copy-start(s32[64]{0:T(128)} %param.17) | copy-start | bytes 772
  13.3 5.2 %copy-start.5 = (s32[64]{0:T(128)S(1)}, s32[64]{0:T(128)}, u32[]{:S(2)}) copy-start(s32[64]{0:T(128)} %param.16) | copy-start | bytes 772
  13.3 5.4 %copy-start.3 = (s32[64]{0:T(128)S(1)}, s32[64]{0:T(128)}, u32[]{:S(2)}) copy-start(s32[64]{0:T(128)} %param.15) | copy-start | bytes 772
  13.3 5.5 %copy-start.2 = (bf16[4,2,64,128]{3,2,1,0:T(8,128)(2,1)S(1)}, bf16[4,2,64,128]{3,2,1,0:T(8,128)(2,1)}, u32[]{:S(2)}) copy-start(bf16[4,2,64,128]{3,2,1,0:T(8,128)(2,1)} %param.14) | copy-start | bytes 393220
  13.3 105.5 %all-to-all-start = ((bf16[4,256,2048]{1,2,0:T(8,128)(2,1)}), bf16[4,256,2048]{1,2,0:T(8,128)(2,1)}, u32[]{:S(2)}, u32[]{:S(2)}) async-start(bf16[4,256,2048]{1,2,0:T(8,128)(2,1)} %broadcast_in_dim.99), calls=%async_computation | async-start | bytes 8388608 | tf_op jit(solution)/shard_map/all_to_all | solution.py:65
  105.4 8.6 %copy-start.1 = (bf16[4,64,2048]{2,1,0:T(8,128)(2,1)S(1)}, bf16[4,64,2048]{2,1,0:T(8,128)(2,1)}, u32[]{:S(2)}) copy-start(bf16[4,64,2048]{2,1,0:T(8,128)(2,1)} %param.9) | copy-start | bytes 3145732
  119.6 34.8 %all-to-all-start.1 = ((f32[4,64,256]{2,1,0:T(8,128)}), f32[4,64,256]{2,1,0:T(8,128)S(1)}, u32[]{:S(2)}, u32[]{:S(2)}) async-start(f32[4,64,256]{2,1,0:T(8,128)} %broadcast_in_dim.104), calls=%async_computation.1 | async-start | bytes 524288 | tf_op jit(solution)/shard_map/all_to_all | solution.py:65
  154.6 8.5 %copy-start = (bf16[2,64,128,128]{3,2,1,0:T(8,128)(2,1)S(1)}, bf16[2,64,128,128]{3,2,1,0:T(8,128)(2,1)}, u32[]{:S(2)}) copy-start(bf16[2,64,128,128]{3,2,1,0:T(8,128)(2,1)} %param.13) | copy-start | bytes 12582916
Sparse Core Ops, SparseCore 0:
  9.7 95.6 all-gather.2

commit v11 on v9

--- a/solution.py
+++ b/solution.py
@@ -116,8 +116,8 @@
         preferred_element_type=jnp.float32,
     )
     query = (base + delta).reshape(steps, requests, heads_width).astype(jnp.bfloat16)
-    query, lengths_all = lax.optimization_barrier((query, lengths_all))
-    return attend(query, key_value_cache, step_key_value, cache_valid_length)
+    lengths_mine = lax.dynamic_slice_in_dim(lengths_all, lax.axis_index("dp") * requests, requests)
+    return attend(query, key_value_cache, step_key_value, lengths_mine)
 
 
 def solution(mesh):

time: 151 us -> 148 us (0.980)
  waiting for transfers between devices: 87.4 us -> 63.9 us
  blocking collectives: 0 us -> 18 us
    all_gather x1, waiting for transfers between devices: 87.3 us -> 10.7 us  [per_device(): both_all = lax.all_gather(both, 'dp', axis=0, tiled=True)]
    all_to_all x2, waiting for transfers between devices: 0.01 us -> 53.2 us  [gather_tensor(): return lax.all_to_all(tiled, axis_name, 0, 0, tiled=True)]
    unnamed x0 -> x1, blocking collectives: none -> 18 us
  transfers between devices with their start and end apart: 3 -> 3, of which waited for: 1 -> 3; matrix products, arithmetic and copies ran while one was open for 12% -> 10% of each run, Pallas kernels for 0% -> 0%
where the time goes in v11:
time: 148 us; the launch traced here: 147 us
  waiting for transfers between devices  63.9 us (43%)
  matrix products  25.8 us (17%)
  blocking collectives  18 us (12%)
  between operations  14.2 us (10%)
  local copies, waits for them, and re-layouts  12.4 us (8%)
  starting transfers between devices  9.15 us (6%)
  other arithmetic  3.81 us (3%)
    all_to_all x2, waiting for transfers between devices, gather_tensor(): return lax.all_to_all(tiled, axis_name, 0, 0, tiled=True)  53.2 us
    unnamed x1, blocking collectives  18 us
    all_gather x1, waiting for transfers between devices, per_device(): both_all = lax.all_gather(both, 'dp', axis=0, tiled=True)  10.7 us
    dot_general x1, matrix products, per_device(): jnp.dot(full_rows, query_projection_weight, preferred_element_type=jnp.fl...  9.9 us
    all_to_all x2, starting transfers between devices, gather_tensor(): return lax.all_to_all(tiled, axis_name, 0, 0, tiled=True)  9.15 us
    dot_general x1, matrix products, per_device(): lax.dot_general(wide_t.reshape(n_pool * ADAPTER_RANK, count_rows), up_all...  5.89 us
    slice x2, local copies, waits for them, and re-layouts, per_device(): down_all = both_all[:, :down_width]  5.77 us
    dot_general x1, matrix products, per_device(): lax.dot_general(down_all, token_rows, (((1,), (1,)), ((), ())), preferred...  4.83 us
  transfers between devices with their start and end apart: 3, of which 3 were waited for; matrix products, arithmetic and copies ran while one was open for 10% of the time, Pallas kernels for 0%

profile of v11, /device:TPU:1, one launch (start us, length us, event | category | flops | bytes accessed | tf_op | source)
XLA Modules:
  0.0 147.3 jit_solution(15333648576705786548)
XLA Ops:
  6.5 0.0 all-gather.2.cloned.1.call-start
  6.5 2.1 %pad_maximum_fusion = bf16[128,3072]{1,0:T(8,128)(2,1)} fusion(bf16[128,1024]{1,0:T(8,128)(2,1)} %param.12, bf16[128,2048]{1,0:T(8,128)(2,1)} %param.11), kind=kLoop, calls=%fused_computation.26 | loop fusion | flops 1572864 | bytes 1572864 | tf_op jit(solution)/shard_map/concatenate | solution.py:86
  8.6 0.0 all-gather.2.cloned.1.call-update
  8.6 1.5 %copy.21 = bf16[256,2048]{0,1:T(8,128)(2,1)S(1)} copy(bf16[256,2048]{1,0:T(8,128)(2,1)} %bitcast.108) | data formatting | bytes 2097152 | tf_op jit(solution)/shard_map/broadcast_in_dim | solution.py:64
  10.1 2.2 %broadcast_in_dim.98 = bf16[4,256,2048]{1,2,0:T(8,128)(2,1)} broadcast(bf16[256,2048]{0,1:T(8,128)(2,1)S(1)} %copy.21), dimensions={1,2} | broadcast | bytes 5242880 | tf_op jit(solution)/shard_map/broadcast_in_dim | solution.py:64
  12.3 0.0 copy-start.3
  12.4 0.0 copy-start.4
  12.4 0.0 copy-start.6
  12.4 0.0 copy-start.2
  12.4 5.1 %all-to-all-start = ((bf16[4,256,2048]{1,2,0:T(8,128)(2,1)}), bf16[4,256,2048]{1,2,0:T(8,128)(2,1)}, u32[]{:S(2)}, u32[]{:S(2)}) async-start(bf16[4,256,2048]{1,2,0:T(8,128)(2,1)} %broadcast_in_dim.98), calls=%async_computation | async-start | bytes 8388608 | tf_op jit(solution)/shard_map/all_to_all | solution.py:65
  17.5 0.0 copy-done.3
  17.5 0.0 copy-done.4
  17.5 0.2 select_reduce_fusion.1
  17.7 0.1 eq.36
  17.8 0.0 copy-done.6
  17.8 0.6 dynamic-slice
  19.1 0.0 copy-done.2
  19.1 47.3 %all-to-all-done = bf16[4,256,2048]{1,2,0:T(8,128)(2,1)} async-done(((bf16[4,256,2048]{1,2,0:T(8,128)(2,1)}), bf16[4,256,2048]{1,2,0:T(8,128)(2,1)}, u32[]{:S(2)}, u32[]{:S(2)}) %all-to-all-start) | async-done | bytes 4194336 | tf_op jit(solution)/shard_map/all_to_all | solution.py:65
  66.4 0.0 copy-start.5
  66.4 9.9 %fusion.49 = f32[256,1024]{1,0:T(8,128)S(1)} fusion(bf16[256,8192]{0,1:T(8,128)(2,1)} %bitcast.2, bf16[8192,1024]{1,0:T(8,128)(2,1)} %param.10), kind=kOutput, calls=%fused_computation.51 | convolution fusion | flops 4294967296 | bytes 22020096 | tf_op jit(solution)/shard_map/dot_general | solution.py:94
  76.3 0.0 copy-done.5
  76.3 0.3 dynamic-update-slice
  76.6 18.0 %all-reduce = s32[2048]{0:T(1024)S(1)} all-reduce(s32[2048]{0:T(1024)S(1)} %dynamic-update-slice), channel_id=1, replica_groups=mesh['dp'=32,'tensor'=4] {'dp'}, use_global_device_ids=true, to_apply=%add | all-reduce | flops 2048 | bytes 16384
  94.6 0.1 dynamic_slice.3
  94.7 0.0 copy-start.1
  94.7 10.7 %all-gather.2.cloned.1.call-done = bf16[4096,3072]{1,0:T(8,128)(2,1)} async-done(((bf16[128,3072]{1,0:T(8,128)(2,1)}), bf16[4096,3072]{1,0:T(8,128)(2,1)}) %all-gather.2.cloned.1.call-update) | async-done | bytes 25165840 | tf_op jit(solution)/shard_map/all_gather | solution.py:87
  105.4 0.0 slice-start
  105.4 0.0 copy-done.1
  105.4 5.8 %slice-done = bf16[4096,2048]{1,0:T(8,128)(2,1)S(1)} async-done(((bf16[4096,3072]{1,0:T(8,128)(2,1)}), bf16[4096,2048]{1,0:T(8,128)(2,1)S(1)}, s32[]{:S(2)}) %slice-start) | async-done | bytes 16777240 | tf_op jit(solution)/shard_map/slice | solution.py:88
  111.2 4.8 %select_reduce_fusion = f32[64,256]{1,0:T(8,128)S(1)} fusion(pred[64,256]{1,0:T(8,128)(4,1)S(1)} %iota_compare_fusion, bf16[64,64,2048]{2,1,0:T(8,128)(2,1)S(1)} %bitcast.104, bf16[256,2048,1]{1,0,2:T(8,128)(2,1)S(1)} %bitcast.109), kind=kOutput, calls=%fused_computation.2 | convolution fusion | flops 4297048064 | bytes 17907712 | tf_op jit(solution)/shard_map/dot_general | solution.py:102
  116.0 0.7 broadcast_in_dim.104
  116.8 4.0 %all-to-all-start.1 = ((f32[4,64,256]{2,1,0:T(8,128)}), f32[4,64,256]{2,1,0:T(8,128)S(1)}, u32[]{:S(2)}, u32[]{:S(2)}) async-start(f32[4,64,256]{2,1,0:T(8,128)} %broadcast_in_dim.104), calls=%async_computation.1 | async-start | bytes 524288 | tf_op jit(solution)/shard_map/all_to_all | solution.py:65
  120.8 0.1 iota_compare_fusion.2
  120.8 5.9 %all-to-all-done.1 = f32[4,64,256]{2,1,0:T(8,128)S(1)} async-done(((f32[4,64,256]{2,1,0:T(8,128)}), f32[4,64,256]{2,1,0:T(8,128)S(1)}, u32[]{:S(2)}, u32[]{:S(2)}) %all-to-all-start.1) | async-done | bytes 262176 | tf_op jit(solution)/shard_map/all_to_all | solution.py:65
  126.7 0.1 broadcast_select_fusion
  126.9 0.0 copy-start
  126.9 5.9 %fusion.28 = bf16[32,8,8,128]{3,1,2,0:T(8,128)(2,1)S(1)} fusion(f32[256,1024]{1,0:T(8,128)S(1)} %fusion.49, bf16[4096,256]{1,0:T(8,128)(2,1)S(1)} %bitcast.105, bf16[4096,3072]{1,0:T(8,128)(2,1)} %all-gather.2.cloned.1.call-done), kind=kOutput, calls=%fused_computation.20 | convolution fusion | flops 2148007936 | bytes 12058624 | tf_op jit(solution)/shard_map/dot_general | solution.py:112
  132.8 0.1 copy.33
  132.9 0.0 copy-done
  132.9 1.3 fusion.47
  134.3 2.5 %fusion.48 = (f32[4,64,8]{2,0,1:T(4,128)S(1)}, f32[4,64,1,8,4]{3,4,0,1,2:T(4,128)S(1)}) fusion(bf16[4,1,64,128]{3,2,1,0:T(8,128)(2,1)S(1)} %get-tuple-element.10, pred[4,4]{1,0:T(4,128)(4,1)S(1)} %iota_compare_fusion.3, bf16[4,64,8,128]{3,2,1,0:T(8,128)(2,1)S(1)} %bitcast.107), kind=kOutput, calls=%fused_computation.50 | convolution fusion | flops 2119680 | bytes 630800 | tf_op jit(solution)/shard_map/trkgd,srkd->trkgs/dot_general | solution.py:36
  136.8 0.7 fusion.2
  137.5 0.7 fusion.32
  138.3 0.5 fusion.39
  138.8 0.6 divide_convert_fusion
  139.4 0.1 convert_element_type.31
  139.5 1.0 copy.26
  (8 shorter events, 0.1 us)
Async XLA Ops:
  6.5 98.9 %all-gather.2.cloned.1.call-start = ((), (), s32[]{:S(2)}) async-start(), calls=%async_computation.2 | async-start | bytes 25952256 | tf_op jit(solution)/shard_map/all_gather | solution.py:87
  12.3 5.2 %copy-start.3 = (s32[64]{0:T(128)S(1)}, s32[64]{0:T(128)}, u32[]{:S(2)}) copy-start(s32[64]{0:T(128)} %param.17) | copy-start | bytes 772
  12.4 5.2 %copy-start.4 = (s32[64]{0:T(128)S(1)}, s32[64]{0:T(128)}, u32[]{:S(2)}) copy-start(s32[64]{0:T(128)} %param.16) | copy-start | bytes 772
  12.4 5.4 %copy-start.6 = (u32[128]{0:T(128)S(1)}, u32[128]{0:T(128)}, u32[]{:S(2)}) copy-start(u32[128]{0:T(128)} %constant.25) | copy-start | bytes 1540
  12.4 6.7 %copy-start.2 = (bf16[4,2,64,128]{3,2,1,0:T(8,128)(2,1)S(1)}, bf16[4,2,64,128]{3,2,1,0:T(8,128)(2,1)}, u32[]{:S(2)}) copy-start(bf16[4,2,64,128]{3,2,1,0:T(8,128)(2,1)} %param.14) | copy-start | bytes 393220
  12.4 54.0 %all-to-all-start = ((bf16[4,256,2048]{1,2,0:T(8,128)(2,1)}), bf16[4,256,2048]{1,2,0:T(8,128)(2,1)}, u32[]{:S(2)}, u32[]{:S(2)}) async-start(bf16[4,256,2048]{1,2,0:T(8,128)(2,1)} %broadcast_in_dim.98), calls=%async_computation | async-start | bytes 8388608 | tf_op jit(solution)/shard_map/all_to_all | solution.py:65
  66.4 9.9 %copy-start.5 = (s32[64]{0:T(128)S(1)}, s32[64]{0:T(128)}, u32[]{:S(2)}) copy-start(s32[64]{0:T(128)} %param.15) | copy-start | bytes 772
  94.7 10.7 %copy-start.1 = (bf16[4,64,2048]{2,1,0:T(8,128)(2,1)S(1)}, bf16[4,64,2048]{2,1,0:T(8,128)(2,1)}, u32[]{:S(2)}) copy-start(bf16[4,64,2048]{2,1,0:T(8,128)(2,1)} %param.9) | copy-start | bytes 3145732
  105.4 5.8 %slice-start = ((bf16[4096,3072]{1,0:T(8,128)(2,1)}), bf16[4096,2048]{1,0:T(8,128)(2,1)S(1)}, s32[]{:S(2)}) async-start(bf16[4096,3072]{1,0:T(8,128)(2,1)} %all-gather.2.cloned.1.call-done), calls=%async_computation.3 | async-start | bytes 33554432 | tf_op jit(solution)/shard_map/slice | solution.py:88
  116.8 9.9 %all-to-all-start.1 = ((f32[4,64,256]{2,1,0:T(8,128)}), f32[4,64,256]{2,1,0:T(8,128)S(1)}, u32[]{:S(2)}, u32[]{:S(2)}) async-start(f32[4,64,256]{2,1,0:T(8,128)} %broadcast_in_dim.104), calls=%async_computation.1 | async-start | bytes 524288 | tf_op jit(solution)/shard_map/all_to_all | solution.py:65
  126.9 6.0 %copy-start = (bf16[2,64,128,128]{3,2,1,0:T(8,128)(2,1)S(1)}, bf16[2,64,128,128]{3,2,1,0:T(8,128)(2,1)}, u32[]{:S(2)}) copy-start(bf16[2,64,128,128]{3,2,1,0:T(8,128)(2,1)} %param.13) | copy-start | bytes 12582916
Sparse Core Ops, SparseCore 0:
  9.6 95.8 all-gather.1

commit v12 on v11

--- a/solution.py
+++ b/solution.py
@@ -99,8 +99,9 @@
     position = pool_lookup(adapter_per_request, adapter_pool_position)
     row_position = jnp.tile(position, steps)
     pick = jnp.arange(n_pool, dtype=jnp.int32)[:, None] == row_position[None, :]
+    padded_rows = jnp.pad(token_rows, ((0, 0), (0, both_all.shape[1] - down_width)))
     full_t = lax.dot_general(
-        down_all, token_rows, (((1,), (1,)), ((), ())), preferred_element_type=jnp.float32
+        both_all, padded_rows, (((1,), (1,)), ((), ())), preferred_element_type=jnp.float32
     ).reshape(n_pool, ADAPTER_RANK, count_rows)
     shrink_local = jnp.sum(jnp.where(pick[:, None, :], full_t, 0.0), axis=0)
     partials = gather_tensor(shrink_local, "tensor", n_tensor)

time: 148 us -> 150 us (1.014)
  matrix products: 25.8 us -> 33.1 us
  local copies, waits for them, and re-layouts: 12.4 us -> 6.67 us
    dot_general x1, matrix products: 4.83 us -> 12.1 us  [per_device(): lax.dot_general(both_all, padded_rows, (((1,), (1,)), ((), ())), preferre...]
    slice x2 -> x0, local copies, waits for them, and re-layouts: 5.77 us -> none  [per_device(): down_all = both_all[:, :down_width]]
where the time goes in v12:
time: 150 us
  waiting for transfers between devices  63.8 us (43%)
  matrix products  33.1 us (22%)
  blocking collectives  18 us (12%)
  between operations  14.2 us (9%)
  starting transfers between devices  9.15 us (6%)
  local copies, waits for them, and re-layouts  6.67 us (4%)
  other arithmetic  4.49 us (3%)
    all_to_all x2, waiting for transfers between devices, gather_tensor(): return lax.all_to_all(tiled, axis_name, 0, 0, tiled=True)  53.2 us
    unnamed x1, blocking collectives  18 us
    dot_general x1, matrix products, per_device(): lax.dot_general(both_all, padded_rows, (((1,), (1,)), ((), ())), preferre...  12.1 us
    all_gather x1, waiting for transfers between devices, per_device(): both_all = lax.all_gather(both, 'dp', axis=0, tiled=True)  10.6 us
    dot_general x1, matrix products, per_device(): jnp.dot(full_rows, query_projection_weight, preferred_element_type=jnp.fl...  9.97 us
    all_to_all x2, starting transfers between devices, gather_tensor(): return lax.all_to_all(tiled, axis_name, 0, 0, tiled=True)  9.15 us
    dot_general x1, matrix products, per_device(): lax.dot_general(wide_t.reshape(n_pool * ADAPTER_RANK, count_rows), up_all...  5.9 us
    broadcast_in_dim x3, local copies, waits for them, and re-layouts, gather_tensor(): tiled = jnp.broadcast_to(value[None], (count,) + value.shape)  4.42 us
  transfers between devices with their start and end apart: 3, of which 3 were waited for; matrix products, arithmetic and copies ran while one was open for 10% of the time, Pallas kernels for 0%

profile of v12, /device:TPU:1, one launch (start us, length us, event | category | flops | bytes accessed | tf_op | source)
XLA Modules:
  0.0 149.5 jit_solution(3311633018892228487)
XLA Ops:
  6.5 0.0 all-gather.2.cloned.1.call-start
  6.5 2.1 %pad_maximum_fusion = bf16[128,3072]{1,0:T(8,128)(2,1)} fusion(bf16[128,1024]{1,0:T(8,128)(2,1)} %param.12, bf16[128,2048]{1,0:T(8,128)(2,1)} %param.11), kind=kLoop, calls=%fused_computation.28 | loop fusion | flops 1572864 | bytes 1572864 | tf_op jit(solution)/shard_map/concatenate | solution.py:86
  8.6 0.0 all-gather.2.cloned.1.call-update
  8.6 1.5 copy.21
  10.1 2.2 %broadcast_in_dim.98 = bf16[4,256,2048]{1,2,0:T(8,128)(2,1)} broadcast(bf16[256,2048]{0,1:T(8,128)(2,1)S(1)} %copy.21), dimensions={1,2} | broadcast | bytes 5242880 | tf_op jit(solution)/shard_map/broadcast_in_dim | solution.py:64
  12.3 0.0 copy-start.3
  12.4 0.0 copy-start.4
  12.4 0.0 copy-start.6
  12.4 0.0 copy-start.2
  12.4 5.1 %all-to-all-start = ((bf16[4,256,2048]{1,2,0:T(8,128)(2,1)}), bf16[4,256,2048]{1,2,0:T(8,128)(2,1)}, u32[]{:S(2)}, u32[]{:S(2)}) async-start(bf16[4,256,2048]{1,2,0:T(8,128)(2,1)} %broadcast_in_dim.98), calls=%async_computation | async-start | bytes 8388608 | tf_op jit(solution)/shard_map/all_to_all | solution.py:65
  17.5 0.0 copy-done.3
  17.5 0.0 copy-done.4
  17.5 0.2 select_reduce_fusion.1
  17.7 0.1 eq.36
  17.8 0.0 copy-done.6
  17.8 0.6 dynamic-slice
  19.1 0.0 copy-done.2
  19.1 47.3 %all-to-all-done = bf16[4,256,2048]{1,2,0:T(8,128)(2,1)} async-done(((bf16[4,256,2048]{1,2,0:T(8,128)(2,1)}), bf16[4,256,2048]{1,2,0:T(8,128)(2,1)}, u32[]{:S(2)}, u32[]{:S(2)}) %all-to-all-start) | async-done | bytes 4194336 | tf_op jit(solution)/shard_map/all_to_all | solution.py:65
  66.4 0.0 copy-start.5
  66.4 0.0 copy-start.1
  66.4 10.0 %fusion.52 = f32[256,1024]{1,0:T(8,128)S(1)} fusion(bf16[256,8192]{0,1:T(8,128)(2,1)} %bitcast.2, bf16[8192,1024]{1,0:T(8,128)(2,1)} %param.10), kind=kOutput, calls=%fused_computation.54 | convolution fusion | flops 4294967296 | bytes 22020096 | tf_op jit(solution)/shard_map/dot_general | solution.py:94
  76.4 0.0 copy-done.5
  76.4 0.3 dynamic-update-slice
  76.7 18.0 %all-reduce.1 = s32[2048]{0:T(1024)S(1)} all-reduce(s32[2048]{0:T(1024)S(1)} %dynamic-update-slice), channel_id=1, replica_groups=mesh['dp'=32,'tensor'=4] {'dp'}, use_global_device_ids=true, to_apply=%add.1 | all-reduce | flops 2048 | bytes 16384
  94.7 0.1 dynamic_slice.3
  94.8 10.6 %all-gather.2.cloned.1.call-done = bf16[4096,3072]{1,0:T(8,128)(2,1)} async-done(((bf16[128,3072]{1,0:T(8,128)(2,1)}), bf16[4096,3072]{1,0:T(8,128)(2,1)}) %all-gather.2.cloned.1.call-update) | async-done | bytes 25165840 | tf_op jit(solution)/shard_map/all_gather | solution.py:87
  105.4 0.0 copy-done.1
  105.4 12.1 %fusion.8 = f32[4096,256]{1,0:T(8,128)S(1)} fusion(bf16[4096,3072]{1,0:T(8,128)(2,1)} %all-gather.2.cloned.1.call-done, bf16[256,2048]{1,0:T(8,128)(2,1)S(1)} %bitcast.106), kind=kOutput, calls=%fused_computation.10 | convolution fusion | flops 6442450944 | bytes 30408704 | tf_op jit(solution)/shard_map/dot_general | solution.py:103
  117.5 0.7 select_reduce_fusion
  118.2 0.7 broadcast_in_dim.104
  119.0 4.0 %all-to-all-start.1 = ((f32[4,64,256]{2,1,0:T(8,128)}), f32[4,64,256]{2,1,0:T(8,128)S(1)}, u32[]{:S(2)}, u32[]{:S(2)}) async-start(f32[4,64,256]{2,1,0:T(8,128)} %broadcast_in_dim.104), calls=%async_computation.1 | async-start | bytes 524288 | tf_op jit(solution)/shard_map/all_to_all | solution.py:65
  123.0 0.1 iota_compare_fusion.2
  123.0 5.9 %all-to-all-done.1 = f32[4,64,256]{2,1,0:T(8,128)S(1)} async-done(((f32[4,64,256]{2,1,0:T(8,128)}), f32[4,64,256]{2,1,0:T(8,128)S(1)}, u32[]{:S(2)}, u32[]{:S(2)}) %all-to-all-start.1) | async-done | bytes 262176 | tf_op jit(solution)/shard_map/all_to_all | solution.py:65
  128.9 0.1 broadcast_select_fusion
  129.1 0.0 copy-start
  129.1 5.9 %fusion.30 = bf16[32,8,8,128]{3,1,2,0:T(8,128)(2,1)S(1)} fusion(f32[256,1024]{1,0:T(8,128)S(1)} %fusion.52, bf16[4096,256]{1,0:T(8,128)(2,1)S(1)} %bitcast.102, bf16[4096,3072]{1,0:T(8,128)(2,1)} %all-gather.2.cloned.1.call-done), kind=kOutput, calls=%fused_computation.22 | convolution fusion | flops 2148007936 | bytes 12058624 | tf_op jit(solution)/shard_map/dot_general | solution.py:113
  135.0 0.1 copy.33
  135.1 0.0 copy-done
  135.1 1.3 fusion.50
  136.5 2.5 %fusion.51 = (f32[4,64,8]{2,0,1:T(4,128)S(1)}, f32[4,64,1,8,4]{3,4,0,1,2:T(4,128)S(1)}) fusion(bf16[4,1,64,128]{3,2,1,0:T(8,128)(2,1)S(1)} %get-tuple-element.10, pred[4,4]{1,0:T(4,128)(4,1)S(1)} %iota_compare_fusion.3, bf16[4,64,8,128]{3,2,1,0:T(8,128)(2,1)S(1)} %bitcast.104), kind=kOutput, calls=%fused_computation.53 | convolution fusion | flops 2119680 | bytes 630800 | tf_op jit(solution)/shard_map/trkgd,srkd->trkgs/dot_general | solution.py:36
  139.0 0.7 fusion.2
  139.7 0.7 fusion.34
  140.4 0.5 fusion.41
  141.0 0.6 divide_convert_fusion
  141.6 0.1 convert_element_type.33
  141.7 1.0 copy.26
  (8 shorter events, 0.1 us)
Async XLA Ops:
  6.5 98.9 %all-gather.2.cloned.1.call-start = ((), (), s32[]{:S(2)}) async-start(), calls=%async_computation.2 | async-start | bytes 25952256 | tf_op jit(solution)/shard_map/all_gather | solution.py:87
  12.3 5.2 %copy-start.3 = (s32[64]{0:T(128)S(1)}, s32[64]{0:T(128)}, u32[]{:S(2)}) copy-start(s32[64]{0:T(128)} %param.17) | copy-start | bytes 772
  12.4 5.2 %copy-start.4 = (s32[64]{0:T(128)S(1)}, s32[64]{0:T(128)}, u32[]{:S(2)}) copy-start(s32[64]{0:T(128)} %param.16) | copy-start | bytes 772
  12.4 5.4 %copy-start.6 = (u32[128]{0:T(128)S(1)}, u32[128]{0:T(128)}, u32[]{:S(2)}) copy-start(u32[128]{0:T(128)} %constant.28) | copy-start | bytes 1540
  12.4 6.7 %copy-start.2 = (bf16[4,2,64,128]{3,2,1,0:T(8,128)(2,1)S(1)}, bf16[4,2,64,128]{3,2,1,0:T(8,128)(2,1)}, u32[]{:S(2)}) copy-start(bf16[4,2,64,128]{3,2,1,0:T(8,128)(2,1)} %param.14) | copy-start | bytes 393220
  12.4 54.0 %all-to-all-start = ((bf16[4,256,2048]{1,2,0:T(8,128)(2,1)}), bf16[4,256,2048]{1,2,0:T(8,128)(2,1)}, u32[]{:S(2)}, u32[]{:S(2)}) async-start(bf16[4,256,2048]{1,2,0:T(8,128)(2,1)} %broadcast_in_dim.98), calls=%async_computation | async-start | bytes 8388608 | tf_op jit(solution)/shard_map/all_to_all | solution.py:65
  66.4 10.0 %copy-start.5 = (s32[64]{0:T(128)S(1)}, s32[64]{0:T(128)}, u32[]{:S(2)}) copy-start(s32[64]{0:T(128)} %param.15) | copy-start | bytes 772
  66.4 39.1 %copy-start.1 = (bf16[4,64,2048]{2,1,0:T(8,128)(2,1)S(1)}, bf16[4,64,2048]{2,1,0:T(8,128)(2,1)}, u32[]{:S(2)}) copy-start(bf16[4,64,2048]{2,1,0:T(8,128)(2,1)} %param.9) | copy-start | bytes 3145732
  119.0 9.9 %all-to-all-start.1 = ((f32[4,64,256]{2,1,0:T(8,128)}), f32[4,64,256]{2,1,0:T(8,128)S(1)}, u32[]{:S(2)}, u32[]{:S(2)}) async-start(f32[4,64,256]{2,1,0:T(8,128)} %broadcast_in_dim.104), calls=%async_computation.1 | async-start | bytes 524288 | tf_op jit(solution)/shard_map/all_to_all | solution.py:65
  129.1 6.0 %copy-start = (bf16[2,64,128,128]{3,2,1,0:T(8,128)(2,1)S(1)}, bf16[2,64,128,128]{3,2,1,0:T(8,128)(2,1)}, u32[]{:S(2)}) copy-start(bf16[2,64,128,128]{3,2,1,0:T(8,128)(2,1)} %param.13) | copy-start | bytes 12582916
Sparse Core Ops, SparseCore 0:
  9.6 95.8 all-gather.1
